TPU v7x, 256 devices: a whole 4x4x8 slice. The times are simulated.
256 devices in a mesh: cfg: 2 (over z_lo), req: 16 (over y, z_hi), mlp: 8 (over x, core).
Axes of the slice: x: 4, y: 4, z: 8 (z_hi: 4, z_lo: 2; z = z_hi * 2 + z_lo), core: 2. Of those that a mesh axis runs over, the one named last changes fastest.
Arguments:
- hidden: bfloat16 [2, 16384, 1152], P('cfg', ('req', 'mlp')), may hold values from -64 to 64
- noisy_latent: float32 [16384, 16], P(('req', 'mlp'), 'cfg'), may hold values from -6 to 6
- labels: int32 [16, 4], replicated, may hold values from 0 to 999
- timesteps: int32 [16, 4], replicated, may hold values from 0 to 999
- lengths: int32 [16, 4], P('req'), may hold values from 1 to 512, 1024 in all within a row
- guidance: float32 [16, 4], P('req'), may hold values from 1.5 to 4
- keep_scale: float32 [16, 4], P('req'), may hold values from 0.9 to 1.2
- noise_scale: float32 [16, 4], P('req'), may hold values from -0.8 to -0.2
- class_table: bfloat16 [1001, 1152], replicated, may hold values from -6 to 6
- time_up: bfloat16 [256, 1152], replicated, may hold values from -0.375 to 0.375
- time_up_bias: bfloat16 [1152], replicated, may hold values from -4 to 4
- time_out: bfloat16 [1152, 1152], replicated, may hold values from -0.1875 to 0.1875
- time_out_bias: bfloat16 [1152], replicated, may hold values from -4 to 4
- mod_weight: bfloat16 [1152, 9216], P(None, 'req'), may hold values from -0.1875 to 0.1875
- mod_bias: bfloat16 [9216], P('req'), may hold values from -4 to 4
- qkv_weight: bfloat16 [1152, 3456], P(None, 'req'), may hold values from -8 to 8
- qkv_bias: bfloat16 [3456], P('req'), may hold values from -4 to 4
- out_weight: bfloat16 [1152, 1152], P(None, 'req'), may hold values from -0.1875 to 0.1875
- out_bias: bfloat16 [1152], P('req'), may hold values from -4 to 4
- up_weight: bfloat16 [1152, 4608], P(None, 'mlp'), may hold values from -0.1875 to 0.1875
- up_bias: bfloat16 [4608], P('mlp'), may hold values from -4 to 4
- down_weight: bfloat16 [4608, 1152], P('mlp'), may hold values from -1 to 1
- down_bias: bfloat16 [1152], replicated, may hold values from -4 to 4
- final_weight: bfloat16 [1152, 16], replicated, may hold values from -0.1875 to 0.1875
- final_bias: bfloat16 [16], replicated, may hold values from -4 to 4
Outputs:
- next_latent: float32 [16384, 16], P(('req', 'mlp'), 'cfg')
Inputs may be any that keep to these rules, and one draw needn't show every extreme that they name: `lengths`: each row sums to 1024, and its largest crop has exactly 512 tokens.
All inputs are finite; a program needn't handle non-finite values.
Results may differ from a plain program's by a relative error of at most 0.015.
Values may be sent and summed in bfloat16 or wider, within the bound.
No kernel may reach another device: no remote copies, remote signals or barrier semaphores. Data moves between devices by JAX's collectives and lax.ppermute only.
A program may use at most 128 MiB of HBM per device.

v0:
```python
import math

import jax
import jax.numpy as jnp
from jax import lax
from jax.sharding import PartitionSpec as P

HEADS = 16
HEAD_DIM = 72
CLASSES = 1000
FREQ = 256


def layer_norm(values):
    values = values.astype(jnp.float32)
    centre = values - jnp.mean(values, axis=-1, keepdims=True)
    variance = jnp.mean(centre * centre, axis=-1, keepdims=True)
    return centre * lax.rsqrt(variance + 1e-06)


def time_features(times_flat):
    half_freq = FREQ // 2
    frequency = jnp.exp(-math.log(10000.0) * jnp.arange(half_freq, dtype=jnp.float32) / half_freq)
    angles = times_flat.astype(jnp.float32)[:, None] * frequency[None, :]
    return jnp.concatenate([jnp.cos(angles), jnp.sin(angles)], axis=1).astype(jnp.bfloat16)


def segment_ids(lengths_row, positions):
    ends = jnp.cumsum(lengths_row)
    return jnp.sum((positions[:, None] >= ends[None, :]).astype(jnp.int32), axis=1)


def attention(queries, keys_all, values_all, query_segment, key_segment):
    scores = jnp.einsum(
        "qhd,khd->hqk", queries, keys_all, preferred_element_type=jnp.float32
    ) / math.sqrt(HEAD_DIM)
    same = (query_segment[:, None] == key_segment[None, :])[None]
    masked = jnp.where(same, scores, -1e30)
    row_max = jnp.max(masked, axis=2, keepdims=True)
    expo = jnp.where(same, jnp.exp(masked - row_max), 0.0)
    denominator = jnp.sum(expo, axis=2)
    weights = expo.astype(jnp.bfloat16)
    mixed = jnp.einsum("hqk,khd->qhd", weights, values_all, preferred_element_type=jnp.float32)
    result = mixed / jnp.transpose(denominator)[:, :, None]
    return result.astype(jnp.bfloat16).reshape(queries.shape[0], -1)


def shards(
    hidden,
    noisy_latent,
    labels,
    timesteps,
    lengths,
    guidance,
    keep_scale,
    noise_scale,
    class_table,
    time_up,
    time_up_bias,
    time_out,
    time_out_bias,
    mod_weight,
    mod_bias,
    qkv_weight,
    qkv_bias,
    out_weight,
    out_bias,
    up_weight,
    up_bias,
    down_weight,
    down_bias,
    final_weight,
    final_bias,
):
    req_count = lax.axis_size("req")
    mlp_count = lax.axis_size("mlp")
    half_index = lax.axis_index("cfg")
    mlp_index = lax.axis_index("mlp")
    tok_rows = hidden.shape[1]
    width = hidden.shape[2]
    group_rows = tok_rows * mlp_count
    per_group = labels.shape[1]
    time_feat = time_features(timesteps.reshape(-1))
    time_mid = jax.nn.silu(
        jnp.dot(time_feat, time_up, preferred_element_type=jnp.float32)
        + time_up_bias.astype(jnp.float32)
    ).astype(jnp.bfloat16)
    time_cond = jnp.dot(
        time_mid, time_out, preferred_element_type=jnp.float32
    ) + time_out_bias.astype(jnp.float32)
    used_labels = jnp.where(half_index == 0, labels.reshape(-1), CLASSES)
    one_hot = (used_labels[:, None] == jnp.arange(CLASSES + 1, dtype=jnp.int32)[None, :]).astype(
        jnp.bfloat16
    )
    cond_act = jax.nn.silu(
        time_cond + jnp.dot(one_hot, class_table, preferred_element_type=jnp.float32)
    ).astype(jnp.bfloat16)
    local_mod = (
        jnp.dot(cond_act, mod_weight, preferred_element_type=jnp.float32)
        + mod_bias.astype(jnp.float32)
    ).astype(jnp.bfloat16)
    local_mod = local_mod.reshape(req_count, per_group, local_mod.shape[1])
    modulation = lax.all_to_all(local_mod, "req", split_axis=0, concat_axis=2, tiled=True)[0]
    positions = jnp.arange(group_rows, dtype=jnp.int32)
    segment_all = segment_ids(lengths[0], positions)
    segment_own = lax.dynamic_slice_in_dim(segment_all, mlp_index * tok_rows, tok_rows)
    member = segment_own[:, None] == jnp.arange(per_group, dtype=jnp.int32)[None, :]
    per_token = jnp.dot(member.astype(jnp.bfloat16), modulation, preferred_element_type=jnp.float32)
    pieces = [per_token[:, index * width : (index + 1) * width] for index in range(8)]
    shift_attn, scale_attn, gate_attn, shift_mlp, scale_mlp, gate_mlp, shift_final, scale_final = (
        pieces
    )
    rows = hidden[0]
    normed = (layer_norm(rows) * (1.0 + scale_attn) + shift_attn).astype(jnp.bfloat16)
    qkv_full, qkv_bias_full, out_full, out_bias_full = (
        lax.all_gather(qkv_weight, "req", axis=1, tiled=True),
        lax.all_gather(qkv_bias, "req", axis=0, tiled=True),
        lax.all_gather(out_weight, "req", axis=1, tiled=True),
        lax.all_gather(out_bias, "req", axis=0, tiled=True),
    )
    qkv = (
        jnp.dot(normed, qkv_full, preferred_element_type=jnp.float32)
        + qkv_bias_full.astype(jnp.float32)
    ).astype(jnp.bfloat16)
    keys_all, values_all = (
        lax.all_gather(qkv[:, width : 2 * width], "mlp", axis=0, tiled=True),
        lax.all_gather(qkv[:, 2 * width :], "mlp", axis=0, tiled=True),
    )
    attended = attention(
        qkv[:, :width].reshape(tok_rows, HEADS, HEAD_DIM),
        keys_all.reshape(group_rows, HEADS, HEAD_DIM),
        values_all.reshape(group_rows, HEADS, HEAD_DIM),
        segment_own,
        segment_all,
    )
    projected = jnp.dot(
        attended, out_full, preferred_element_type=jnp.float32
    ) + out_bias_full.astype(jnp.float32)
    mid_hidden = (rows.astype(jnp.float32) + gate_attn * projected).astype(jnp.bfloat16)
    normed_mlp = (layer_norm(mid_hidden) * (1.0 + scale_mlp) + shift_mlp).astype(jnp.bfloat16)
    gathered = lax.all_gather(normed_mlp, "mlp", axis=0, tiled=True)
    inner = jax.nn.gelu(
        jnp.dot(gathered, up_weight, preferred_element_type=jnp.float32)
        + up_bias.astype(jnp.float32),
        approximate=True,
    ).astype(jnp.bfloat16)
    mlp_out = lax.psum_scatter(
        jnp.dot(inner, down_weight, preferred_element_type=jnp.float32).astype(jnp.bfloat16),
        "mlp",
        scatter_dimension=0,
        tiled=True,
    ).astype(jnp.float32)
    final_hidden = mid_hidden.astype(jnp.float32) + gate_mlp * (
        mlp_out + down_bias.astype(jnp.float32)
    )
    normed_final = (layer_norm(final_hidden) * (1.0 + scale_final) + shift_final).astype(
        jnp.bfloat16
    )
    predicted = jnp.dot(
        normed_final, final_weight, preferred_element_type=jnp.float32
    ) + final_bias.astype(jnp.float32)
    halves = lax.all_to_all(predicted[None], "cfg", split_axis=2, concat_axis=0, tiled=True)
    eps_cond = halves[0]
    eps_free = halves[1]
    member_f = member.astype(jnp.float32)
    guide_tok = jnp.sum(member_f * guidance, axis=1, keepdims=True)
    keep_tok = jnp.sum(member_f * keep_scale, axis=1, keepdims=True)
    noise_tok = jnp.sum(member_f * noise_scale, axis=1, keepdims=True)
    return keep_tok * noisy_latent + noise_tok * (eps_free + guide_tok * (eps_cond - eps_free))


def solution(mesh):
    return jax.shard_map(
        shards,
        mesh=mesh,
        in_specs=(
            P("cfg", ("req", "mlp"), None),
            P(("req", "mlp"), "cfg"),
            P(),
            P(),
            P("req", None),
            P("req", None),
            P("req", None),
            P("req", None),
            P(),
            P(),
            P(),
            P(),
            P(),
            P(None, "req"),
            P("req"),
            P(None, "req"),
            P("req"),
            P(None, "req"),
            P("req"),
            P(None, "mlp"),
            P("mlp"),
            P("mlp", None),
            P(),
            P(),
            P(),
        ),
        out_specs=P(("req", "mlp"), "cfg"),
        check_vma=False,
    )
```

profile of v0, /device:TPU:8, one launch (start us, length us, event | category | flops | bytes accessed | tf_op | source)
XLA Modules:
  0.0 357.1 jit_solution(16776291229437060213)
XLA Ops:
  6.5 0.7 all-gather.6.cloned.1.call-update
  7.3 0.8 convert_element_type.94
  8.2 0.7 convert_element_type.96
  8.9 0.7 convert_element_type.98
  9.6 0.7 broadcast_select_fusion
  10.4 0.7 convert_element_type.100
  11.4 1.8 convolution_add_fusion.3
  13.2 3.0 fusion.29
  16.2 0.7 reshape.143
  16.9 11.6 %all-to-all-start = ((bf16[16,4,576]{2,1,0:T(4,128)(2,1)}), bf16[16,4,576]{2,1,0:T(4,128)(2,1)S(1)}, u32[]{:S(2)}, u32[]{:S(2)}) async-start(bf16[16,4,576]{2,1,0:T(4,128)(2,1)} %reshape.143), calls=%async_computation | async-start | bytes 163840 | tf_op jit(solution)/shard_map/all_to_all | solution.py:103
  31.1 82.8 %all-reduce.2 = (bf16[3456]{0:T(1024)(128)(2,1)S(1)}, bf16[1152]{0:T(1024)(128)(2,1)S(1)}) all-reduce(bf16[3456]{0:T(1024)(128)(2,1)S(1)} %dynamic-update-slice, bf16[1152]{0:T(1024)(128)(2,1)S(1)} %dynamic-update-slice.1), channel_id=1, replica_groups=mesh['cfg'=2,'req'=16,'mlp'=8] {'req'}, use_global_device_ids=true, to_apply=%add | all-reduce | flops 4608 | bytes 18432
  114.6 3.0 fusion.67
  117.6 6.1 %fusion.2 = bf16[128,3456]{1,0:T(8,128)(2,1)S(1)} fusion(bf16[1152,3456]{0,1:T(8,128)(2,1)} %all-gather.6.cloned.1.call-done, f32[3456]{0:T(1024)S(1)} %convert_element_type.103, bf16[1,128,1152]{2,1,0:T(8,128)(2,1)S(1)} %copy-done.1, f32[128,9216]{1,0:T(8,128)} %fusion.67, f32[128]{0:T(128)S(1)} %add_rsqrt_fusion.2, f32[128]{0:T(128)S(1)} %broadcast_multiply_fusion.2), kind=kOutput, calls=%fused_computation.5 | convolution fusion | flops 1021132800 | bytes 10336768 | tf_op jit(solution)/shard_map/dot_general | solution.py:122
  123.7 0.9 fusion.83
  124.7 0.7 all-gather.8.cloned.1.call-update
  126.2 0.8 broadcast_compare_fusion
  127.2 37.7 %all-gather.10.cloned.1.call-done = bf16[1024,1152]{1,0:T(8,128)(2,1)} async-done(((bf16[128,1152]{1,0:T(8,128)(2,1)}), bf16[1024,1152]{1,0:T(8,128)(2,1)}) %all-gather.10.cloned.1.call-update) | async-done | bytes 2359312 | tf_op jit(solution)/shard_map/all_gather | solution.py:126
  164.9 4.3 %copy.52 = bf16[1024,1152]{0,1:T(8,128)(2,1)} copy(bf16[1024,1152]{1,0:T(8,128)(2,1)} %all-gather.10.cloned.1.call-done) | data formatting | bytes 4718592 | tf_op jit(solution)/shard_map/all_gather | solution.py:126
  169.2 26.3 %all-gather.8.cloned.1.call-done = bf16[1024,1152]{1,0:T(8,128)(2,1)} async-done(((bf16[128,1152]{1,0:T(8,128)(2,1)}), bf16[1024,1152]{1,0:T(8,128)(2,1)}) %all-gather.8.cloned.1.call-update) | async-done | bytes 2359312 | tf_op jit(solution)/shard_map/all_gather | solution.py:127
  195.5 4.3 %copy.50 = bf16[1024,1152]{0,1:T(8,128)(2,1)} copy(bf16[1024,1152]{1,0:T(8,128)(2,1)} %all-gather.8.cloned.1.call-done) | data formatting | bytes 4718592 | tf_op jit(solution)/shard_map/all_gather | solution.py:127
  199.8 7.5 %fusion.84 = (f32[16,128]{1,0:T(8,128)S(1)}, bf16[16,128,1024]{2,1,0:T(8,128)(2,1)}) fusion(pred[128,1024]{1,0:T(8,128)(4,1)S(1)} %copy-done.2, bf16[128,16,72]{0,2,1:T(8,128)(2,1)S(1)} %bitcast.88, bf16[1024,16,72]{0,2,1:T(8,128)(2,1)} %bitcast.84), kind=kOutput, calls=%fused_computation.112 | convolution fusion | flops 314573824 | bytes 6987776 | tf_op jit(solution)/shard_map/sub | solution.py:40
  207.2 5.2 %fusion.26 = bf16[128,16,72]{0,2,1:T(8,128)(2,1)} fusion(bf16[1024,16,72]{0,2,1:T(8,128)(2,1)} %bitcast.85, bf16[16,128,1024]{2,1,0:T(8,128)(2,1)} %get-tuple-element.18, f32[128,16]{0,1:T(8,128)S(1)} %bitcast.95), kind=kOutput, calls=%fused_computation.31 | convolution fusion | flops 302284800 | bytes 6856704 | tf_op jit(solution)/shard_map/hqk,khd->qhd/dot_general | solution.py:43
  212.4 49.4 %all-gather.12.cloned.1.call-done = bf16[1152,1152]{0,1:T(8,128)(2,1)} async-done(((bf16[1152,72]{0,1:T(8,128)(2,1)}), bf16[1152,1152]{0,1:T(8,128)(2,1)}) %all-gather.12.cloned.1.call-update) | async-done | bytes 2654224 | tf_op jit(solution)/shard_map/all_gather | solution.py:118
  261.8 3.0 fusion.85
  265.0 2.2 fusion.41
  267.3 26.1 %all-gather.14.cloned.1.call-done = bf16[1024,1152]{1,0:T(8,128)(2,1)} async-done(((bf16[128,1152]{1,0:T(8,128)(2,1)}), bf16[1024,1152]{1,0:T(8,128)(2,1)}) %all-gather.14.cloned.1.call-update) | async-done | bytes 2359312 | tf_op jit(solution)/shard_map/all_gather | solution.py:141
  293.4 7.8 %convolution_convert_fusion = bf16[1024,1152]{1,0:T(8,128)(2,1)} fusion(bf16[576,1152]{1,0:T(8,128)(2,1)} %param.46, bf16[1024,1152]{1,0:T(8,128)(2,1)} %all-gather.14.cloned.1.call-done, bf16[1152,576]{0,1:T(8,128)(2,1)} %param.44, f32[576]{0:T(1024)S(1)} %convert_element_type.111), kind=kOutput, calls=%fused_computation.11 | convolution fusion | flops 2724986880 | bytes 7375104 | tf_op jit(solution)/shard_map/dot_general | solution.py:148
  301.9 36.9 %reduce-scatter.2.cloned.1.call-done = bf16[128,1152]{1,0:T(8,128)(2,1)} async-done(((bf16[1024,1152]{1,0:T(8,128)(2,1)}), bf16[128,1152]{1,0:T(8,128)(2,1)}) %reduce-scatter.2.cloned.1.call-update) | async-done | bytes 294928 | tf_op jit(solution)/shard_map/reduce_scatter | solution.py:147
  338.8 1.3 fusion.81
  340.4 2.2 convolution_add_fusion.6
  342.6 3.2 all-to-all-start.1
  345.9 3.7 %all-to-all-done.1 = f32[1,128,16]{1,0,2:T(1,128)S(1)} async-done(((f32[1,128,16]{1,0,2:T(1,128)}), f32[1,128,16]{1,0,2:T(1,128)S(1)}, u32[]{:S(2)}, u32[]{:S(2)}) %all-to-all-start.1) | async-done | bytes 8224 | tf_op jit(solution)/shard_map/all_to_all | solution.py:162
  (76 shorter events, 5.5 us)
Async XLA Ops:
  6.5 4.8 %copy-start = (bf16[1152,1152]{1,0:T(8,128)(2,1)S(1)}, bf16[1152,1152]{1,0:T(8,128)(2,1)}, u32[]{:S(2)}) copy-start(bf16[1152,1152]{1,0:T(8,128)(2,1)} %param.36) | copy-start | bytes 7962628
  6.5 111.0 %all-gather.6.cloned.1.call-start = ((), (), s32[]{:S(2)}) async-start(), calls=%async_computation.3 | async-start | bytes 8460288 | tf_op jit(solution)/shard_map/all_gather | solution.py:116
  13.2 15.4 %copy-start.10 = (s32[1,4]{1,0:T(1,128)S(1)}, s32[1,4]{1,0:T(1,128)}, u32[]{:S(2)}) copy-start(s32[1,4]{1,0:T(1,128)} %param.29) | copy-start | bytes 52
  13.2 15.5 %copy-start.14 = (u32[256]{0:T(256)S(1)}, u32[256]{0:T(256)}, u32[]{:S(2)}) copy-start(u32[256]{0:T(256)} %constant.70) | copy-start | bytes 3076
  13.2 17.4 %copy-start.11 = (bf16[216]{0:T(256)(128)(2,1)S(1)}, bf16[216]{0:T(256)(128)(2,1)}, u32[]{:S(2)}) copy-start(bf16[216]{0:T(256)(128)(2,1)} %param.41) | copy-start | bytes 1300
  13.2 17.7 %copy-start.12 = (bf16[72]{0:T(256)(128)(2,1)S(1)}, bf16[72]{0:T(256)(128)(2,1)}, u32[]{:S(2)}) copy-start(bf16[72]{0:T(256)(128)(2,1)} %param.43) | copy-start | bytes 436
  13.2 100.9 %copy-start.1 = (bf16[1,128,1152]{2,1,0:T(8,128)(2,1)S(1)}, bf16[1,128,1152]{2,1,0:T(8,128)(2,1)}, u32[]{:S(2)}) copy-start(bf16[1,128,1152]{2,1,0:T(8,128)(2,1)} %param.25) | copy-start | bytes 884740
  16.9 97.5 %all-to-all-start = ((bf16[16,4,576]{2,1,0:T(4,128)(2,1)}), bf16[16,4,576]{2,1,0:T(4,128)(2,1)S(1)}, u32[]{:S(2)}, u32[]{:S(2)}) async-start(bf16[16,4,576]{2,1,0:T(4,128)(2,1)} %reshape.143), calls=%async_computation | async-start | bytes 163840 | tf_op jit(solution)/shard_map/all_to_all | solution.py:103
  28.5 136.4 %all-gather.10.cloned.1.call-start = ((), (), s32[]{:S(2)}) async-start(), calls=%async_computation.5 | async-start | bytes 2654208 | tf_op jit(solution)/shard_map/all_gather | solution.py:126
  124.6 70.8 %all-gather.8.cloned.1.call-start = ((), (), s32[]{:S(2)}) async-start(), calls=%async_computation.4 | async-start | bytes 2654208 | tf_op jit(solution)/shard_map/all_gather | solution.py:127
  125.4 136.4 %all-gather.12.cloned.1.call-start = ((), (), s32[]{:S(2)}) async-start(), calls=%async_computation.6 | async-start | bytes 2820096 | tf_op jit(solution)/shard_map/all_gather | solution.py:118
  125.9 167.4 %all-gather.14.cloned.1.call-start = ((), (), s32[]{:S(2)}) async-start(), calls=%async_computation.7 | async-start | bytes 2654208 | tf_op jit(solution)/shard_map/all_gather | solution.py:141
  169.2 30.6 %copy-start.2 = (pred[128,1024]{1,0:T(8,128)(4,1)S(1)}, pred[128,1024]{1,0:T(8,128)(4,1)}, u32[]{:S(2)}) copy-start(pred[128,1024]{1,0:T(8,128)(4,1)} %broadcast_compare_fusion) | copy-start | bytes 393220
  264.8 2.5 copy-start.6
  267.2 71.7 %reduce-scatter.2.cloned.1.call-start = ((), (), s32[]{:S(2)}) async-start(), calls=%async_computation.8 | async-start | bytes 2654208 | tf_op jit(solution)/shard_map/reduce_scatter | solution.py:147
  301.2 0.7 copy-start.4
  301.2 0.7 copy-start.13
  301.2 39.2 %copy-start.3 = (bf16[1152,16]{0,1:T(8,128)(2,1)S(1)}, bf16[1152,16]{0,1:T(8,128)(2,1)}, u32[]{:S(2)}) copy-start(bf16[1152,16]{0,1:T(8,128)(2,1)} %param.48) | copy-start | bytes 110596
  301.9 43.9 %copy-start.7 = (f32[1,4]{1,0:T(1,128)S(1)}, f32[1,4]{1,0:T(1,128)}, u32[]{:S(2)}) copy-start(f32[1,4]{1,0:T(1,128)} %param.31) | copy-start | bytes 52
  301.9 44.0 %copy-start.8 = (f32[1,4]{1,0:T(1,128)S(1)}, f32[1,4]{1,0:T(1,128)}, u32[]{:S(2)}) copy-start(f32[1,4]{1,0:T(1,128)} %param.30) | copy-start | bytes 52
  301.9 44.0 %copy-start.9 = (f32[1,4]{1,0:T(1,128)S(1)}, f32[1,4]{1,0:T(1,128)}, u32[]{:S(2)}) copy-start(f32[1,4]{1,0:T(1,128)} %param.32) | copy-start | bytes 52
  301.9 47.7 %copy-start.5 = (f32[128,8]{0,1:T(8,128)S(1)}, f32[128,8]{0,1:T(8,128)}, u32[]{:S(2)}) copy-start(f32[128,8]{0,1:T(8,128)} %param.26) | copy-start | bytes 12292
  342.6 7.0 %all-to-all-start.1 = ((f32[1,128,16]{1,0,2:T(1,128)}), f32[1,128,16]{1,0,2:T(1,128)S(1)}, u32[]{:S(2)}, u32[]{:S(2)}) async-start(f32[1,128,16]{1,0,2:T(1,128)} %bitcast.16), calls=%async_computation.2 | async-start | bytes 16384 | tf_op jit(solution)/shard_map/all_to_all | solution.py:162
Sparse Core Ops, SparseCore 0:
  9.8 107.0 all-gather.5
  124.8 40.0 all-gather.9
  166.7 28.6 all-gather.7
  197.8 63.9 all-gather.11
  267.3 26.0 all-gather.13
  301.3 37.4 reduce-scatter.1
where the time goes:
time: 358 us; the launch traced here: 357 us
  waiting for transfers between devices  182 us (51%)
  blocking collectives  82.8 us (23%)
  matrix products  39.5 us (11%)
  starting transfers between devices  15.2 us (4%)
  between operations  15 us (4%)
  local copies, waits for them, and re-layouts  12.7 us (4%)
  other arithmetic  9.78 us (3%)
    unnamed x1, blocking collectives  82.8 us
    all_gather x1, waiting for transfers between devices, shards(): lax.all_gather(out_weight, 'req', axis=1, tiled=True)  49.4 us
    all_gather x1, waiting for transfers between devices, shards(): lax.all_gather(qkv[:, width:2 * width], 'mlp', axis=0, tiled=True)  37.7 us
    reduce_scatter x1, waiting for transfers between devices, shards(): lax.psum_scatter(jnp.dot(inner, down_weight, preferred_element_type=jnp.f...  36.9 us
    all_gather x1, waiting for transfers between devices, shards(): lax.all_gather(qkv[:, 2 * width:], 'mlp', axis=0, tiled=True)  26.3 us
    all_gather x1, waiting for transfers between devices, shards(): gathered = lax.all_gather(normed_mlp, 'mlp', axis=0, tiled=True)  26.1 us
    all_to_all x1, starting transfers between devices, shards(): lax.all_to_all(local_mod, 'req', split_axis=0, concat_axis=2, tiled=True)[0]  11.6 us
    dot_general x1, matrix products, shards(): jnp.dot(inner, down_weight, preferred_element_type=jnp.float32)  7.81 us
  transfers between devices with their start and end apart: 8, of which 6 were waited for; matrix products, arithmetic and copies ran while one was open for 10% of the time, Pallas kernels for 0%

commit v1 on v0

--- a/solution.py
+++ b/solution.py
@@ -112,30 +112,45 @@
     )
     rows = hidden[0]
     normed = (layer_norm(rows) * (1.0 + scale_attn) + shift_attn).astype(jnp.bfloat16)
-    qkv_full, qkv_bias_full, out_full, out_bias_full = (
-        lax.all_gather(qkv_weight, "req", axis=1, tiled=True),
-        lax.all_gather(qkv_bias, "req", axis=0, tiled=True),
-        lax.all_gather(out_weight, "req", axis=1, tiled=True),
-        lax.all_gather(out_bias, "req", axis=0, tiled=True),
-    )
-    qkv = (
-        jnp.dot(normed, qkv_full, preferred_element_type=jnp.float32)
-        + qkv_bias_full.astype(jnp.float32)
-    ).astype(jnp.bfloat16)
-    keys_all, values_all = (
-        lax.all_gather(qkv[:, width : 2 * width], "mlp", axis=0, tiled=True),
-        lax.all_gather(qkv[:, 2 * width :], "mlp", axis=0, tiled=True),
-    )
-    attended = attention(
-        qkv[:, :width].reshape(tok_rows, HEADS, HEAD_DIM),
-        keys_all.reshape(group_rows, HEADS, HEAD_DIM),
-        values_all.reshape(group_rows, HEADS, HEAD_DIM),
-        segment_own,
+    core = mlp_index % 2
+    half_rows = width // 2
+    pair = [(index, index ^ 1) for index in range(mlp_count)]
+
+    def split_gather(weight, bias):
+        mine = lax.dynamic_slice_in_dim(weight, core * half_rows, half_rows, axis=0)
+        bias_rows = jnp.zeros((16, weight.shape[1]), weight.dtype).at[0].set(bias)
+        gathered = lax.all_gather(
+            jnp.concatenate([mine, bias_rows], axis=0), "req", axis=1, tiled=True
+        )
+        return gathered, lax.ppermute(gathered, "mlp", pair)
+
+    def split_dot(values, mine, other):
+        values_mine = lax.dynamic_slice_in_dim(values, core * half_rows, half_rows, axis=1)
+        values_other = lax.dynamic_slice_in_dim(values, (1 - core) * half_rows, half_rows, axis=1)
+        return (
+            jnp.dot(values_mine, mine[:half_rows], preferred_element_type=jnp.float32)
+            + jnp.dot(values_other, other[:half_rows], preferred_element_type=jnp.float32)
+            + mine[half_rows].astype(jnp.float32)
+        )
+
+    qkv_mine, qkv_other = split_gather(qkv_weight, qkv_bias)
+    out_mine, out_other = split_gather(out_weight, out_bias)
+    qkv = split_dot(normed, qkv_mine, qkv_other).astype(jnp.bfloat16)
+    heads_per = HEADS // mlp_count
+    head_cols = heads_per * HEAD_DIM
+    packed = jnp.transpose(
+        qkv.reshape(tok_rows, 3, mlp_count, head_cols), (0, 2, 1, 3)
+    ).reshape(tok_rows, mlp_count * 3 * head_cols)
+    own_heads = lax.all_to_all(packed, "mlp", split_axis=1, concat_axis=0, tiled=True)
+    attended_heads = attention(
+        own_heads[:, :head_cols].reshape(group_rows, heads_per, HEAD_DIM),
+        own_heads[:, head_cols : 2 * head_cols].reshape(group_rows, heads_per, HEAD_DIM),
+        own_heads[:, 2 * head_cols :].reshape(group_rows, heads_per, HEAD_DIM),
         segment_all,
-    )
-    projected = jnp.dot(
-        attended, out_full, preferred_element_type=jnp.float32
-    ) + out_bias_full.astype(jnp.float32)
+        segment_all,
+    )
+    attended = lax.all_to_all(attended_heads, "mlp", split_axis=0, concat_axis=1, tiled=True)
+    projected = split_dot(attended, out_mine, out_other)
     mid_hidden = (rows.astype(jnp.float32) + gate_attn * projected).astype(jnp.bfloat16)
     normed_mlp = (layer_norm(mid_hidden) * (1.0 + scale_mlp) + shift_mlp).astype(jnp.bfloat16)
     gathered = lax.all_gather(normed_mlp, "mlp", axis=0, tiled=True)

time: 358 us -> 297 us (0.83)
  blocking collectives: 82.8 us -> 0 us
  local copies, waits for them, and re-layouts: 12.7 us -> 24.1 us
  starting transfers between devices: 15.2 us -> 21.3 us
    unnamed x1 -> x0, blocking collectives: 82.8 us -> none
    all_to_all x0 -> x2, starting transfers between devices: none -> 8.46 us  [the longest x1 4.24 us: shards(): lax.all_to_all(packed, 'mlp', split_axis=1, concat_axis=0, tiled=True)]
    all_gather x4 -> x2, waiting for transfers between devices: 113 us -> 106 us  [split_gather(): lax.all_gather(jnp.concatenate([mine, bias_rows], axis=0), 'req', axis=1,...]
    all_to_all x1, waiting for transfers between devices: 0.01 us -> 6.92 us  [shards(): lax.all_to_all(local_mod, 'req', split_axis=0, concat_axis=2, tiled=True)[0]]
    all_to_all x0 -> x2, waiting for transfers between devices: none -> 6.59 us  [the longest x1 6.58 us: shards(): lax.all_to_all(attended_heads, 'mlp', split_axis=0, concat_axis=1, tiled=...]
    dot_general x2 -> x4, matrix products: 9.13 us -> 11.9 us  [the longest x2 6.13 us: split_dot(): jnp.dot(values_other, other[:half_rows], preferred_element_type=jnp.float32)]
  transfers between devices with their start and end apart: 8 -> 10, of which waited for: 6 -> 7; matrix products, arithmetic and copies ran while one was open for 10% -> 16% of each run, Pallas kernels for 0% -> 0%
where the time goes in v1:
time: 297 us; the launch traced here: 296 us
  waiting for transfers between devices  185 us (62%)
  matrix products  39.1 us (13%)
  local copies, waits for them, and re-layouts  24.1 us (8%)
  starting transfers between devices  21.3 us (7%)
  between operations  13.6 us (5%)
  other arithmetic  12 us (4%)
    all_gather x2, waiting for transfers between devices, split_gather(): lax.all_gather(jnp.concatenate([mine, bias_rows], axis=0), 'req', axis=1,...  106 us
    reduce_scatter x1, waiting for transfers between devices, shards(): lax.psum_scatter(jnp.dot(inner, down_weight, preferred_element_type=jnp.f...  37 us
    all_gather x1, waiting for transfers between devices, shards(): gathered = lax.all_gather(normed_mlp, 'mlp', axis=0, tiled=True)  25 us
    all_gather x2, local copies, waits for them, and re-layouts, split_gather(): lax.all_gather(jnp.concatenate([mine, bias_rows], axis=0), 'req', axis=1,...  10.6 us
    all_to_all x1, starting transfers between devices, shards(): lax.all_to_all(local_mod, 'req', split_axis=0, concat_axis=2, tiled=True)[0]  9.51 us
    sub x1, matrix products, attention(): expo = jnp.where(same, jnp.exp(masked - row_max), 0.0)  8.43 us
    dot_general x1, matrix products, shards(): jnp.dot(inner, down_weight, preferred_element_type=jnp.float32)  7.88 us
    all_to_all x1, waiting for transfers between devices, shards(): lax.all_to_all(local_mod, 'req', split_axis=0, concat_axis=2, tiled=True)[0]  6.92 us
  transfers between devices with their start and end apart: 10, of which 7 were waited for; matrix products, arithmetic and copies ran while one was open for 16% of the time, Pallas kernels for 0%

profile of v1, /device:TPU:8, one launch (start us, length us, event | category | flops | bytes accessed | tf_op | source)
XLA Modules:
  0.0 295.6 jit_solution(11914430172864486977)
XLA Ops:
  9.5 79.9 %all-gather.4.cloned.1.call-done = bf16[592,3456]{0,1:T(8,128)(2,1)} async-done(((bf16[592,216]{0,1:T(8,128)(2,1)}), bf16[592,3456]{0,1:T(8,128)(2,1)}) %all-gather.4.cloned.1.call-update) | async-done | bytes 4091920 | tf_op jit(solution)/shard_map/all_gather | solution.py:122
  89.3 7.0 %copy.82 = bf16[592,3456]{1,0:T(8,128)(2,1)} copy(bf16[592,3456]{0,1:T(8,128)(2,1)} %all-gather.4.cloned.1.call-done) | data formatting | bytes 8183808 | tf_op jit(solution)/shard_map/all_gather | solution.py:122
  97.0 1.8 convolution_add_fusion.3
  98.9 3.0 %fusion.37 = bf16[64,576]{1,0:T(8,128)(2,1)S(1)} fusion(bf16[1152,576]{0,1:T(8,128)(2,1)} %param.42, f32[64,1152]{1,0:T(8,128)S(1)} %convolution_add_fusion.3, bf16[1001,1152]{1,0:T(8,128)(2,1)} %param.37, s32[64]{0:T(128)S(1)} %select_n.45, f32[576]{0:T(1024)S(1)} %convert_element_type.98), kind=kOutput, calls=%fused_computation.43 | convolution fusion | flops 233118272 | bytes 4004608 | tf_op jit(solution)/shard_map/dot_general | solution.py:99
  102.6 9.5 %all-to-all-start = ((bf16[16,4,576]{2,1,0:T(4,128)(2,1)}), bf16[16,4,576]{2,1,0:T(4,128)(2,1)S(1)}, u32[]{:S(2)}, u32[]{:S(2)}) async-start(bf16[16,4,576]{2,1,0:T(4,128)(2,1)} %reshape.206), calls=%async_computation | async-start | bytes 163840 | tf_op jit(solution)/shard_map/all_to_all | solution.py:103
  113.8 6.9 %all-to-all-done = bf16[16,4,576]{2,1,0:T(4,128)(2,1)S(1)} async-done(((bf16[16,4,576]{2,1,0:T(4,128)(2,1)}), bf16[16,4,576]{2,1,0:T(4,128)(2,1)S(1)}, u32[]{:S(2)}, u32[]{:S(2)}) %all-to-all-start) | async-done | bytes 73760 | tf_op jit(solution)/shard_map/all_to_all | solution.py:103
  121.8 2.1 copy-done.1
  124.1 1.8 convert_reduce_fusion
  125.9 3.7 %fusion.4 = f32[128,3456]{1,0:T(8,128)S(1)} fusion(bf16[592,3456]{0,1:T(8,128)(2,1)} %all-gather.4.cloned.1.call-done, bf16[128,1152]{1,0:T(8,128)(2,1)S(1)} %fusion.46, s32[]{:T(128)S(6)} %select_n.47), kind=kOutput, calls=%fused_computation.7 | convolution fusion | flops 509607936 | bytes 6025220 | tf_op jit(solution)/shard_map/dot_general | solution.py:131
  129.7 4.0 %fusion.3 = bf16[128,3456]{1,0:T(8,128)(2,1)} fusion(f32[128,3456]{1,0:T(8,128)S(1)} %fusion.4, bf16[592,3456]{1,0:T(8,128)(2,1)} %collective-permute-done, f32[3456]{0:T(1024)S(1)} %convert_reduce_fusion, bf16[128,1152]{1,0:T(8,128)(2,1)S(1)} %fusion.46, s32[]{:T(128)S(6)} %select_n.48), kind=kOutput, calls=%fused_computation.6 | convolution fusion | flops 510935040 | bytes 6815748 | tf_op jit(solution)/shard_map/dot_general | solution.py:132
  133.7 2.2 copy.83
  136.0 2.2 copy.84
  138.1 4.2 %all-to-all-start.1 = ((bf16[128,8,432]{0,2,1:T(8,128)(2,1)}), bf16[128,8,432]{0,2,1:T(8,128)(2,1)}, u32[]{:S(2)}, u32[]{:S(2)}) async-start(bf16[128,8,432]{0,2,1:T(8,128)(2,1)} %bitcast.96), calls=%async_computation.1 | async-start | bytes 1769472 | tf_op jit(solution)/shard_map/all_to_all | solution.py:144
  142.4 1.6 broadcast_compare_fusion
  144.0 26.4 %all-gather.6.cloned.1.call-done = bf16[592,1152]{0,1:T(8,128)(2,1)} async-done(((bf16[592,72]{0,1:T(8,128)(2,1)}), bf16[592,1152]{0,1:T(8,128)(2,1)}) %all-gather.6.cloned.1.call-update) | async-done | bytes 1363984 | tf_op jit(solution)/shard_map/all_gather | solution.py:122
  170.4 3.6 %copy.89 = bf16[592,1152]{1,0:T(8,128)(2,1)} copy(bf16[592,1152]{0,1:T(8,128)(2,1)} %all-gather.6.cloned.1.call-done) | data formatting | bytes 2727936 | tf_op jit(solution)/shard_map/all_gather | solution.py:122
  174.0 1.3 copy_bitcast_fusion
  176.1 8.4 %fusion.99 = (f32[2,1024]{1,0:T(2,128)S(1)}, bf16[2,1024,1024]{1,2,0:T(8,128)(2,1)}) fusion(pred[1024,1024]{0,1:T(8,128)(4,1)} %broadcast_compare_fusion, bf16[1024,2,72]{0,2,1:T(8,128)(2,1)} %bitcast.104, bf16[1024,2,72]{0,2,1:T(8,128)(2,1)S(1)} %bitcast.103), kind=kOutput, calls=%fused_computation.135 | convolution fusion | flops 314573824 | bytes 5840896 | tf_op jit(solution)/shard_map/sub | solution.py:40
  184.5 3.0 %fusion.34 = bf16[1024,2,72]{0,2,1:T(8,128)(2,1)S(1)} fusion(bf16[1024,2,72]{0,2,1:T(8,128)(2,1)S(1)} %bitcast.102, bf16[2,1024,1024]{1,2,0:T(8,128)(2,1)} %get-tuple-element.40, f32[1024,2]{0,1:T(2,128)S(1)} %bitcast.113), kind=kOutput, calls=%fused_computation.41 | convolution fusion | flops 302284800 | bytes 4792320 | tf_op jit(solution)/shard_map/hqk,khd->qhd/dot_general | solution.py:43
  188.3 4.2 %all-to-all-start.2 = ((bf16[8,128,144]{1,2,0:T(8,128)(2,1)}), bf16[8,128,144]{1,2,0:T(8,128)(2,1)S(1)}, u32[]{:S(2)}, u32[]{:S(2)}) async-start(bf16[8,128,144]{1,2,0:T(8,128)(2,1)} %copy.87), calls=%async_computation.2 | async-start | bytes 589824 | tf_op jit(solution)/shard_map/all_to_all | solution.py:152
  192.6 1.2 convert_reduce_fusion.2
  193.8 6.6 %all-to-all-done.2 = bf16[8,128,144]{1,2,0:T(8,128)(2,1)S(1)} async-done(((bf16[8,128,144]{1,2,0:T(8,128)(2,1)}), bf16[8,128,144]{1,2,0:T(8,128)(2,1)S(1)}, u32[]{:S(2)}, u32[]{:S(2)}) %all-to-all-start.2) | async-done | bytes 294944 | tf_op jit(solution)/shard_map/all_to_all | solution.py:152
  200.4 2.1 fusion.25
  202.5 2.1 fusion.100
  204.8 2.2 fusion.49
  207.1 25.0 %all-gather.8.cloned.1.call-done = bf16[1024,1152]{1,0:T(8,128)(2,1)} async-done(((bf16[128,1152]{1,0:T(8,128)(2,1)}), bf16[1024,1152]{1,0:T(8,128)(2,1)}) %all-gather.8.cloned.1.call-update) | async-done | bytes 2359312 | tf_op jit(solution)/shard_map/all_gather | solution.py:156
  232.1 7.9 %convolution_convert_fusion = bf16[1024,1152]{1,0:T(8,128)(2,1)} fusion(bf16[576,1152]{1,0:T(8,128)(2,1)} %param.50, bf16[1024,1152]{1,0:T(8,128)(2,1)} %all-gather.8.cloned.1.call-done, bf16[1152,576]{0,1:T(8,128)(2,1)} %param.48, f32[576]{0:T(1024)S(1)} %convert_element_type.107), kind=kOutput, calls=%fused_computation.15 | convolution fusion | flops 2724986880 | bytes 7375104 | tf_op jit(solution)/shard_map/dot_general | solution.py:163
  240.7 37.0 %reduce-scatter.2.cloned.1.call-done = bf16[128,1152]{1,0:T(8,128)(2,1)} async-done(((bf16[1024,1152]{1,0:T(8,128)(2,1)}), bf16[128,1152]{1,0:T(8,128)(2,1)}) %reduce-scatter.2.cloned.1.call-update) | async-done | bytes 294928 | tf_op jit(solution)/shard_map/reduce_scatter | solution.py:162
  277.7 1.3 fusion.96
  279.3 2.2 convolution_add_fusion.6
  281.4 3.2 %all-to-all-start.3 = ((f32[1,128,16]{1,0,2:T(1,128)}), f32[1,128,16]{1,0,2:T(1,128)S(1)}, u32[]{:S(2)}, u32[]{:S(2)}) async-start(f32[1,128,16]{1,0,2:T(1,128)} %bitcast.21), calls=%async_computation.4 | async-start | bytes 16384 | tf_op jit(solution)/shard_map/all_to_all | solution.py:177
  284.8 3.7 %all-to-all-done.3 = f32[1,128,16]{1,0,2:T(1,128)S(1)} async-done(((f32[1,128,16]{1,0,2:T(1,128)}), f32[1,128,16]{1,0,2:T(1,128)S(1)}, u32[]{:S(2)}, u32[]{:S(2)}) %all-to-all-start.3) | async-done | bytes 8224 | tf_op jit(solution)/shard_map/all_to_all | solution.py:177
  (95 shorter events, 10.6 us)
Async XLA Ops:
  6.5 90.5 %copy-start = (bf16[1152,1152]{1,0:T(8,128)(2,1)S(1)}, bf16[1152,1152]{1,0:T(8,128)(2,1)}, u32[]{:S(2)}) copy-start(bf16[1152,1152]{1,0:T(8,128)(2,1)} %param.40) | copy-start | bytes 7962628
  6.5 82.8 %all-gather.4.cloned.1.call-start = ((), (), s32[]{:S(2)}) async-start(), calls=%async_computation.5 | async-start | bytes 4700160 | tf_op jit(solution)/shard_map/all_gather | solution.py:122
  9.4 87.0 %copy-start.12 = (s32[16,4]{0,1:T(4,128)S(1)}, s32[16,4]{0,1:T(4,128)}, u32[]{:S(2)}) copy-start(s32[16,4]{0,1:T(4,128)} %param.32) | copy-start | bytes 772
  9.4 87.1 %copy-start.6 = (bf16[1152]{0:T(1024)(128)(2,1)S(1)}, bf16[1152]{0:T(1024)(128)(2,1)}, u32[]{:S(2)}) copy-start(bf16[1152]{0:T(1024)(128)(2,1)} %param.39) | copy-start | bytes 6916
  9.4 87.1 %copy-start.7 = (bf16[1152]{0:T(1024)(128)(2,1)S(1)}, bf16[1152]{0:T(1024)(128)(2,1)}, u32[]{:S(2)}) copy-start(bf16[1152]{0:T(1024)(128)(2,1)} %param.41) | copy-start | bytes 6916
  9.4 87.1 %copy-start.13 = (s32[16,4]{0,1:T(4,128)S(1)}, s32[16,4]{0,1:T(4,128)}, u32[]{:S(2)}) copy-start(s32[16,4]{0,1:T(4,128)} %param.31) | copy-start | bytes 772
  9.4 87.3 %copy-start.10 = (bf16[576]{0:T(1024)(128)(2,1)S(1)}, bf16[576]{0:T(1024)(128)(2,1)}, u32[]{:S(2)}) copy-start(bf16[576]{0:T(1024)(128)(2,1)} %param.43) | copy-start | bytes 3460
  96.3 33.3 %collective-permute-start = (bf16[592,3456]{1,0:T(8,128)(2,1)}, bf16[592,3456]{1,0:T(8,128)(2,1)}, u32[]{:S(2)}, u32[]{:S(2)}) collective-permute-start(bf16[592,3456]{1,0:T(8,128)(2,1)} %copy.82), channel_id=1, source_target_pairs={{0,1},{1,0},{2,3},{3,2},{4,5},{5,4},{6,7},{7,6},{8,9},{9,8},{10,11... | collective-permute-start | bytes 12275720 | tf_op jit(solution)/shard_map/ppermute | solution.py:125
  98.8 13.3 %copy-start.14 = (bf16[72]{0:T(256)(128)(2,1)S(1)}, bf16[72]{0:T(256)(128)(2,1)}, u32[]{:S(2)}) copy-start(bf16[72]{0:T(256)(128)(2,1)} %param.47) | copy-start | bytes 436
  98.8 13.4 %copy-start.4 = (bf16[1152,72]{0,1:T(8,128)(2,1)S(1)}, bf16[1152,72]{0,1:T(8,128)(2,1)}, u32[]{:S(2)}) copy-start(bf16[1152,72]{0,1:T(8,128)(2,1)} %param.46) | copy-start | bytes 497668
  98.9 14.3 %copy-start.18 = (s32[1,4]{1,0:T(1,128)S(1)}, s32[1,4]{1,0:T(1,128)}, u32[]{:S(2)}) copy-start(s32[1,4]{1,0:T(1,128)} %param.33) | copy-start | bytes 52
  98.9 14.6 %copy-start.2 = (bf16[1,128,1152]{2,1,0:T(8,128)(2,1)S(1)}, bf16[1,128,1152]{2,1,0:T(8,128)(2,1)}, u32[]{:S(2)}) copy-start(bf16[1,128,1152]{2,1,0:T(8,128)(2,1)} %param.29) | copy-start | bytes 884740
  102.6 18.2 %all-to-all-start = ((bf16[16,4,576]{2,1,0:T(4,128)(2,1)}), bf16[16,4,576]{2,1,0:T(4,128)(2,1)S(1)}, u32[]{:S(2)}, u32[]{:S(2)}) async-start(bf16[16,4,576]{2,1,0:T(4,128)(2,1)} %reshape.206), calls=%async_computation | async-start | bytes 163840 | tf_op jit(solution)/shard_map/all_to_all | solution.py:103
  112.1 58.3 %all-gather.6.cloned.1.call-start = ((), (), s32[]{:S(2)}) async-start(), calls=%async_computation.6 | async-start | bytes 1566720 | tf_op jit(solution)/shard_map/all_gather | solution.py:122
  121.7 2.1 copy-start.1
  138.1 35.9 %all-to-all-start.1 = ((bf16[128,8,432]{0,2,1:T(8,128)(2,1)}), bf16[128,8,432]{0,2,1:T(8,128)(2,1)}, u32[]{:S(2)}, u32[]{:S(2)}) async-start(bf16[128,8,432]{0,2,1:T(8,128)(2,1)} %bitcast.96), calls=%async_computation.1 | async-start | bytes 1769472 | tf_op jit(solution)/shard_map/all_to_all | solution.py:144
  174.0 28.5 %collective-permute-start.1 = (bf16[592,1152]{1,0:T(8,128)(2,1)}, bf16[592,1152]{1,0:T(8,128)(2,1)}, u32[]{:S(2)}, u32[]{:S(2)}) collective-permute-start(bf16[592,1152]{1,0:T(8,128)(2,1)} %copy.89), channel_id=1, source_target_pairs={{0,1},{1,0},{2,3},{3,2},{4,5},{5,4},{6,7},{7,6},{8,9},{9,8},{10,11... | collective-permute-start | bytes 4091912 | tf_op jit(solution)/shard_map/ppermute | solution.py:125
  188.3 12.1 %all-to-all-start.2 = ((bf16[8,128,144]{1,2,0:T(8,128)(2,1)}), bf16[8,128,144]{1,2,0:T(8,128)(2,1)S(1)}, u32[]{:S(2)}, u32[]{:S(2)}) async-start(bf16[8,128,144]{1,2,0:T(8,128)(2,1)} %copy.87), calls=%async_computation.2 | async-start | bytes 589824 | tf_op jit(solution)/shard_map/all_to_all | solution.py:152
  192.6 39.5 %all-gather.8.cloned.1.call-start = ((), (), s32[]{:S(2)}) async-start(), calls=%async_computation.7 | async-start | bytes 2654208 | tf_op jit(solution)/shard_map/all_gather | solution.py:156
  200.4 2.1 copy-start.3
  204.6 2.5 copy-start.11
  207.0 70.6 %reduce-scatter.2.cloned.1.call-start = ((), (), s32[]{:S(2)}) async-start(), calls=%async_computation.8 | async-start | bytes 2654208 | tf_op jit(solution)/shard_map/reduce_scatter | solution.py:162
  240.0 0.7 copy-start.8
  240.0 0.7 copy-start.19
  240.0 39.3 %copy-start.5 = (bf16[1152,16]{0,1:T(8,128)(2,1)S(1)}, bf16[1152,16]{0,1:T(8,128)(2,1)}, u32[]{:S(2)}) copy-start(bf16[1152,16]{0,1:T(8,128)(2,1)} %param.52) | copy-start | bytes 110596
  240.7 44.0 %copy-start.15 = (f32[1,4]{1,0:T(1,128)S(1)}, f32[1,4]{1,0:T(1,128)}, u32[]{:S(2)}) copy-start(f32[1,4]{1,0:T(1,128)} %param.35) | copy-start | bytes 52
  240.7 44.0 %copy-start.16 = (f32[1,4]{1,0:T(1,128)S(1)}, f32[1,4]{1,0:T(1,128)}, u32[]{:S(2)}) copy-start(f32[1,4]{1,0:T(1,128)} %param.34) | copy-start | bytes 52
  240.7 44.0 %copy-start.17 = (f32[1,4]{1,0:T(1,128)S(1)}, f32[1,4]{1,0:T(1,128)}, u32[]{:S(2)}) copy-start(f32[1,4]{1,0:T(1,128)} %param.36) | copy-start | bytes 52
  240.7 47.8 %copy-start.9 = (f32[128,8]{0,1:T(8,128)S(1)}, f32[128,8]{0,1:T(8,128)}, u32[]{:S(2)}) copy-start(f32[128,8]{0,1:T(8,128)} %param.30) | copy-start | bytes 12292
  281.4 7.0 %all-to-all-start.3 = ((f32[1,128,16]{1,0,2:T(1,128)}), f32[1,128,16]{1,0,2:T(1,128)S(1)}, u32[]{:S(2)}, u32[]{:S(2)}) async-start(f32[1,128,16]{1,0,2:T(1,128)} %bitcast.21), calls=%async_computation.4 | async-start | bytes 16384 | tf_op jit(solution)/shard_map/all_to_all | solution.py:177
Sparse Core Ops, SparseCore 0:
  9.8 79.4 all-gather.3
  115.4 54.9 all-gather.5
  207.2 24.8 all-gather.7
  240.1 37.4 reduce-scatter.1

commit v2 on v1

--- a/solution.py
+++ b/solution.py
@@ -45,7 +45,7 @@
     return result.astype(jnp.bfloat16).reshape(queries.shape[0], -1)
 
 
-def shards(
+def block_body(
     hidden,
     noisy_latent,
     labels,
@@ -116,13 +116,24 @@
     half_rows = width // 2
     pair = [(index, index ^ 1) for index in range(mlp_count)]
 
-    def split_gather(weight, bias):
-        mine = lax.dynamic_slice_in_dim(weight, core * half_rows, half_rows, axis=0)
-        bias_rows = jnp.zeros((16, weight.shape[1]), weight.dtype).at[0].set(bias)
-        gathered = lax.all_gather(
-            jnp.concatenate([mine, bias_rows], axis=0), "req", axis=1, tiled=True
-        )
-        return gathered, lax.ppermute(gathered, "mlp", pair)
+    qkv_cols = qkv_weight.shape[1]
+    out_cols = out_weight.shape[1]
+    block = jnp.concatenate(
+        [
+            lax.dynamic_slice_in_dim(qkv_weight, core * half_rows, half_rows, axis=0),
+            lax.dynamic_slice_in_dim(out_weight, core * half_rows, half_rows, axis=0),
+        ],
+        axis=1,
+    )
+    bias_rows = jnp.zeros((16, qkv_cols + out_cols), block.dtype).at[0].set(
+        jnp.concatenate([qkv_bias, out_bias])
+    )
+    both = lax.all_gather(jnp.concatenate([block, bias_rows], axis=0), "req", axis=1, tiled=True)
+    both = both.reshape(half_rows + 16, req_count, qkv_cols + out_cols)
+    qkv_mine = both[:, :, :qkv_cols].reshape(half_rows + 16, req_count * qkv_cols)
+    out_mine = both[:, :, qkv_cols:].reshape(half_rows + 16, req_count * out_cols)
+    qkv_other = lax.ppermute(qkv_mine, "mlp", pair)
+    out_other = lax.ppermute(out_mine, "mlp", pair)
 
     def split_dot(values, mine, other):
         values_mine = lax.dynamic_slice_in_dim(values, core * half_rows, half_rows, axis=1)
@@ -133,8 +144,6 @@
             + mine[half_rows].astype(jnp.float32)
         )
 
-    qkv_mine, qkv_other = split_gather(qkv_weight, qkv_bias)
-    out_mine, out_other = split_gather(out_weight, out_bias)
     qkv = split_dot(normed, qkv_mine, qkv_other).astype(jnp.bfloat16)
     heads_per = HEADS // mlp_count
     head_cols = heads_per * HEAD_DIM
@@ -186,7 +195,7 @@
 
 def solution(mesh):
     return jax.shard_map(
-        shards,
+        block_body,
         mesh=mesh,
         in_specs=(
             P("cfg", ("req", "mlp"), None),

time: 297 us -> 301 us (1.013)
  local copies, waits for them, and re-layouts: 24.1 us -> 40.5 us
  waiting for transfers between devices: 185 us -> 169 us
  starting transfers between devices: 21.3 us -> 26.9 us
    all_gather x3 -> x2, waiting for transfers between devices: 131 us -> 111 us  [the longest x1 88.2 us: block_body(): lax.all_gather(jnp.concatenate([block, bias_rows], axis=0), 'req', axis=1...]
    slice x1 -> x6, local copies, waits for them, and re-layouts: 0.79 us -> 16.7 us  [the longest x2 7.41 us: split_dot(): mine[:half_rows]]
    reshape x1 -> x3, local copies, waits for them, and re-layouts: 0.65 us -> 11.3 us  [the longest x1 7.08 us: block_body(): both[:, :, :qkv_cols].reshape(half_rows + 16, req_count * qkv_cols)]
    all_gather x2 -> x0, local copies, waits for them, and re-layouts: 10.6 us -> none  [split_gather(): lax.all_gather(jnp.concatenate([mine, bias_rows], axis=0), 'req', axis=1,...]
    all_to_all x4, starting transfers between devices: 21.2 us -> 26.3 us  [the longest x1 15.4 us: block_body(): lax.all_to_all(local_mod, 'req', split_axis=0, concat_axis=2, tiled=True)[0]]
    all_to_all x4, waiting for transfers between devices: 17.2 us -> 21.3 us  [the longest x1 8 us: block_body(): lax.all_to_all(local_mod, 'req', split_axis=0, concat_axis=2, tiled=True)[0]]
    add x3 -> x1, other arithmetic: 3.63 us -> 0.6 us  [block_body(): keep_tok * noisy_latent]
  transfers between devices with their start and end apart: 10 -> 9, of which waited for: 7 -> 7; matrix products, arithmetic and copies ran while one was open for 16% -> 16% of each run, Pallas kernels for 0% -> 0%
where the time goes in v2:
time: 301 us; the launch traced here: 300 us
  waiting for transfers between devices  169 us (56%)
  local copies, waits for them, and re-layouts  40.5 us (13%)
  matrix products  39 us (13%)
  starting transfers between devices  26.9 us (9%)
  between operations  13.5 us (4%)
  other arithmetic  11 us (4%)
    all_gather x1, waiting for transfers between devices, block_body(): lax.all_gather(jnp.concatenate([block, bias_rows], axis=0), 'req', axis=1...  88.2 us
    reduce_scatter x1, waiting for transfers between devices, block_body(): lax.psum_scatter(jnp.dot(inner, down_weight, preferred_element_type=jnp.f...  37 us
    all_gather x1, waiting for transfers between devices, block_body(): gathered = lax.all_gather(normed_mlp, 'mlp', axis=0, tiled=True)  22.4 us
    all_to_all x1, starting transfers between devices, block_body(): lax.all_to_all(local_mod, 'req', split_axis=0, concat_axis=2, tiled=True)[0]  15.4 us
    sub x1, matrix products, attention(): expo = jnp.where(same, jnp.exp(masked - row_max), 0.0)  8.44 us
    all_to_all x1, waiting for transfers between devices, block_body(): lax.all_to_all(local_mod, 'req', split_axis=0, concat_axis=2, tiled=True)[0]  8 us
    dot_general x1, matrix products, block_body(): jnp.dot(inner, down_weight, preferred_element_type=jnp.float32)  7.81 us
    slice x2, local copies, waits for them, and re-layouts, split_dot(): mine[:half_rows]  7.41 us
  transfers between devices with their start and end apart: 9, of which 7 were waited for; matrix products, arithmetic and copies ran while one was open for 16% of the time, Pallas kernels for 0%

profile of v2, /device:TPU:8, one launch (start us, length us, event | category | flops | bytes accessed | tf_op | source)
XLA Modules:
  0.0 299.8 jit_solution(15664262957505312257)
XLA Ops:
  10.6 88.2 %all-gather.3.cloned.1.call-done = bf16[592,4608]{0,1:T(8,128)(2,1)} async-done(((bf16[592,288]{0,1:T(8,128)(2,1)}), bf16[592,4608]{0,1:T(8,128)(2,1)}) %all-gather.3.cloned.1.call-update) | async-done | bytes 5455888 | tf_op jit(solution)/shard_map/all_gather | solution.py:131
  98.7 4.7 %slice.118 = bf16[592,16,216]{0,2,1:T(8,128)(2,1)} slice(bf16[592,16,288]{0,2,1:T(8,128)(2,1)} %bitcast.102), slice={[0:592], [0:16], [0:216]} | slice | bytes 8183808 | tf_op jit(solution)/shard_map/slice | solution.py:133
  103.5 7.1 %copy.86 = bf16[592,3456]{1,0:T(8,128)(2,1)} copy(bf16[592,3456]{0,1:T(8,128)(2,1)} %bitcast.109) | data formatting | bytes 8183808 | tf_op jit(solution)/shard_map/reshape | solution.py:133
  111.2 1.8 convolution_add_fusion.3
  113.1 3.0 %fusion.33 = bf16[64,576]{1,0:T(8,128)(2,1)S(1)} fusion(bf16[1152,576]{0,1:T(8,128)(2,1)} %param.40, f32[64,1152]{1,0:T(8,128)S(1)} %convolution_add_fusion.3, bf16[1001,1152]{1,0:T(8,128)(2,1)} %param.35, s32[64]{0:T(128)S(1)} %select_n.45, f32[576]{0:T(1024)S(1)} %convert_element_type.114), kind=kOutput, calls=%fused_computation.39 | convolution fusion | flops 233118272 | bytes 4004608 | tf_op jit(solution)/shard_map/dot_general | solution.py:99
  116.7 15.4 %all-to-all-start = ((bf16[16,4,576]{2,1,0:T(4,128)(2,1)}), bf16[16,4,576]{2,1,0:T(4,128)(2,1)S(1)}, u32[]{:S(2)}, u32[]{:S(2)}) async-start(bf16[16,4,576]{2,1,0:T(4,128)(2,1)} %reshape.210), calls=%async_computation | async-start | bytes 163840 | tf_op jit(solution)/shard_map/all_to_all | solution.py:103
  132.9 8.0 %all-to-all-done = bf16[16,4,576]{2,1,0:T(4,128)(2,1)S(1)} async-done(((bf16[16,4,576]{2,1,0:T(4,128)(2,1)}), bf16[16,4,576]{2,1,0:T(4,128)(2,1)S(1)}, u32[]{:S(2)}, u32[]{:S(2)}) %all-to-all-start) | async-done | bytes 73760 | tf_op jit(solution)/shard_map/all_to_all | solution.py:103
  141.9 2.2 copy-done.1
  144.3 4.8 %slice.117 = bf16[576,16,216]{0,2,1:T(8,128)(2,1)} slice(bf16[592,16,288]{0,2,1:T(8,128)(2,1)} %bitcast.103), slice={[0:576], [0:16], [0:216]} | slice | bytes 7962624 | tf_op jit(solution)/shard_map/slice | solution.py:142
  149.1 1.8 convert_reduce_fusion
  151.1 3.7 %fusion.52 = f32[128,3456]{1,0:T(8,128)S(1)} fusion(bf16[576,3456]{0,1:T(8,128)(2,1)} %bitcast.108, bf16[128,1152]{1,0:T(8,128)(2,1)S(1)} %fusion.43, s32[]{:T(128)S(6)} %select_n.47), kind=kOutput, calls=%fused_computation.72 | convolution fusion | flops 509607936 | bytes 5914628 | tf_op jit(solution)/shard_map/dot_general | solution.py:142
  154.8 4.1 %fusion.3 = bf16[128,3456]{1,0:T(8,128)(2,1)} fusion(f32[128,3456]{1,0:T(8,128)S(1)} %fusion.52, bf16[592,3456]{1,0:T(8,128)(2,1)} %collective-permute-done, f32[3456]{0:T(1024)S(1)} %reshape.219, bf16[128,1152]{1,0:T(8,128)(2,1)S(1)} %fusion.43, s32[]{:T(128)S(6)} %select_n.48), kind=kOutput, calls=%fused_computation.6 | convolution fusion | flops 510935040 | bytes 6815748 | tf_op jit(solution)/shard_map/dot_general | solution.py:143
  158.9 2.2 copy.87
  161.1 2.2 copy.88
  163.3 4.2 %all-to-all-start.1 = ((bf16[128,8,432]{0,2,1:T(8,128)(2,1)}), bf16[128,8,432]{0,2,1:T(8,128)(2,1)}, u32[]{:S(2)}, u32[]{:S(2)}) async-start(bf16[128,8,432]{0,2,1:T(8,128)(2,1)} %bitcast.112), calls=%async_computation.1 | async-start | bytes 1769472 | tf_op jit(solution)/shard_map/all_to_all | solution.py:153
  169.2 2.6 slice.125
  171.8 3.6 %copy.92 = bf16[592,1152]{1,0:T(8,128)(2,1)} copy(bf16[592,1152]{0,1:T(8,128)(2,1)} %bitcast.111) | data formatting | bytes 2727936 | tf_op jit(solution)/shard_map/reshape | solution.py:134
  175.8 5.9 %all-to-all-done.1 = bf16[128,8,432]{0,2,1:T(8,128)(2,1)} async-done(((bf16[128,8,432]{0,2,1:T(8,128)(2,1)}), bf16[128,8,432]{0,2,1:T(8,128)(2,1)}, u32[]{:S(2)}, u32[]{:S(2)}) %all-to-all-start.1) | async-done | bytes 884768 | tf_op jit(solution)/shard_map/all_to_all | solution.py:153
  183.8 8.4 %fusion.95 = (f32[2,1024]{1,0:T(2,128)S(1)}, bf16[2,1024,1024]{1,2,0:T(8,128)(2,1)}) fusion(pred[1024,1024]{0,1:T(8,128)(4,1)} %broadcast_compare_fusion, bf16[1024,2,72]{0,2,1:T(8,128)(2,1)} %bitcast.120, bf16[1024,2,72]{0,2,1:T(8,128)(2,1)S(1)} %bitcast.119), kind=kOutput, calls=%fused_computation.130 | convolution fusion | flops 314573824 | bytes 5840896 | tf_op jit(solution)/shard_map/sub | solution.py:40
  192.3 3.0 %fusion.30 = bf16[1024,2,72]{0,2,1:T(8,128)(2,1)S(1)} fusion(bf16[1024,2,72]{0,2,1:T(8,128)(2,1)S(1)} %bitcast.118, bf16[2,1024,1024]{1,2,0:T(8,128)(2,1)} %get-tuple-element.28, f32[1024,2]{0,1:T(2,128)S(1)} %bitcast.128), kind=kOutput, calls=%fused_computation.37 | convolution fusion | flops 302284800 | bytes 4792320 | tf_op jit(solution)/shard_map/hqk,khd->qhd/dot_general | solution.py:43
  196.1 3.4 %all-to-all-start.2 = ((bf16[8,128,144]{1,2,0:T(8,128)(2,1)}), bf16[8,128,144]{1,2,0:T(8,128)(2,1)S(1)}, u32[]{:S(2)}, u32[]{:S(2)}) async-start(bf16[8,128,144]{1,2,0:T(8,128)(2,1)} %copy.91), calls=%async_computation.2 | async-start | bytes 589824 | tf_op jit(solution)/shard_map/all_to_all | solution.py:161
  200.7 2.6 slice.124
  203.6 3.7 %all-to-all-done.2 = bf16[8,128,144]{1,2,0:T(8,128)(2,1)S(1)} async-done(((bf16[8,128,144]{1,2,0:T(8,128)(2,1)}), bf16[8,128,144]{1,2,0:T(8,128)(2,1)S(1)}, u32[]{:S(2)}, u32[]{:S(2)}) %all-to-all-start.2) | async-done | bytes 294944 | tf_op jit(solution)/shard_map/all_to_all | solution.py:161
  207.3 2.1 fusion.55
  209.4 2.1 fusion.96
  211.8 2.2 fusion.46
  214.0 22.4 %all-gather.5.cloned.1.call-done = bf16[1024,1152]{1,0:T(8,128)(2,1)} async-done(((bf16[128,1152]{1,0:T(8,128)(2,1)}), bf16[1024,1152]{1,0:T(8,128)(2,1)}) %all-gather.5.cloned.1.call-update) | async-done | bytes 2359312 | tf_op jit(solution)/shard_map/all_gather | solution.py:165
  236.4 7.8 %convolution_convert_fusion = bf16[1024,1152]{1,0:T(8,128)(2,1)} fusion(bf16[576,1152]{1,0:T(8,128)(2,1)} %param.48, bf16[1024,1152]{1,0:T(8,128)(2,1)} %all-gather.5.cloned.1.call-done, bf16[1152,576]{0,1:T(8,128)(2,1)} %param.46, f32[576]{0:T(1024)S(1)} %convert_element_type.127), kind=kOutput, calls=%fused_computation.13 | convolution fusion | flops 2724986880 | bytes 7375104 | tf_op jit(solution)/shard_map/dot_general | solution.py:172
  244.9 37.0 %reduce-scatter.2.cloned.1.call-done = bf16[128,1152]{1,0:T(8,128)(2,1)} async-done(((bf16[1024,1152]{1,0:T(8,128)(2,1)}), bf16[128,1152]{1,0:T(8,128)(2,1)}) %reduce-scatter.2.cloned.1.call-update) | async-done | bytes 294928 | tf_op jit(solution)/shard_map/reduce_scatter | solution.py:171
  283.4 2.2 convolution_add_fusion.6
  285.6 3.2 %all-to-all-start.3 = ((f32[1,128,16]{1,0,2:T(1,128)}), f32[1,128,16]{1,0,2:T(1,128)S(1)}, u32[]{:S(2)}, u32[]{:S(2)}) async-start(f32[1,128,16]{1,0,2:T(1,128)} %bitcast.25), calls=%async_computation.4 | async-start | bytes 16384 | tf_op jit(solution)/shard_map/all_to_all | solution.py:186
  288.9 3.7 %all-to-all-done.3 = f32[1,128,16]{1,0,2:T(1,128)S(1)} async-done(((f32[1,128,16]{1,0,2:T(1,128)}), f32[1,128,16]{1,0,2:T(1,128)S(1)}, u32[]{:S(2)}, u32[]{:S(2)}) %all-to-all-start.3) | async-done | bytes 8224 | tf_op jit(solution)/shard_map/all_to_all | solution.py:186
  (94 shorter events, 17.0 us)
Async XLA Ops:
  6.5 104.7 %copy-start = (bf16[1152,1152]{1,0:T(8,128)(2,1)S(1)}, bf16[1152,1152]{1,0:T(8,128)(2,1)}, u32[]{:S(2)}) copy-start(bf16[1152,1152]{1,0:T(8,128)(2,1)} %param.38) | copy-start | bytes 7962628
  6.5 92.2 %all-gather.3.cloned.1.call-start = ((), (), s32[]{:S(2)}) async-start(), calls=%async_computation.5 | async-start | bytes 6266880 | tf_op jit(solution)/shard_map/all_gather | solution.py:131
  103.5 7.1 %copy-start.11 = (s32[16,4]{0,1:T(4,128)S(1)}, s32[16,4]{0,1:T(4,128)}, u32[]{:S(2)}) copy-start(s32[16,4]{0,1:T(4,128)} %param.30) | copy-start | bytes 772
  103.5 7.1 %copy-start.9 = (bf16[576]{0:T(1024)(128)(2,1)S(1)}, bf16[576]{0:T(1024)(128)(2,1)}, u32[]{:S(2)}) copy-start(bf16[576]{0:T(1024)(128)(2,1)} %param.41) | copy-start | bytes 3460
  103.5 7.3 %copy-start.12 = (s32[16,4]{0,1:T(4,128)S(1)}, s32[16,4]{0,1:T(4,128)}, u32[]{:S(2)}) copy-start(s32[16,4]{0,1:T(4,128)} %param.29) | copy-start | bytes 772
  103.5 7.5 %copy-start.5 = (bf16[1152]{0:T(1024)(128)(2,1)S(1)}, bf16[1152]{0:T(1024)(128)(2,1)}, u32[]{:S(2)}) copy-start(bf16[1152]{0:T(1024)(128)(2,1)} %param.37) | copy-start | bytes 6916
  103.5 7.5 %copy-start.6 = (bf16[1152]{0:T(1024)(128)(2,1)S(1)}, bf16[1152]{0:T(1024)(128)(2,1)}, u32[]{:S(2)}) copy-start(bf16[1152]{0:T(1024)(128)(2,1)} %param.39) | copy-start | bytes 6916
  110.6 44.3 %collective-permute-start = (bf16[592,3456]{1,0:T(8,128)(2,1)}, bf16[592,3456]{1,0:T(8,128)(2,1)}, u32[]{:S(2)}, u32[]{:S(2)}) collective-permute-start(bf16[592,3456]{1,0:T(8,128)(2,1)} %copy.86), channel_id=1, source_target_pairs={{0,1},{1,0},{2,3},{3,2},{4,5},{5,4},{6,7},{7,6},{8,9},{9,8},{10,11... | collective-permute-start | bytes 12275720 | tf_op jit(solution)/shard_map/ppermute | solution.py:135
  113.0 19.1 %copy-start.16 = (s32[1,4]{1,0:T(1,128)S(1)}, s32[1,4]{1,0:T(1,128)}, u32[]{:S(2)}) copy-start(s32[1,4]{1,0:T(1,128)} %param.31) | copy-start | bytes 52
  113.0 19.5 %copy-start.2 = (bf16[1,128,1152]{2,1,0:T(8,128)(2,1)S(1)}, bf16[1,128,1152]{2,1,0:T(8,128)(2,1)}, u32[]{:S(2)}) copy-start(bf16[1,128,1152]{2,1,0:T(8,128)(2,1)} %param.27) | copy-start | bytes 884740
  116.7 24.2 %all-to-all-start = ((bf16[16,4,576]{2,1,0:T(4,128)(2,1)}), bf16[16,4,576]{2,1,0:T(4,128)(2,1)S(1)}, u32[]{:S(2)}, u32[]{:S(2)}) async-start(bf16[16,4,576]{2,1,0:T(4,128)(2,1)} %reshape.210), calls=%async_computation | async-start | bytes 163840 | tf_op jit(solution)/shard_map/all_to_all | solution.py:103
  141.9 2.2 copy-start.1
  163.3 18.5 %all-to-all-start.1 = ((bf16[128,8,432]{0,2,1:T(8,128)(2,1)}), bf16[128,8,432]{0,2,1:T(8,128)(2,1)}, u32[]{:S(2)}, u32[]{:S(2)}) async-start(bf16[128,8,432]{0,2,1:T(8,128)(2,1)} %bitcast.112), calls=%async_computation.1 | async-start | bytes 1769472 | tf_op jit(solution)/shard_map/all_to_all | solution.py:153
  175.3 34.1 %collective-permute-start.1 = (bf16[592,1152]{1,0:T(8,128)(2,1)}, bf16[592,1152]{1,0:T(8,128)(2,1)}, u32[]{:S(2)}, u32[]{:S(2)}) collective-permute-start(bf16[592,1152]{1,0:T(8,128)(2,1)} %copy.92), channel_id=1, source_target_pairs={{0,1},{1,0},{2,3},{3,2},{4,5},{5,4},{6,7},{7,6},{8,9},{9,8},{10,11... | collective-permute-start | bytes 4091912 | tf_op jit(solution)/shard_map/ppermute | solution.py:136
  196.1 11.2 %all-to-all-start.2 = ((bf16[8,128,144]{1,2,0:T(8,128)(2,1)}), bf16[8,128,144]{1,2,0:T(8,128)(2,1)S(1)}, u32[]{:S(2)}, u32[]{:S(2)}) async-start(bf16[8,128,144]{1,2,0:T(8,128)(2,1)} %copy.91), calls=%async_computation.2 | async-start | bytes 589824 | tf_op jit(solution)/shard_map/all_to_all | solution.py:161
  199.5 36.8 %all-gather.5.cloned.1.call-start = ((), (), s32[]{:S(2)}) async-start(), calls=%async_computation.6 | async-start | bytes 2654208 | tf_op jit(solution)/shard_map/all_gather | solution.py:165
  207.3 2.1 copy-start.3
  211.5 2.5 copy-start.10
  213.9 67.9 %reduce-scatter.2.cloned.1.call-start = ((), (), s32[]{:S(2)}) async-start(), calls=%async_computation.7 | async-start | bytes 2654208 | tf_op jit(solution)/shard_map/reduce_scatter | solution.py:171
  244.2 0.7 copy-start.17
  244.2 0.7 copy-start.7
  244.2 39.2 %copy-start.4 = (bf16[1152,16]{0,1:T(8,128)(2,1)S(1)}, bf16[1152,16]{0,1:T(8,128)(2,1)}, u32[]{:S(2)}) copy-start(bf16[1152,16]{0,1:T(8,128)(2,1)} %param.50) | copy-start | bytes 110596
  244.8 44.0 %copy-start.13 = (f32[1,4]{1,0:T(1,128)S(1)}, f32[1,4]{1,0:T(1,128)}, u32[]{:S(2)}) copy-start(f32[1,4]{1,0:T(1,128)} %param.33) | copy-start | bytes 52
  244.8 44.0 %copy-start.14 = (f32[1,4]{1,0:T(1,128)S(1)}, f32[1,4]{1,0:T(1,128)}, u32[]{:S(2)}) copy-start(f32[1,4]{1,0:T(1,128)} %param.32) | copy-start | bytes 52
  244.8 44.0 %copy-start.15 = (f32[1,4]{1,0:T(1,128)S(1)}, f32[1,4]{1,0:T(1,128)}, u32[]{:S(2)}) copy-start(f32[1,4]{1,0:T(1,128)} %param.34) | copy-start | bytes 52
  244.9 47.8 %copy-start.8 = (f32[128,8]{0,1:T(8,128)S(1)}, f32[128,8]{0,1:T(8,128)}, u32[]{:S(2)}) copy-start(f32[128,8]{0,1:T(8,128)} %param.28) | copy-start | bytes 12292
  285.6 7.0 %all-to-all-start.3 = ((f32[1,128,16]{1,0,2:T(1,128)}), f32[1,128,16]{1,0,2:T(1,128)S(1)}, u32[]{:S(2)}, u32[]{:S(2)}) async-start(f32[1,128,16]{1,0,2:T(1,128)} %bitcast.25), calls=%async_computation.4 | async-start | bytes 16384 | tf_op jit(solution)/shard_map/all_to_all | solution.py:186
Sparse Core Ops, SparseCore 0:
  10.7 88.0 all-gather.2
  214.1 22.2 all-gather.4
  244.3 37.4 reduce-scatter.1

commit v3 on v2

--- a/solution.py
+++ b/solution.py
@@ -128,23 +128,35 @@
     bias_rows = jnp.zeros((16, qkv_cols + out_cols), block.dtype).at[0].set(
         jnp.concatenate([qkv_bias, out_bias])
     )
-    both = lax.all_gather(jnp.concatenate([block, bias_rows], axis=0), "req", axis=1, tiled=True)
-    both = both.reshape(half_rows + 16, req_count, qkv_cols + out_cols)
-    qkv_mine = both[:, :, :qkv_cols].reshape(half_rows + 16, req_count * qkv_cols)
-    out_mine = both[:, :, qkv_cols:].reshape(half_rows + 16, req_count * out_cols)
-    qkv_other = lax.ppermute(qkv_mine, "mlp", pair)
-    out_other = lax.ppermute(out_mine, "mlp", pair)
-
-    def split_dot(values, mine, other):
-        values_mine = lax.dynamic_slice_in_dim(values, core * half_rows, half_rows, axis=1)
-        values_other = lax.dynamic_slice_in_dim(values, (1 - core) * half_rows, half_rows, axis=1)
-        return (
-            jnp.dot(values_mine, mine[:half_rows], preferred_element_type=jnp.float32)
-            + jnp.dot(values_other, other[:half_rows], preferred_element_type=jnp.float32)
-            + mine[half_rows].astype(jnp.float32)
+    both = lax.all_gather(
+        jnp.transpose(jnp.concatenate([block, bias_rows], axis=0)), "req", axis=0, tiled=True
+    )
+    both_other = lax.ppermute(both, "mlp", pair)
+    bias_pick = (jnp.arange(16) == 0).astype(jnp.bfloat16)
+
+    def wide_dot(values):
+        values_mine = jnp.concatenate(
+            [
+                lax.dynamic_slice_in_dim(values, core * half_rows, half_rows, axis=1),
+                jnp.broadcast_to(bias_pick, (values.shape[0], 16)),
+            ],
+            axis=1,
         )
-
-    qkv = split_dot(normed, qkv_mine, qkv_other).astype(jnp.bfloat16)
+        values_other = jnp.concatenate(
+            [
+                lax.dynamic_slice_in_dim(values, (1 - core) * half_rows, half_rows, axis=1),
+                jnp.zeros((values.shape[0], 16), jnp.bfloat16),
+            ],
+            axis=1,
+        )
+        contract = (((1,), (1,)), ((), ()))
+        wide = lax.dot_general(
+            both, values_mine, contract, preferred_element_type=jnp.float32
+        ) + lax.dot_general(both_other, values_other, contract, preferred_element_type=jnp.float32)
+        return jnp.transpose(wide).reshape(values.shape[0], req_count, qkv_cols + out_cols)
+
+    qkv = wide_dot(normed)[:, :, :qkv_cols].reshape(tok_rows, req_count * qkv_cols)
+    qkv = qkv.astype(jnp.bfloat16)
     heads_per = HEADS // mlp_count
     head_cols = heads_per * HEAD_DIM
     packed = jnp.transpose(
@@ -159,21 +171,34 @@
         segment_all,
     )
     attended = lax.all_to_all(attended_heads, "mlp", split_axis=0, concat_axis=1, tiled=True)
-    projected = split_dot(attended, out_mine, out_other)
+    projected = wide_dot(attended)[:, :, qkv_cols:].reshape(tok_rows, req_count * out_cols)
     mid_hidden = (rows.astype(jnp.float32) + gate_attn * projected).astype(jnp.bfloat16)
     normed_mlp = (layer_norm(mid_hidden) * (1.0 + scale_mlp) + shift_mlp).astype(jnp.bfloat16)
-    gathered = lax.all_gather(normed_mlp, "mlp", axis=0, tiled=True)
+    gathered = lax.all_to_all(
+        jnp.broadcast_to(normed_mlp[None], (mlp_count,) + normed_mlp.shape),
+        "mlp",
+        split_axis=0,
+        concat_axis=0,
+        tiled=True,
+    ).reshape(group_rows, width)
     inner = jax.nn.gelu(
         jnp.dot(gathered, up_weight, preferred_element_type=jnp.float32)
         + up_bias.astype(jnp.float32),
         approximate=True,
     ).astype(jnp.bfloat16)
-    mlp_out = lax.psum_scatter(
-        jnp.dot(inner, down_weight, preferred_element_type=jnp.float32).astype(jnp.bfloat16),
-        "mlp",
-        scatter_dimension=0,
-        tiled=True,
-    ).astype(jnp.float32)
+    partial_out = jnp.dot(inner, down_weight, preferred_element_type=jnp.float32).astype(
+        jnp.bfloat16
+    )
+    mlp_out = jnp.sum(
+        lax.all_to_all(
+            partial_out.reshape(mlp_count, tok_rows, width),
+            "mlp",
+            split_axis=0,
+            concat_axis=0,
+            tiled=True,
+        ).astype(jnp.float32),
+        axis=0,
+    )
     final_hidden = mid_hidden.astype(jnp.float32) + gate_mlp * (
         mlp_out + down_bias.astype(jnp.float32)
     )

time: 301 us -> 307 us (1.020)
  local copies, waits for them, and re-layouts: 40.5 us -> 21.8 us
  blocking collectives: 0 us -> 10.2 us
  matrix products: 39 us -> 44.7 us
  starting transfers between devices: 26.9 us -> 31.1 us
    all_to_all x1 -> x2, waiting for transfers between devices: 3.69 us -> 59.8 us  [the longest x1 29.9 us: block_body(): lax.all_to_all(partial_out.reshape(mlp_count, tok_rows, width), 'mlp', sp...]
    reduce_scatter x1 -> x0, waiting for transfers between devices: 37 us -> none  [block_body(): lax.psum_scatter(jnp.dot(inner, down_weight, preferred_element_type=jnp.f...]
    all_gather x2 -> x1, waiting for transfers between devices: 111 us -> 88.1 us  [block_body(): lax.all_gather(jnp.transpose(jnp.concatenate([block, bias_rows], axis=0))...]
    slice x5 -> x2, local copies, waits for them, and re-layouts: 15.9 us -> 0.11 us  [the longest x1 0.06 us: block_body(): wide_dot(normed)[:, :, :qkv_cols].reshape(tok_rows, req_count * qkv_cols)]
    reshape x2 -> x1, local copies, waits for them, and re-layouts: 10.6 us -> 0.23 us  [block_body(): wide_dot(attended)[:, :, qkv_cols:].reshape(tok_rows, req_count * out_cols)]
    all_to_all x0 -> x1, blocking collectives: none -> 10.2 us  [block_body(): lax.all_to_all(attended_heads, 'mlp', split_axis=0, concat_axis=1, tiled=...]
    all_gather x0 -> x1, local copies, waits for them, and re-layouts: none -> 8.77 us  [block_body(): lax.all_gather(jnp.transpose(jnp.concatenate([block, bias_rows], axis=0))...]
    dot_general x4, matrix products: 11.9 us -> 19.4 us  [the longest x2 9.88 us: wide_dot(): lax.dot_general(both_other, values_other, contract, preferred_element_typ...]
  transfers between devices with their start and end apart: 9 -> 7, of which waited for: 7 -> 6; matrix products, arithmetic and copies ran while one was open for 16% -> 5% of each run, Pallas kernels for 0% -> 0%
where the time goes in v3:
time: 307 us; the launch traced here: 306 us
  waiting for transfers between devices  172 us (56%)
  matrix products  44.7 us (15%)
  starting transfers between devices  31.1 us (10%)
  local copies, waits for them, and re-layouts  21.8 us (7%)
  between operations  13.9 us (5%)
  other arithmetic  11.8 us (4%)
  blocking collectives  10.2 us (3%)
    all_gather x1, waiting for transfers between devices, block_body(): lax.all_gather(jnp.transpose(jnp.concatenate([block, bias_rows], axis=0))...  88.1 us
    all_to_all x1, waiting for transfers between devices, block_body(): lax.all_to_all(partial_out.reshape(mlp_count, tok_rows, width), 'mlp', sp...  29.9 us
    all_to_all x1, waiting for transfers between devices, block_body(): lax.all_to_all(jnp.broadcast_to(normed_mlp[None], (mlp_count,) + normed_m...  29.9 us
    all_to_all x1, starting transfers between devices, block_body(): lax.all_to_all(local_mod, 'req', split_axis=0, concat_axis=2, tiled=True)[0]  15.4 us
    all_to_all x1, waiting for transfers between devices, block_body(): lax.all_to_all(packed, 'mlp', split_axis=1, concat_axis=0, tiled=True)  12.5 us
    all_to_all x1, blocking collectives, block_body(): lax.all_to_all(attended_heads, 'mlp', split_axis=0, concat_axis=1, tiled=...  10.2 us
    dot_general x2, matrix products, wide_dot(): lax.dot_general(both_other, values_other, contract, preferred_element_typ...  9.88 us
    dot_general x2, matrix products, wide_dot(): lax.dot_general(both, values_mine, contract, preferred_element_type=jnp.f...  9.55 us
  transfers between devices with their start and end apart: 7, of which 6 were waited for; matrix products, arithmetic and copies ran while one was open for 5% of the time, Pallas kernels for 0%

profile of v3, /device:TPU:8, one launch (start us, length us, event | category | flops | bytes accessed | tf_op | source)
XLA Modules:
  0.0 305.6 jit_solution(16565618758011187320)
XLA Ops:
  6.5 1.3 constant_dynamic-slice_fusion.4
  10.6 88.1 %all-gather.2.cloned.1.call-done = bf16[4608,592]{1,0:T(8,128)(2,1)} async-done(((bf16[288,592]{1,0:T(8,128)(2,1)}), bf16[4608,592]{1,0:T(8,128)(2,1)}) %all-gather.2.cloned.1.call-update) | async-done | bytes 5455888 | tf_op jit(solution)/shard_map/all_gather | solution.py:131
  98.7 8.8 %copy.89 = bf16[4608,592]{0,1:T(8,128)(2,1)} copy(bf16[4608,592]{1,0:T(8,128)(2,1)} %all-gather.2.cloned.1.call-done) | data formatting | bytes 10911744 | tf_op jit(solution)/shard_map/all_gather | solution.py:131
  108.2 1.8 convolution_add_fusion.3
  110.0 3.0 fusion.25
  113.7 15.4 %all-to-all-start = ((bf16[16,4,576]{2,1,0:T(4,128)(2,1)}), bf16[16,4,576]{2,1,0:T(4,128)(2,1)S(1)}, u32[]{:S(2)}, u32[]{:S(2)}) async-start(bf16[16,4,576]{2,1,0:T(4,128)(2,1)} %reshape.199), calls=%async_computation | async-start | bytes 163840 | tf_op jit(solution)/shard_map/all_to_all | solution.py:103
  129.9 7.9 %all-to-all-done = bf16[16,4,576]{2,1,0:T(4,128)(2,1)S(1)} async-done(((bf16[16,4,576]{2,1,0:T(4,128)(2,1)}), bf16[16,4,576]{2,1,0:T(4,128)(2,1)S(1)}, u32[]{:S(2)}, u32[]{:S(2)}) %all-to-all-start) | async-done | bytes 73760 | tf_op jit(solution)/shard_map/all_to_all | solution.py:103
  138.8 2.1 copy-done.2
  141.4 4.7 %fusion.49 = f32[128,4608]{1,0:T(8,128)S(1)} fusion(bf16[4608,592]{1,0:T(8,128)(2,1)} %all-gather.2.cloned.1.call-done, bf16[128,576]{1,0:T(8,128)(2,1)S(1)} %get-tuple-element.30, bf16[592]{0:T(1024)(128)(2,1)S(1)} %pad.13.clone), kind=kOutput, calls=%fused_computation.71 | convolution fusion | flops 698654720 | bytes 7963808 | tf_op jit(solution)/shard_map/dot_general | solution.py:153
  146.1 4.7 %fusion.2 = bf16[128,4608]{1,0:T(8,128)(2,1)} fusion(f32[128,4608]{1,0:T(8,128)S(1)} %fusion.49, bf16[4608,592]{0,1:T(8,128)(2,1)} %collective-permute-done, bf16[128,576]{1,0:T(8,128)(2,1)S(1)} %get-tuple-element.29), kind=kOutput, calls=%fused_computation.6 | convolution fusion | flops 699531264 | bytes 9142272 | tf_op jit(solution)/shard_map/dot_general | solution.py:155
  150.9 1.7 copy.90
  153.6 4.2 %all-to-all-start.1 = ((bf16[128,8,432]{0,2,1:T(8,128)(2,1)}), bf16[128,8,432]{0,2,1:T(8,128)(2,1)S(1)}, u32[]{:S(2)}, u32[]{:S(2)}) async-start(bf16[128,8,432]{0,2,1:T(8,128)(2,1)} %bitcast.11), calls=%async_computation.1 | async-start | bytes 1769472 | tf_op jit(solution)/shard_map/all_to_all | solution.py:165
  157.8 1.6 broadcast_compare_fusion
  159.4 12.5 %all-to-all-done.1 = bf16[128,8,432]{0,2,1:T(8,128)(2,1)S(1)} async-done(((bf16[128,8,432]{0,2,1:T(8,128)(2,1)}), bf16[128,8,432]{0,2,1:T(8,128)(2,1)S(1)}, u32[]{:S(2)}, u32[]{:S(2)}) %all-to-all-start.1) | async-done | bytes 884768 | tf_op jit(solution)/shard_map/all_to_all | solution.py:165
  172.1 7.3 %fusion.97 = (f32[2,1024]{1,0:T(2,128)S(1)}, bf16[2,1024,1024]{1,2,0:T(8,128)(2,1)}) fusion(pred[1024,1024]{0,1:T(8,128)(4,1)} %broadcast_compare_fusion, bf16[1024,2,72]{0,2,1:T(8,128)(2,1)S(1)} %bitcast.120, bf16[1024,2,72]{0,2,1:T(8,128)(2,1)S(1)} %bitcast.119), kind=kOutput, calls=%fused_computation.139 | convolution fusion | flops 314573824 | bytes 5840896 | tf_op jit(solution)/shard_map/sub | solution.py:40
  179.5 3.0 fusion.22
  182.6 10.2 %all_to_all.78 = bf16[8,128,144]{1,2,0:T(8,128)(2,1)S(1)} all-to-all(bf16[8,128,144]{1,2,0:T(8,128)(2,1)S(1)} %copy.94), channel_id=1, replica_groups=mesh['cfg'=2,'req'=16,'mlp'=8] {'mlp'}, dimensions={0} | all-to-all | bytes 589824 | tf_op jit(solution)/shard_map/all_to_all | solution.py:173
  192.9 4.8 %fusion.53 = f32[128,4608]{1,0:T(8,128)S(1)} fusion(bf16[4608,592]{1,0:T(8,128)(2,1)} %all-gather.2.cloned.1.call-done, bf16[128,576]{0,1:T(8,128)(2,1)S(1)} %get-tuple-element.28, bf16[592]{0:T(1024)(128)(2,1)S(1)} %pad.13.clone), kind=kOutput, calls=%fused_computation.75 | convolution fusion | flops 698654720 | bytes 7963808 | tf_op jit(solution)/shard_map/dot_general | solution.py:153
  197.7 5.2 %convolution_add_fusion = f32[128,4608]{1,0:T(8,128)} fusion(f32[128,4608]{1,0:T(8,128)S(1)} %fusion.53, bf16[4608,592]{0,1:T(8,128)(2,1)} %collective-permute-done, bf16[128,576]{0,1:T(8,128)(2,1)S(1)} %get-tuple-element.27), kind=kOutput, calls=%fused_computation.4 | convolution fusion | flops 698941440 | bytes 10321920 | tf_op jit(solution)/shard_map/dot_general | solution.py:155
  202.9 2.0 copy.96
  206.7 1.5 fusion.38
  208.2 1.7 broadcast_in_dim.35
  209.9 3.7 %all-to-all-start.3 = ((bf16[8,128,1152]{2,1,0:T(8,128)(2,1)}), bf16[8,128,1152]{2,1,0:T(8,128)(2,1)S(1)}, u32[]{:S(2)}, u32[]{:S(2)}) async-start(bf16[8,128,1152]{2,1,0:T(8,128)(2,1)} %broadcast_in_dim.35), calls=%async_computation.3 | async-start | bytes 4718592 | tf_op jit(solution)/shard_map/all_to_all | solution.py:177
  213.7 29.9 %all-to-all-done.3 = bf16[8,128,1152]{2,1,0:T(8,128)(2,1)S(1)} async-done(((bf16[8,128,1152]{2,1,0:T(8,128)(2,1)}), bf16[8,128,1152]{2,1,0:T(8,128)(2,1)S(1)}, u32[]{:S(2)}, u32[]{:S(2)}) %all-to-all-start.3) | async-done | bytes 2359328 | tf_op jit(solution)/shard_map/all_to_all | solution.py:177
  243.6 7.1 %convolution_convert_fusion = bf16[1024,1152]{1,0:T(8,128)(2,1)} fusion(bf16[576,1152]{1,0:T(8,128)(2,1)} %param.48, bf16[1024,1152]{1,0:T(8,128)(2,1)S(1)} %bitcast.112, bf16[1152,576]{0,1:T(8,128)(2,1)} %param.46, f32[576]{0:T(1024)S(1)} %convert_element_type.111), kind=kOutput, calls=%fused_computation.13 | convolution fusion | flops 2724986880 | bytes 7375104 | tf_op jit(solution)/shard_map/dot_general | solution.py:189
  250.7 4.5 %all-to-all-start.4 = ((bf16[8,128,1152]{2,1,0:T(8,128)(2,1)}), bf16[8,128,1152]{2,1,0:T(8,128)(2,1)}, u32[]{:S(2)}, u32[]{:S(2)}) async-start(bf16[8,128,1152]{2,1,0:T(8,128)(2,1)} %bitcast.113), calls=%async_computation.4 | async-start | bytes 4718592 | tf_op jit(solution)/shard_map/all_to_all | solution.py:193
  255.2 29.9 %all-to-all-done.4 = bf16[8,128,1152]{2,1,0:T(8,128)(2,1)} async-done(((bf16[8,128,1152]{2,1,0:T(8,128)(2,1)}), bf16[8,128,1152]{2,1,0:T(8,128)(2,1)}, u32[]{:S(2)}, u32[]{:S(2)}) %all-to-all-start.4) | async-done | bytes 2359328 | tf_op jit(solution)/shard_map/all_to_all | solution.py:193
  285.2 2.2 convert_reduce_fusion
  287.4 1.3 fusion.94
  288.9 2.2 convolution_add_fusion.6
  291.1 3.2 %all-to-all-start.5 = ((f32[1,128,16]{1,0,2:T(1,128)}), f32[1,128,16]{1,0,2:T(1,128)S(1)}, u32[]{:S(2)}, u32[]{:S(2)}) async-start(f32[1,128,16]{1,0,2:T(1,128)} %bitcast.26), calls=%async_computation.5 | async-start | bytes 16384 | tf_op jit(solution)/shard_map/all_to_all | solution.py:211
  294.4 3.7 %all-to-all-done.5 = f32[1,128,16]{1,0,2:T(1,128)S(1)} async-done(((f32[1,128,16]{1,0,2:T(1,128)}), f32[1,128,16]{1,0,2:T(1,128)S(1)}, u32[]{:S(2)}, u32[]{:S(2)}) %all-to-all-start.5) | async-done | bytes 8224 | tf_op jit(solution)/shard_map/all_to_all | solution.py:211
  (90 shorter events, 10.2 us)
Async XLA Ops:
  6.5 101.6 %copy-start = (bf16[1152,1152]{1,0:T(8,128)(2,1)S(1)}, bf16[1152,1152]{1,0:T(8,128)(2,1)}, u32[]{:S(2)}) copy-start(bf16[1152,1152]{1,0:T(8,128)(2,1)} %param.38) | copy-start | bytes 7962628
  6.5 92.2 %all-gather.2.cloned.1.call-start = ((), (), s32[]{:S(2)}) async-start(), calls=%async_computation.6 | async-start | bytes 6266880 | tf_op jit(solution)/shard_map/all_gather | solution.py:131
  10.5 97.0 %copy-start.11 = (s32[16,4]{0,1:T(4,128)S(1)}, s32[16,4]{0,1:T(4,128)}, u32[]{:S(2)}) copy-start(s32[16,4]{0,1:T(4,128)} %param.30) | copy-start | bytes 772
  10.6 97.1 %copy-start.5 = (bf16[1152]{0:T(1024)(128)(2,1)S(1)}, bf16[1152]{0:T(1024)(128)(2,1)}, u32[]{:S(2)}) copy-start(bf16[1152]{0:T(1024)(128)(2,1)} %param.37) | copy-start | bytes 6916
  10.6 97.1 %copy-start.6 = (bf16[1152]{0:T(1024)(128)(2,1)S(1)}, bf16[1152]{0:T(1024)(128)(2,1)}, u32[]{:S(2)}) copy-start(bf16[1152]{0:T(1024)(128)(2,1)} %param.39) | copy-start | bytes 6916
  10.6 97.2 %copy-start.12 = (s32[16,4]{0,1:T(4,128)S(1)}, s32[16,4]{0,1:T(4,128)}, u32[]{:S(2)}) copy-start(s32[16,4]{0,1:T(4,128)} %param.29) | copy-start | bytes 772
  10.6 97.3 %copy-start.9 = (bf16[576]{0:T(1024)(128)(2,1)S(1)}, bf16[576]{0:T(1024)(128)(2,1)}, u32[]{:S(2)}) copy-start(bf16[576]{0:T(1024)(128)(2,1)} %param.41) | copy-start | bytes 3460
  107.5 38.6 %collective-permute-start = (bf16[4608,592]{0,1:T(8,128)(2,1)}, bf16[4608,592]{0,1:T(8,128)(2,1)}, u32[]{:S(2)}, u32[]{:S(2)}) collective-permute-start(bf16[4608,592]{0,1:T(8,128)(2,1)} %copy.89), channel_id=1, source_target_pairs={{0,1},{1,0},{2,3},{3,2},{4,5},{5,4},{6,7},{7,6},{8,9},{9,8},{10,11... | collective-permute-start | bytes 16367624 | tf_op jit(solution)/shard_map/ppermute | solution.py:134
  110.0 19.1 %copy-start.16 = (s32[1,4]{1,0:T(1,128)S(1)}, s32[1,4]{1,0:T(1,128)}, u32[]{:S(2)}) copy-start(s32[1,4]{1,0:T(1,128)} %param.31) | copy-start | bytes 52
  110.0 19.6 %copy-start.3 = (bf16[1,128,1152]{2,1,0:T(8,128)(2,1)S(1)}, bf16[1,128,1152]{2,1,0:T(8,128)(2,1)}, u32[]{:S(2)}) copy-start(bf16[1,128,1152]{2,1,0:T(8,128)(2,1)} %param.27) | copy-start | bytes 884740
  113.7 24.2 %all-to-all-start = ((bf16[16,4,576]{2,1,0:T(4,128)(2,1)}), bf16[16,4,576]{2,1,0:T(4,128)(2,1)S(1)}, u32[]{:S(2)}, u32[]{:S(2)}) async-start(bf16[16,4,576]{2,1,0:T(4,128)(2,1)} %reshape.199), calls=%async_computation | async-start | bytes 163840 | tf_op jit(solution)/shard_map/all_to_all | solution.py:103
  138.8 2.1 copy-start.2
  153.6 18.4 %all-to-all-start.1 = ((bf16[128,8,432]{0,2,1:T(8,128)(2,1)}), bf16[128,8,432]{0,2,1:T(8,128)(2,1)S(1)}, u32[]{:S(2)}, u32[]{:S(2)}) async-start(bf16[128,8,432]{0,2,1:T(8,128)(2,1)} %bitcast.11), calls=%async_computation.1 | async-start | bytes 1769472 | tf_op jit(solution)/shard_map/all_to_all | solution.py:165
  209.9 3.8 %copy-start.10 = (bf16[576]{0:T(1024)(128)(2,1)S(1)}, bf16[576]{0:T(1024)(128)(2,1)}, u32[]{:S(2)}) copy-start(bf16[576]{0:T(1024)(128)(2,1)} %param.47) | copy-start | bytes 3460
  209.9 33.7 %all-to-all-start.3 = ((bf16[8,128,1152]{2,1,0:T(8,128)(2,1)}), bf16[8,128,1152]{2,1,0:T(8,128)(2,1)S(1)}, u32[]{:S(2)}, u32[]{:S(2)}) async-start(bf16[8,128,1152]{2,1,0:T(8,128)(2,1)} %broadcast_in_dim.35), calls=%async_computation.3 | async-start | bytes 4718592 | tf_op jit(solution)/shard_map/all_to_all | solution.py:177
  250.7 4.5 %copy-start.7 = (bf16[1152]{0:T(1024)(128)(2,1)S(1)}, bf16[1152]{0:T(1024)(128)(2,1)}, u32[]{:S(2)}) copy-start(bf16[1152]{0:T(1024)(128)(2,1)} %param.49) | copy-start | bytes 6916
  250.7 4.5 %copy-start.17 = (bf16[16]{0:T(256)(128)(2,1)S(1)}, bf16[16]{0:T(256)(128)(2,1)}, u32[]{:S(2)}) copy-start(bf16[16]{0:T(256)(128)(2,1)} %param.51) | copy-start | bytes 100
  250.7 34.5 %all-to-all-start.4 = ((bf16[8,128,1152]{2,1,0:T(8,128)(2,1)}), bf16[8,128,1152]{2,1,0:T(8,128)(2,1)}, u32[]{:S(2)}, u32[]{:S(2)}) async-start(bf16[8,128,1152]{2,1,0:T(8,128)(2,1)} %bitcast.113), calls=%async_computation.4 | async-start | bytes 4718592 | tf_op jit(solution)/shard_map/all_to_all | solution.py:193
  255.2 33.7 %copy-start.4 = (bf16[1152,16]{0,1:T(8,128)(2,1)S(1)}, bf16[1152,16]{0,1:T(8,128)(2,1)}, u32[]{:S(2)}) copy-start(bf16[1152,16]{0,1:T(8,128)(2,1)} %param.50) | copy-start | bytes 110596
  285.2 13.6 %copy-start.1 = (bf16[1152,1152]{1,0:T(8,128)(2,1)S(1)}, bf16[1152,1152]{1,0:T(8,128)(2,1)}, u32[]{:S(2)}) copy-start(bf16[1152,1152]{1,0:T(8,128)(2,1)} %param.38) | copy-start | bytes 7962628
  287.4 7.0 %copy-start.13 = (f32[1,4]{1,0:T(1,128)S(1)}, f32[1,4]{1,0:T(1,128)}, u32[]{:S(2)}) copy-start(f32[1,4]{1,0:T(1,128)} %param.33) | copy-start | bytes 52
  287.4 7.0 %copy-start.14 = (f32[1,4]{1,0:T(1,128)S(1)}, f32[1,4]{1,0:T(1,128)}, u32[]{:S(2)}) copy-start(f32[1,4]{1,0:T(1,128)} %param.32) | copy-start | bytes 52
  287.4 7.0 %copy-start.15 = (f32[1,4]{1,0:T(1,128)S(1)}, f32[1,4]{1,0:T(1,128)}, u32[]{:S(2)}) copy-start(f32[1,4]{1,0:T(1,128)} %param.34) | copy-start | bytes 52
  287.4 10.7 %copy-start.8 = (f32[128,8]{0,1:T(8,128)S(1)}, f32[128,8]{0,1:T(8,128)}, u32[]{:S(2)}) copy-start(f32[128,8]{0,1:T(8,128)} %param.28) | copy-start | bytes 12292
  291.1 7.0 %all-to-all-start.5 = ((f32[1,128,16]{1,0,2:T(1,128)}), f32[1,128,16]{1,0,2:T(1,128)S(1)}, u32[]{:S(2)}, u32[]{:S(2)}) async-start(f32[1,128,16]{1,0,2:T(1,128)} %bitcast.26), calls=%async_computation.5 | async-start | bytes 16384 | tf_op jit(solution)/shard_map/all_to_all | solution.py:211
Sparse Core Ops, SparseCore 0:
  10.7 88.0 all-gather.1

commit v4 on v1

--- a/solution.py
+++ b/solution.py
@@ -45,7 +45,7 @@
     return result.astype(jnp.bfloat16).reshape(queries.shape[0], -1)
 
 
-def shards(
+def block_body(
     hidden,
     noisy_latent,
     labels,
@@ -116,13 +116,19 @@
     half_rows = width // 2
     pair = [(index, index ^ 1) for index in range(mlp_count)]
 
-    def split_gather(weight, bias):
+    def half_gather(weight, bias):
         mine = lax.dynamic_slice_in_dim(weight, core * half_rows, half_rows, axis=0)
         bias_rows = jnp.zeros((16, weight.shape[1]), weight.dtype).at[0].set(bias)
         gathered = lax.all_gather(
             jnp.concatenate([mine, bias_rows], axis=0), "req", axis=1, tiled=True
         )
-        return gathered, lax.ppermute(gathered, "mlp", pair)
+        return gathered
+
+    qkv_mine = half_gather(qkv_weight, qkv_bias)
+    out_weight, out_bias, modulation = lax.optimization_barrier((out_weight, out_bias, modulation))
+    out_mine = half_gather(out_weight, out_bias)
+    qkv_other = lax.ppermute(qkv_mine, "mlp", pair)
+    out_other = lax.ppermute(out_mine, "mlp", pair)
 
     def split_dot(values, mine, other):
         values_mine = lax.dynamic_slice_in_dim(values, core * half_rows, half_rows, axis=1)
@@ -133,8 +139,6 @@
             + mine[half_rows].astype(jnp.float32)
         )
 
-    qkv_mine, qkv_other = split_gather(qkv_weight, qkv_bias)
-    out_mine, out_other = split_gather(out_weight, out_bias)
     qkv = split_dot(normed, qkv_mine, qkv_other).astype(jnp.bfloat16)
     heads_per = HEADS // mlp_count
     head_cols = heads_per * HEAD_DIM
@@ -186,7 +190,7 @@
 
 def solution(mesh):
     return jax.shard_map(
-        shards,
+        block_body,
         mesh=mesh,
         in_specs=(
             P("cfg", ("req", "mlp"), None),

time: 297 us -> 298 us (level)
  transfers between devices with their start and end apart: 10 -> 10, of which waited for: 7 -> 7; matrix products, arithmetic and copies ran while one was open for 16% -> 15% of each run, Pallas kernels for 0% -> 0%
where the time goes in v4:
time: 298 us; the launch traced here: 297 us
  waiting for transfers between devices  187 us (63%)
  matrix products  39.1 us (13%)
  local copies, waits for them, and re-layouts  24.1 us (8%)
  starting transfers between devices  21.3 us (7%)
  between operations  13.6 us (5%)
  other arithmetic  12 us (4%)
    all_gather x2, waiting for transfers between devices, half_gather(): lax.all_gather(jnp.concatenate([mine, bias_rows], axis=0), 'req', axis=1,...  107 us
    reduce_scatter x1, waiting for transfers between devices, block_body(): lax.psum_scatter(jnp.dot(inner, down_weight, preferred_element_type=jnp.f...  36.9 us
    all_gather x1, waiting for transfers between devices, block_body(): gathered = lax.all_gather(normed_mlp, 'mlp', axis=0, tiled=True)  25 us
    all_gather x2, local copies, waits for them, and re-layouts, half_gather(): lax.all_gather(jnp.concatenate([mine, bias_rows], axis=0), 'req', axis=1,...  10.6 us
    all_to_all x1, starting transfers between devices, block_body(): lax.all_to_all(local_mod, 'req', split_axis=0, concat_axis=2, tiled=True)[0]  9.51 us
    sub x1, matrix products, attention(): expo = jnp.where(same, jnp.exp(masked - row_max), 0.0)  8.43 us
    all_to_all x1, waiting for transfers between devices, block_body(): lax.all_to_all(local_mod, 'req', split_axis=0, concat_axis=2, tiled=True)[0]  7.89 us
    dot_general x1, matrix products, block_body(): jnp.dot(inner, down_weight, preferred_element_type=jnp.float32)  7.88 us
  transfers between devices with their start and end apart: 10, of which 7 were waited for; matrix products, arithmetic and copies ran while one was open for 15% of the time, Pallas kernels for 0%

profile of v4, /device:TPU:8, one launch (start us, length us, event | category | flops | bytes accessed | tf_op | source)
XLA Modules:
  0.0 297.2 jit_solution(9793444150371890816)
XLA Ops:
  9.5 79.9 %all-gather.4.cloned.1.call-done = bf16[592,3456]{0,1:T(8,128)(2,1)} async-done(((bf16[592,216]{0,1:T(8,128)(2,1)}), bf16[592,3456]{0,1:T(8,128)(2,1)}) %all-gather.4.cloned.1.call-update) | async-done | bytes 4091920 | tf_op jit(solution)/shard_map/all_gather | solution.py:122
  89.3 7.0 %copy.82 = bf16[592,3456]{1,0:T(8,128)(2,1)} copy(bf16[592,3456]{0,1:T(8,128)(2,1)} %all-gather.4.cloned.1.call-done) | data formatting | bytes 8183808 | tf_op jit(solution)/shard_map/all_gather | solution.py:122
  97.0 1.8 convolution_add_fusion.3
  98.9 3.0 %fusion.37 = bf16[64,576]{1,0:T(8,128)(2,1)S(1)} fusion(bf16[1152,576]{0,1:T(8,128)(2,1)} %param.42, f32[64,1152]{1,0:T(8,128)S(1)} %convolution_add_fusion.3, bf16[1001,1152]{1,0:T(8,128)(2,1)} %param.37, s32[64]{0:T(128)S(1)} %select_n.45, f32[576]{0:T(1024)S(1)} %convert_element_type.98), kind=kOutput, calls=%fused_computation.43 | convolution fusion | flops 233118272 | bytes 4004608 | tf_op jit(solution)/shard_map/dot_general | solution.py:99
  102.5 9.5 %all-to-all-start = ((bf16[16,4,576]{2,1,0:T(4,128)(2,1)}), bf16[16,4,576]{2,1,0:T(4,128)(2,1)S(1)}, u32[]{:S(2)}, u32[]{:S(2)}) async-start(bf16[16,4,576]{2,1,0:T(4,128)(2,1)} %reshape.206), calls=%async_computation | async-start | bytes 163840 | tf_op jit(solution)/shard_map/all_to_all | solution.py:103
  112.8 7.9 %all-to-all-done = bf16[16,4,576]{2,1,0:T(4,128)(2,1)S(1)} async-done(((bf16[16,4,576]{2,1,0:T(4,128)(2,1)}), bf16[16,4,576]{2,1,0:T(4,128)(2,1)S(1)}, u32[]{:S(2)}, u32[]{:S(2)}) %all-to-all-start) | async-done | bytes 73760 | tf_op jit(solution)/shard_map/all_to_all | solution.py:103
  122.7 2.1 copy-done.1
  125.1 1.8 convert_reduce_fusion
  126.9 3.7 %fusion.4 = f32[128,3456]{1,0:T(8,128)S(1)} fusion(bf16[592,3456]{0,1:T(8,128)(2,1)} %all-gather.4.cloned.1.call-done, bf16[128,1152]{1,0:T(8,128)(2,1)S(1)} %fusion.46, s32[]{:T(128)S(6)} %select_n.47), kind=kOutput, calls=%fused_computation.7 | convolution fusion | flops 509607936 | bytes 6025220 | tf_op jit(solution)/shard_map/dot_general | solution.py:137
  130.6 4.1 %fusion.3 = bf16[128,3456]{1,0:T(8,128)(2,1)} fusion(f32[128,3456]{1,0:T(8,128)S(1)} %fusion.4, bf16[592,3456]{1,0:T(8,128)(2,1)} %collective-permute-done, f32[3456]{0:T(1024)S(1)} %convert_reduce_fusion, bf16[128,1152]{1,0:T(8,128)(2,1)S(1)} %fusion.46, s32[]{:T(128)S(6)} %select_n.48), kind=kOutput, calls=%fused_computation.6 | convolution fusion | flops 510935040 | bytes 6815748 | tf_op jit(solution)/shard_map/dot_general | solution.py:138
  134.7 2.2 copy.83
  136.9 2.2 copy.84
  139.1 4.2 %all-to-all-start.1 = ((bf16[128,8,432]{0,2,1:T(8,128)(2,1)}), bf16[128,8,432]{0,2,1:T(8,128)(2,1)}, u32[]{:S(2)}, u32[]{:S(2)}) async-start(bf16[128,8,432]{0,2,1:T(8,128)(2,1)} %bitcast.96), calls=%async_computation.1 | async-start | bytes 1769472 | tf_op jit(solution)/shard_map/all_to_all | solution.py:148
  143.3 1.6 broadcast_compare_fusion
  145.0 27.0 %all-gather.6.cloned.1.call-done = bf16[592,1152]{0,1:T(8,128)(2,1)} async-done(((bf16[592,72]{0,1:T(8,128)(2,1)}), bf16[592,1152]{0,1:T(8,128)(2,1)}) %all-gather.6.cloned.1.call-update) | async-done | bytes 1363984 | tf_op jit(solution)/shard_map/all_gather | solution.py:122
  172.0 3.6 %copy.89 = bf16[592,1152]{1,0:T(8,128)(2,1)} copy(bf16[592,1152]{0,1:T(8,128)(2,1)} %all-gather.6.cloned.1.call-done) | data formatting | bytes 2727936 | tf_op jit(solution)/shard_map/all_gather | solution.py:122
  175.6 1.3 copy_bitcast_fusion
  177.7 8.4 %fusion.99 = (f32[2,1024]{1,0:T(2,128)S(1)}, bf16[2,1024,1024]{1,2,0:T(8,128)(2,1)}) fusion(pred[1024,1024]{0,1:T(8,128)(4,1)} %broadcast_compare_fusion, bf16[1024,2,72]{0,2,1:T(8,128)(2,1)} %bitcast.104, bf16[1024,2,72]{0,2,1:T(8,128)(2,1)S(1)} %bitcast.103), kind=kOutput, calls=%fused_computation.135 | convolution fusion | flops 314573824 | bytes 5840896 | tf_op jit(solution)/shard_map/sub | solution.py:40
  186.1 3.0 %fusion.34 = bf16[1024,2,72]{0,2,1:T(8,128)(2,1)S(1)} fusion(bf16[1024,2,72]{0,2,1:T(8,128)(2,1)S(1)} %bitcast.102, bf16[2,1024,1024]{1,2,0:T(8,128)(2,1)} %get-tuple-element.44, f32[1024,2]{0,1:T(2,128)S(1)} %bitcast.113), kind=kOutput, calls=%fused_computation.41 | convolution fusion | flops 302284800 | bytes 4792320 | tf_op jit(solution)/shard_map/hqk,khd->qhd/dot_general | solution.py:43
  190.0 4.2 %all-to-all-start.2 = ((bf16[8,128,144]{1,2,0:T(8,128)(2,1)}), bf16[8,128,144]{1,2,0:T(8,128)(2,1)S(1)}, u32[]{:S(2)}, u32[]{:S(2)}) async-start(bf16[8,128,144]{1,2,0:T(8,128)(2,1)} %copy.87), calls=%async_computation.2 | async-start | bytes 589824 | tf_op jit(solution)/shard_map/all_to_all | solution.py:156
  194.2 1.2 convert_reduce_fusion.2
  195.5 6.6 %all-to-all-done.2 = bf16[8,128,144]{1,2,0:T(8,128)(2,1)S(1)} async-done(((bf16[8,128,144]{1,2,0:T(8,128)(2,1)}), bf16[8,128,144]{1,2,0:T(8,128)(2,1)S(1)}, u32[]{:S(2)}, u32[]{:S(2)}) %all-to-all-start.2) | async-done | bytes 294944 | tf_op jit(solution)/shard_map/all_to_all | solution.py:156
  202.1 2.1 fusion.25
  204.1 2.1 fusion.100
  206.5 2.2 fusion.49
  208.8 25.0 %all-gather.8.cloned.1.call-done = bf16[1024,1152]{1,0:T(8,128)(2,1)} async-done(((bf16[128,1152]{1,0:T(8,128)(2,1)}), bf16[1024,1152]{1,0:T(8,128)(2,1)}) %all-gather.8.cloned.1.call-update) | async-done | bytes 2359312 | tf_op jit(solution)/shard_map/all_gather | solution.py:160
  233.7 7.9 %convolution_convert_fusion = bf16[1024,1152]{1,0:T(8,128)(2,1)} fusion(bf16[576,1152]{1,0:T(8,128)(2,1)} %param.50, bf16[1024,1152]{1,0:T(8,128)(2,1)} %all-gather.8.cloned.1.call-done, bf16[1152,576]{0,1:T(8,128)(2,1)} %param.48, f32[576]{0:T(1024)S(1)} %convert_element_type.107), kind=kOutput, calls=%fused_computation.15 | convolution fusion | flops 2724986880 | bytes 7375104 | tf_op jit(solution)/shard_map/dot_general | solution.py:167
  242.4 36.9 %reduce-scatter.2.cloned.1.call-done = bf16[128,1152]{1,0:T(8,128)(2,1)} async-done(((bf16[1024,1152]{1,0:T(8,128)(2,1)}), bf16[128,1152]{1,0:T(8,128)(2,1)}) %reduce-scatter.2.cloned.1.call-update) | async-done | bytes 294928 | tf_op jit(solution)/shard_map/reduce_scatter | solution.py:166
  279.3 1.3 fusion.96
  280.9 2.2 convolution_add_fusion.6
  283.0 3.2 %all-to-all-start.3 = ((f32[1,128,16]{1,0,2:T(1,128)}), f32[1,128,16]{1,0,2:T(1,128)S(1)}, u32[]{:S(2)}, u32[]{:S(2)}) async-start(f32[1,128,16]{1,0,2:T(1,128)} %bitcast.21), calls=%async_computation.4 | async-start | bytes 16384 | tf_op jit(solution)/shard_map/all_to_all | solution.py:181
  286.4 3.7 %all-to-all-done.3 = f32[1,128,16]{1,0,2:T(1,128)S(1)} async-done(((f32[1,128,16]{1,0,2:T(1,128)}), f32[1,128,16]{1,0,2:T(1,128)S(1)}, u32[]{:S(2)}, u32[]{:S(2)}) %all-to-all-start.3) | async-done | bytes 8224 | tf_op jit(solution)/shard_map/all_to_all | solution.py:181
  (95 shorter events, 10.6 us)
Async XLA Ops:
  6.5 90.5 %copy-start = (bf16[1152,1152]{1,0:T(8,128)(2,1)S(1)}, bf16[1152,1152]{1,0:T(8,128)(2,1)}, u32[]{:S(2)}) copy-start(bf16[1152,1152]{1,0:T(8,128)(2,1)} %param.40) | copy-start | bytes 7962628
  6.5 82.8 %all-gather.4.cloned.1.call-start = ((), (), s32[]{:S(2)}) async-start(), calls=%async_computation.5 | async-start | bytes 4700160 | tf_op jit(solution)/shard_map/all_gather | solution.py:122
  9.4 87.0 %copy-start.12 = (s32[16,4]{0,1:T(4,128)S(1)}, s32[16,4]{0,1:T(4,128)}, u32[]{:S(2)}) copy-start(s32[16,4]{0,1:T(4,128)} %param.32) | copy-start | bytes 772
  9.4 87.1 %copy-start.6 = (bf16[1152]{0:T(1024)(128)(2,1)S(1)}, bf16[1152]{0:T(1024)(128)(2,1)}, u32[]{:S(2)}) copy-start(bf16[1152]{0:T(1024)(128)(2,1)} %param.39) | copy-start | bytes 6916
  9.4 87.1 %copy-start.7 = (bf16[1152]{0:T(1024)(128)(2,1)S(1)}, bf16[1152]{0:T(1024)(128)(2,1)}, u32[]{:S(2)}) copy-start(bf16[1152]{0:T(1024)(128)(2,1)} %param.41) | copy-start | bytes 6916
  9.4 87.1 %copy-start.13 = (s32[16,4]{0,1:T(4,128)S(1)}, s32[16,4]{0,1:T(4,128)}, u32[]{:S(2)}) copy-start(s32[16,4]{0,1:T(4,128)} %param.31) | copy-start | bytes 772
  9.4 87.3 %copy-start.10 = (bf16[576]{0:T(1024)(128)(2,1)S(1)}, bf16[576]{0:T(1024)(128)(2,1)}, u32[]{:S(2)}) copy-start(bf16[576]{0:T(1024)(128)(2,1)} %param.43) | copy-start | bytes 3460
  96.3 34.3 %collective-permute-start = (bf16[592,3456]{1,0:T(8,128)(2,1)}, bf16[592,3456]{1,0:T(8,128)(2,1)}, u32[]{:S(2)}, u32[]{:S(2)}) collective-permute-start(bf16[592,3456]{1,0:T(8,128)(2,1)} %copy.82), channel_id=1, source_target_pairs={{0,1},{1,0},{2,3},{3,2},{4,5},{5,4},{6,7},{7,6},{8,9},{9,8},{10,11... | collective-permute-start | bytes 12275720 | tf_op jit(solution)/shard_map/ppermute | solution.py:130
  98.8 13.3 %copy-start.18 = (s32[1,4]{1,0:T(1,128)S(1)}, s32[1,4]{1,0:T(1,128)}, u32[]{:S(2)}) copy-start(s32[1,4]{1,0:T(1,128)} %param.33) | copy-start | bytes 52
  98.8 13.6 %copy-start.2 = (bf16[1,128,1152]{2,1,0:T(8,128)(2,1)S(1)}, bf16[1,128,1152]{2,1,0:T(8,128)(2,1)}, u32[]{:S(2)}) copy-start(bf16[1,128,1152]{2,1,0:T(8,128)(2,1)} %param.29) | copy-start | bytes 884740
  98.9 22.0 %copy-start.14 = (bf16[72]{0:T(256)(128)(2,1)S(1)}, bf16[72]{0:T(256)(128)(2,1)}, u32[]{:S(2)}) copy-start(bf16[72]{0:T(256)(128)(2,1)} %param.47) | copy-start | bytes 436
  98.9 22.2 %copy-start.4 = (bf16[1152,72]{0,1:T(8,128)(2,1)S(1)}, bf16[1152,72]{0,1:T(8,128)(2,1)}, u32[]{:S(2)}) copy-start(bf16[1152,72]{0,1:T(8,128)(2,1)} %param.46) | copy-start | bytes 497668
  102.5 18.2 %all-to-all-start = ((bf16[16,4,576]{2,1,0:T(4,128)(2,1)}), bf16[16,4,576]{2,1,0:T(4,128)(2,1)S(1)}, u32[]{:S(2)}, u32[]{:S(2)}) async-start(bf16[16,4,576]{2,1,0:T(4,128)(2,1)} %reshape.206), calls=%async_computation | async-start | bytes 163840 | tf_op jit(solution)/shard_map/all_to_all | solution.py:103
  112.1 60.0 %all-gather.6.cloned.1.call-start = ((), (), s32[]{:S(2)}) async-start(), calls=%async_computation.6 | async-start | bytes 1566720 | tf_op jit(solution)/shard_map/all_gather | solution.py:122
  122.7 2.1 copy-start.1
  139.1 36.5 %all-to-all-start.1 = ((bf16[128,8,432]{0,2,1:T(8,128)(2,1)}), bf16[128,8,432]{0,2,1:T(8,128)(2,1)}, u32[]{:S(2)}, u32[]{:S(2)}) async-start(bf16[128,8,432]{0,2,1:T(8,128)(2,1)} %bitcast.96), calls=%async_computation.1 | async-start | bytes 1769472 | tf_op jit(solution)/shard_map/all_to_all | solution.py:148
  175.6 28.5 %collective-permute-start.1 = (bf16[592,1152]{1,0:T(8,128)(2,1)}, bf16[592,1152]{1,0:T(8,128)(2,1)}, u32[]{:S(2)}, u32[]{:S(2)}) collective-permute-start(bf16[592,1152]{1,0:T(8,128)(2,1)} %copy.89), channel_id=1, source_target_pairs={{0,1},{1,0},{2,3},{3,2},{4,5},{5,4},{6,7},{7,6},{8,9},{9,8},{10,11... | collective-permute-start | bytes 4091912 | tf_op jit(solution)/shard_map/ppermute | solution.py:131
  190.0 12.1 %all-to-all-start.2 = ((bf16[8,128,144]{1,2,0:T(8,128)(2,1)}), bf16[8,128,144]{1,2,0:T(8,128)(2,1)S(1)}, u32[]{:S(2)}, u32[]{:S(2)}) async-start(bf16[8,128,144]{1,2,0:T(8,128)(2,1)} %copy.87), calls=%async_computation.2 | async-start | bytes 589824 | tf_op jit(solution)/shard_map/all_to_all | solution.py:156
  194.2 39.5 %all-gather.8.cloned.1.call-start = ((), (), s32[]{:S(2)}) async-start(), calls=%async_computation.7 | async-start | bytes 2654208 | tf_op jit(solution)/shard_map/all_gather | solution.py:160
  202.1 2.1 copy-start.3
  206.2 2.5 copy-start.11
  208.7 70.6 %reduce-scatter.2.cloned.1.call-start = ((), (), s32[]{:S(2)}) async-start(), calls=%async_computation.8 | async-start | bytes 2654208 | tf_op jit(solution)/shard_map/reduce_scatter | solution.py:166
  241.6 0.7 copy-start.8
  241.6 0.7 copy-start.19
  241.6 39.2 %copy-start.5 = (bf16[1152,16]{0,1:T(8,128)(2,1)S(1)}, bf16[1152,16]{0,1:T(8,128)(2,1)}, u32[]{:S(2)}) copy-start(bf16[1152,16]{0,1:T(8,128)(2,1)} %param.52) | copy-start | bytes 110596
  242.3 43.9 %copy-start.15 = (f32[1,4]{1,0:T(1,128)S(1)}, f32[1,4]{1,0:T(1,128)}, u32[]{:S(2)}) copy-start(f32[1,4]{1,0:T(1,128)} %param.35) | copy-start | bytes 52
  242.3 44.0 %copy-start.16 = (f32[1,4]{1,0:T(1,128)S(1)}, f32[1,4]{1,0:T(1,128)}, u32[]{:S(2)}) copy-start(f32[1,4]{1,0:T(1,128)} %param.34) | copy-start | bytes 52
  242.3 44.0 %copy-start.17 = (f32[1,4]{1,0:T(1,128)S(1)}, f32[1,4]{1,0:T(1,128)}, u32[]{:S(2)}) copy-start(f32[1,4]{1,0:T(1,128)} %param.36) | copy-start | bytes 52
  242.3 47.7 %copy-start.9 = (f32[128,8]{0,1:T(8,128)S(1)}, f32[128,8]{0,1:T(8,128)}, u32[]{:S(2)}) copy-start(f32[128,8]{0,1:T(8,128)} %param.30) | copy-start | bytes 12292
  283.0 7.0 %all-to-all-start.3 = ((f32[1,128,16]{1,0,2:T(1,128)}), f32[1,128,16]{1,0,2:T(1,128)S(1)}, u32[]{:S(2)}, u32[]{:S(2)}) async-start(f32[1,128,16]{1,0,2:T(1,128)} %bitcast.21), calls=%async_computation.4 | async-start | bytes 16384 | tf_op jit(solution)/shard_map/all_to_all | solution.py:181
Sparse Core Ops, SparseCore 0:
  9.8 79.4 all-gather.3
  122.0 50.0 all-gather.5
  208.8 24.8 all-gather.7
  241.8 37.4 reduce-scatter.1

commit v5 on v4

--- a/solution.py
+++ b/solution.py
@@ -178,9 +178,15 @@
     predicted = jnp.dot(
         normed_final, final_weight, preferred_element_type=jnp.float32
     ) + final_bias.astype(jnp.float32)
-    halves = lax.all_to_all(predicted[None], "cfg", split_axis=2, concat_axis=0, tiled=True)
-    eps_cond = halves[0]
-    eps_free = halves[1]
+    own_cols = noisy_latent.shape[1]
+    kept = lax.dynamic_slice_in_dim(predicted, half_index * own_cols, own_cols, axis=1)
+    received = lax.ppermute(
+        lax.dynamic_slice_in_dim(predicted, (1 - half_index) * own_cols, own_cols, axis=1),
+        "cfg",
+        [(0, 1), (1, 0)],
+    )
+    eps_cond = jnp.where(half_index == 0, kept, received)
+    eps_free = jnp.where(half_index == 0, received, kept)
     member_f = member.astype(jnp.float32)
     guide_tok = jnp.sum(member_f * guidance, axis=1, keepdims=True)
     keep_tok = jnp.sum(member_f * keep_scale, axis=1, keepdims=True)

time: 298 us -> 294 us (0.987)
    all_to_all x1 -> x0, waiting for transfers between devices: 3.68 us -> none  [block_body(): lax.all_to_all(predicted[None], 'cfg', split_axis=2, concat_axis=0, tiled...]
    all_to_all x1 -> x0, starting transfers between devices: 3.22 us -> none  [block_body(): lax.all_to_all(predicted[None], 'cfg', split_axis=2, concat_axis=0, tiled...]
  transfers between devices with their start and end apart: 10 -> 10, of which waited for: 7 -> 7; matrix products, arithmetic and copies ran while one was open for 15% -> 16% of each run, Pallas kernels for 0% -> 0%
where the time goes in v5:
time: 294 us; the launch traced here: 293 us
  waiting for transfers between devices  185 us (63%)
  matrix products  38.5 us (13%)
  local copies, waits for them, and re-layouts  24.1 us (8%)
  starting transfers between devices  19.7 us (7%)
  between operations  13.5 us (5%)
  other arithmetic  12 us (4%)
    all_gather x2, waiting for transfers between devices, half_gather(): lax.all_gather(jnp.concatenate([mine, bias_rows], axis=0), 'req', axis=1,...  107 us
    reduce_scatter x1, waiting for transfers between devices, block_body(): lax.psum_scatter(jnp.dot(inner, down_weight, preferred_element_type=jnp.f...  37 us
    all_gather x1, waiting for transfers between devices, block_body(): gathered = lax.all_gather(normed_mlp, 'mlp', axis=0, tiled=True)  25 us
    all_gather x2, local copies, waits for them, and re-layouts, half_gather(): lax.all_gather(jnp.concatenate([mine, bias_rows], axis=0), 'req', axis=1,...  10.6 us
    all_to_all x1, starting transfers between devices, block_body(): lax.all_to_all(local_mod, 'req', split_axis=0, concat_axis=2, tiled=True)[0]  9.51 us
    sub x1, matrix products, attention(): expo = jnp.where(same, jnp.exp(masked - row_max), 0.0)  8.43 us
    all_to_all x1, waiting for transfers between devices, block_body(): lax.all_to_all(local_mod, 'req', split_axis=0, concat_axis=2, tiled=True)[0]  7.89 us
    dot_general x1, matrix products, block_body(): jnp.dot(inner, down_weight, preferred_element_type=jnp.float32)  7.88 us
  transfers between devices with their start and end apart: 10, of which 7 were waited for; matrix products, arithmetic and copies ran while one was open for 16% of the time, Pallas kernels for 0%

profile of v5, /device:TPU:8, one launch (start us, length us, event | category | flops | bytes accessed | tf_op | source)
XLA Modules:
  0.0 293.3 jit_solution(10310250866719478599)
XLA Ops:
  9.5 79.9 %all-gather.4.cloned.1.call-done = bf16[592,3456]{0,1:T(8,128)(2,1)} async-done(((bf16[592,216]{0,1:T(8,128)(2,1)}), bf16[592,3456]{0,1:T(8,128)(2,1)}) %all-gather.4.cloned.1.call-update) | async-done | bytes 4091920 | tf_op jit(solution)/shard_map/all_gather | solution.py:122
  89.3 7.0 %copy.75 = bf16[592,3456]{1,0:T(8,128)(2,1)} copy(bf16[592,3456]{0,1:T(8,128)(2,1)} %all-gather.4.cloned.1.call-done) | data formatting | bytes 8183808 | tf_op jit(solution)/shard_map/all_gather | solution.py:122
  97.0 1.8 convolution_add_fusion.3
  98.9 3.0 %fusion.37 = bf16[64,576]{1,0:T(8,128)(2,1)S(1)} fusion(bf16[1152,576]{0,1:T(8,128)(2,1)} %param.42, f32[64,1152]{1,0:T(8,128)S(1)} %convolution_add_fusion.3, bf16[1001,1152]{1,0:T(8,128)(2,1)} %param.37, s32[64]{0:T(128)S(1)} %select_n.64, f32[576]{0:T(1024)S(1)} %convert_element_type.98), kind=kOutput, calls=%fused_computation.43 | convolution fusion | flops 233118272 | bytes 4004608 | tf_op jit(solution)/shard_map/dot_general | solution.py:99
  102.6 9.5 %all-to-all-start = ((bf16[16,4,576]{2,1,0:T(4,128)(2,1)}), bf16[16,4,576]{2,1,0:T(4,128)(2,1)S(1)}, u32[]{:S(2)}, u32[]{:S(2)}) async-start(bf16[16,4,576]{2,1,0:T(4,128)(2,1)} %reshape.202), calls=%async_computation | async-start | bytes 163840 | tf_op jit(solution)/shard_map/all_to_all | solution.py:103
  112.9 7.9 %all-to-all-done = bf16[16,4,576]{2,1,0:T(4,128)(2,1)S(1)} async-done(((bf16[16,4,576]{2,1,0:T(4,128)(2,1)}), bf16[16,4,576]{2,1,0:T(4,128)(2,1)S(1)}, u32[]{:S(2)}, u32[]{:S(2)}) %all-to-all-start) | async-done | bytes 73760 | tf_op jit(solution)/shard_map/all_to_all | solution.py:103
  122.7 2.1 copy-done.1
  125.1 1.8 convert_reduce_fusion
  126.9 3.7 %fusion.4 = f32[128,3456]{1,0:T(8,128)S(1)} fusion(bf16[592,3456]{0,1:T(8,128)(2,1)} %all-gather.4.cloned.1.call-done, bf16[128,1152]{1,0:T(8,128)(2,1)S(1)} %fusion.46, s32[]{:T(128)S(6)} %select_n.66), kind=kOutput, calls=%fused_computation.7 | convolution fusion | flops 509607936 | bytes 6025220 | tf_op jit(solution)/shard_map/dot_general | solution.py:137
  130.7 4.1 %fusion.3 = bf16[128,3456]{1,0:T(8,128)(2,1)} fusion(f32[128,3456]{1,0:T(8,128)S(1)} %fusion.4, bf16[592,3456]{1,0:T(8,128)(2,1)} %collective-permute-done, f32[3456]{0:T(1024)S(1)} %convert_reduce_fusion, bf16[128,1152]{1,0:T(8,128)(2,1)S(1)} %fusion.46, s32[]{:T(128)S(6)} %select_n.67), kind=kOutput, calls=%fused_computation.6 | convolution fusion | flops 510935040 | bytes 6815748 | tf_op jit(solution)/shard_map/dot_general | solution.py:138
  134.7 2.2 copy.76
  137.0 2.1 copy.77
  139.1 4.2 %all-to-all-start.1 = ((bf16[128,8,432]{0,2,1:T(8,128)(2,1)}), bf16[128,8,432]{0,2,1:T(8,128)(2,1)}, u32[]{:S(2)}, u32[]{:S(2)}) async-start(bf16[128,8,432]{0,2,1:T(8,128)(2,1)} %bitcast.72), calls=%async_computation.1 | async-start | bytes 1769472 | tf_op jit(solution)/shard_map/all_to_all | solution.py:148
  143.3 1.7 broadcast_compare_fusion
  145.0 27.1 %all-gather.6.cloned.1.call-done = bf16[592,1152]{0,1:T(8,128)(2,1)} async-done(((bf16[592,72]{0,1:T(8,128)(2,1)}), bf16[592,1152]{0,1:T(8,128)(2,1)}) %all-gather.6.cloned.1.call-update) | async-done | bytes 1363984 | tf_op jit(solution)/shard_map/all_gather | solution.py:122
  172.1 3.6 %copy.82 = bf16[592,1152]{1,0:T(8,128)(2,1)} copy(bf16[592,1152]{0,1:T(8,128)(2,1)} %all-gather.6.cloned.1.call-done) | data formatting | bytes 2727936 | tf_op jit(solution)/shard_map/all_gather | solution.py:122
  175.7 1.3 copy_bitcast_fusion
  177.7 8.4 %fusion.94 = (f32[2,1024]{1,0:T(2,128)S(1)}, bf16[2,1024,1024]{1,2,0:T(8,128)(2,1)}) fusion(pred[1024,1024]{0,1:T(8,128)(4,1)} %broadcast_compare_fusion, bf16[1024,2,72]{0,2,1:T(8,128)(2,1)} %bitcast.80, bf16[1024,2,72]{0,2,1:T(8,128)(2,1)S(1)} %bitcast.79), kind=kOutput, calls=%fused_computation.130 | convolution fusion | flops 314573824 | bytes 5840896 | tf_op jit(solution)/shard_map/sub | solution.py:40
  186.2 3.0 %fusion.34 = bf16[1024,2,72]{0,2,1:T(8,128)(2,1)S(1)} fusion(bf16[1024,2,72]{0,2,1:T(8,128)(2,1)S(1)} %bitcast.78, bf16[2,1024,1024]{1,2,0:T(8,128)(2,1)} %get-tuple-element.44, f32[1024,2]{0,1:T(2,128)S(1)} %bitcast.88), kind=kOutput, calls=%fused_computation.41 | convolution fusion | flops 302284800 | bytes 4792320 | tf_op jit(solution)/shard_map/hqk,khd->qhd/dot_general | solution.py:43
  190.0 4.2 %all-to-all-start.2 = ((bf16[8,128,144]{1,2,0:T(8,128)(2,1)}), bf16[8,128,144]{1,2,0:T(8,128)(2,1)S(1)}, u32[]{:S(2)}, u32[]{:S(2)}) async-start(bf16[8,128,144]{1,2,0:T(8,128)(2,1)} %copy.80), calls=%async_computation.2 | async-start | bytes 589824 | tf_op jit(solution)/shard_map/all_to_all | solution.py:156
  194.3 1.2 convert_reduce_fusion.2
  195.5 6.6 %all-to-all-done.2 = bf16[8,128,144]{1,2,0:T(8,128)(2,1)S(1)} async-done(((bf16[8,128,144]{1,2,0:T(8,128)(2,1)}), bf16[8,128,144]{1,2,0:T(8,128)(2,1)S(1)}, u32[]{:S(2)}, u32[]{:S(2)}) %all-to-all-start.2) | async-done | bytes 294944 | tf_op jit(solution)/shard_map/all_to_all | solution.py:156
  202.1 2.1 fusion.25
  204.2 2.1 fusion.95
  206.5 2.2 fusion.49
  208.8 25.0 %all-gather.8.cloned.1.call-done = bf16[1024,1152]{1,0:T(8,128)(2,1)} async-done(((bf16[128,1152]{1,0:T(8,128)(2,1)}), bf16[1024,1152]{1,0:T(8,128)(2,1)}) %all-gather.8.cloned.1.call-update) | async-done | bytes 2359312 | tf_op jit(solution)/shard_map/all_gather | solution.py:160
  233.8 7.9 %convolution_convert_fusion = bf16[1024,1152]{1,0:T(8,128)(2,1)} fusion(bf16[576,1152]{1,0:T(8,128)(2,1)} %param.50, bf16[1024,1152]{1,0:T(8,128)(2,1)} %all-gather.8.cloned.1.call-done, bf16[1152,576]{0,1:T(8,128)(2,1)} %param.48, f32[576]{0:T(1024)S(1)} %convert_element_type.107), kind=kOutput, calls=%fused_computation.15 | convolution fusion | flops 2724986880 | bytes 7375104 | tf_op jit(solution)/shard_map/dot_general | solution.py:167
  242.4 37.0 %reduce-scatter.2.cloned.1.call-done = bf16[128,1152]{1,0:T(8,128)(2,1)} async-done(((bf16[1024,1152]{1,0:T(8,128)(2,1)}), bf16[128,1152]{1,0:T(8,128)(2,1)}) %reduce-scatter.2.cloned.1.call-update) | async-done | bytes 294928 | tf_op jit(solution)/shard_map/reduce_scatter | solution.py:166
  279.3 1.3 fusion.91
  280.9 1.5 convolution_add_fusion.6
  282.5 1.6 collective-permute-start.2
  284.2 1.9 collective-permute-done.2
  (96 shorter events, 10.6 us)
Async XLA Ops:
  6.5 90.5 %copy-start = (bf16[1152,1152]{1,0:T(8,128)(2,1)S(1)}, bf16[1152,1152]{1,0:T(8,128)(2,1)}, u32[]{:S(2)}) copy-start(bf16[1152,1152]{1,0:T(8,128)(2,1)} %param.40) | copy-start | bytes 7962628
  6.5 82.8 %all-gather.4.cloned.1.call-start = ((), (), s32[]{:S(2)}) async-start(), calls=%async_computation.4 | async-start | bytes 4700160 | tf_op jit(solution)/shard_map/all_gather | solution.py:122
  9.4 87.0 %copy-start.12 = (s32[16,4]{0,1:T(4,128)S(1)}, s32[16,4]{0,1:T(4,128)}, u32[]{:S(2)}) copy-start(s32[16,4]{0,1:T(4,128)} %param.31) | copy-start | bytes 772
  9.4 87.1 %copy-start.13 = (s32[16,4]{0,1:T(4,128)S(1)}, s32[16,4]{0,1:T(4,128)}, u32[]{:S(2)}) copy-start(s32[16,4]{0,1:T(4,128)} %param.32) | copy-start | bytes 772
  9.4 87.3 %copy-start.6 = (bf16[1152]{0:T(1024)(128)(2,1)S(1)}, bf16[1152]{0:T(1024)(128)(2,1)}, u32[]{:S(2)}) copy-start(bf16[1152]{0:T(1024)(128)(2,1)} %param.39) | copy-start | bytes 6916
  9.4 87.3 %copy-start.7 = (bf16[1152]{0:T(1024)(128)(2,1)S(1)}, bf16[1152]{0:T(1024)(128)(2,1)}, u32[]{:S(2)}) copy-start(bf16[1152]{0:T(1024)(128)(2,1)} %param.41) | copy-start | bytes 6916
  9.4 87.3 %copy-start.10 = (bf16[576]{0:T(1024)(128)(2,1)S(1)}, bf16[576]{0:T(1024)(128)(2,1)}, u32[]{:S(2)}) copy-start(bf16[576]{0:T(1024)(128)(2,1)} %param.43) | copy-start | bytes 3460
  96.4 34.3 %collective-permute-start = (bf16[592,3456]{1,0:T(8,128)(2,1)}, bf16[592,3456]{1,0:T(8,128)(2,1)}, u32[]{:S(2)}, u32[]{:S(2)}) collective-permute-start(bf16[592,3456]{1,0:T(8,128)(2,1)} %copy.75), channel_id=1, source_target_pairs={{0,1},{1,0},{2,3},{3,2},{4,5},{5,4},{6,7},{7,6},{8,9},{9,8},{10,11... | collective-permute-start | bytes 12275720 | tf_op jit(solution)/shard_map/ppermute | solution.py:130
  98.8 13.3 %copy-start.18 = (s32[1,4]{1,0:T(1,128)S(1)}, s32[1,4]{1,0:T(1,128)}, u32[]{:S(2)}) copy-start(s32[1,4]{1,0:T(1,128)} %param.33) | copy-start | bytes 52
  98.8 13.6 %copy-start.2 = (bf16[1,128,1152]{2,1,0:T(8,128)(2,1)S(1)}, bf16[1,128,1152]{2,1,0:T(8,128)(2,1)}, u32[]{:S(2)}) copy-start(bf16[1,128,1152]{2,1,0:T(8,128)(2,1)} %param.29) | copy-start | bytes 884740
  98.9 22.0 %copy-start.14 = (bf16[72]{0:T(256)(128)(2,1)S(1)}, bf16[72]{0:T(256)(128)(2,1)}, u32[]{:S(2)}) copy-start(bf16[72]{0:T(256)(128)(2,1)} %param.47) | copy-start | bytes 436
  98.9 22.2 %copy-start.4 = (bf16[1152,72]{0,1:T(8,128)(2,1)S(1)}, bf16[1152,72]{0,1:T(8,128)(2,1)}, u32[]{:S(2)}) copy-start(bf16[1152,72]{0,1:T(8,128)(2,1)} %param.46) | copy-start | bytes 497668
  102.6 18.2 %all-to-all-start = ((bf16[16,4,576]{2,1,0:T(4,128)(2,1)}), bf16[16,4,576]{2,1,0:T(4,128)(2,1)S(1)}, u32[]{:S(2)}, u32[]{:S(2)}) async-start(bf16[16,4,576]{2,1,0:T(4,128)(2,1)} %reshape.202), calls=%async_computation | async-start | bytes 163840 | tf_op jit(solution)/shard_map/all_to_all | solution.py:103
  112.1 60.0 %all-gather.6.cloned.1.call-start = ((), (), s32[]{:S(2)}) async-start(), calls=%async_computation.5 | async-start | bytes 1566720 | tf_op jit(solution)/shard_map/all_gather | solution.py:122
  122.7 2.1 copy-start.1
  139.1 36.5 %all-to-all-start.1 = ((bf16[128,8,432]{0,2,1:T(8,128)(2,1)}), bf16[128,8,432]{0,2,1:T(8,128)(2,1)}, u32[]{:S(2)}, u32[]{:S(2)}) async-start(bf16[128,8,432]{0,2,1:T(8,128)(2,1)} %bitcast.72), calls=%async_computation.1 | async-start | bytes 1769472 | tf_op jit(solution)/shard_map/all_to_all | solution.py:148
  175.6 28.5 %collective-permute-start.1 = (bf16[592,1152]{1,0:T(8,128)(2,1)}, bf16[592,1152]{1,0:T(8,128)(2,1)}, u32[]{:S(2)}, u32[]{:S(2)}) collective-permute-start(bf16[592,1152]{1,0:T(8,128)(2,1)} %copy.82), channel_id=1, source_target_pairs={{0,1},{1,0},{2,3},{3,2},{4,5},{5,4},{6,7},{7,6},{8,9},{9,8},{10,11... | collective-permute-start | bytes 4091912 | tf_op jit(solution)/shard_map/ppermute | solution.py:131
  190.0 12.1 %all-to-all-start.2 = ((bf16[8,128,144]{1,2,0:T(8,128)(2,1)}), bf16[8,128,144]{1,2,0:T(8,128)(2,1)S(1)}, u32[]{:S(2)}, u32[]{:S(2)}) async-start(bf16[8,128,144]{1,2,0:T(8,128)(2,1)} %copy.80), calls=%async_computation.2 | async-start | bytes 589824 | tf_op jit(solution)/shard_map/all_to_all | solution.py:156
  194.2 39.5 %all-gather.8.cloned.1.call-start = ((), (), s32[]{:S(2)}) async-start(), calls=%async_computation.6 | async-start | bytes 2654208 | tf_op jit(solution)/shard_map/all_gather | solution.py:160
  202.1 2.1 copy-start.3
  206.3 2.5 copy-start.11
  208.7 70.6 %reduce-scatter.2.cloned.1.call-start = ((), (), s32[]{:S(2)}) async-start(), calls=%async_computation.7 | async-start | bytes 2654208 | tf_op jit(solution)/shard_map/reduce_scatter | solution.py:166
  241.7 0.7 copy-start.8
  241.7 0.7 copy-start.19
  241.7 39.2 %copy-start.5 = (bf16[1152,16]{0,1:T(8,128)(2,1)S(1)}, bf16[1152,16]{0,1:T(8,128)(2,1)}, u32[]{:S(2)}) copy-start(bf16[1152,16]{0,1:T(8,128)(2,1)} %param.52) | copy-start | bytes 110596
  241.7 42.4 %copy-start.15 = (f32[1,4]{1,0:T(1,128)S(1)}, f32[1,4]{1,0:T(1,128)}, u32[]{:S(2)}) copy-start(f32[1,4]{1,0:T(1,128)} %param.35) | copy-start | bytes 52
  241.7 42.4 %copy-start.16 = (f32[1,4]{1,0:T(1,128)S(1)}, f32[1,4]{1,0:T(1,128)}, u32[]{:S(2)}) copy-start(f32[1,4]{1,0:T(1,128)} %param.34) | copy-start | bytes 52
  241.7 42.4 %copy-start.17 = (f32[1,4]{1,0:T(1,128)S(1)}, f32[1,4]{1,0:T(1,128)}, u32[]{:S(2)}) copy-start(f32[1,4]{1,0:T(1,128)} %param.36) | copy-start | bytes 52
  241.7 44.4 %copy-start.9 = (f32[128,8]{0,1:T(8,128)S(1)}, f32[128,8]{0,1:T(8,128)}, u32[]{:S(2)}) copy-start(f32[128,8]{0,1:T(8,128)} %param.30) | copy-start | bytes 12292
  282.5 3.7 %collective-permute-start.2 = (f32[128,8]{0,1:T(8,128)S(1)}, f32[128,8]{0,1:T(8,128)S(1)}, u32[]{:S(2)}, u32[]{:S(2)}) collective-permute-start(f32[128,8]{0,1:T(8,128)S(1)} %constant_dynamic-slice_fusion), channel_id=1, source_target_pairs={{0,128},{128,0},{1,129},{129,1},{2,130},{130,2},{3,131},{131,3},{4... | collective-permute-start | bytes 12296 | tf_op jit(solution)/shard_map/ppermute | solution.py:183
Sparse Core Ops, SparseCore 0:
  9.8 79.4 all-gather.3
  122.0 50.0 all-gather.5
  208.8 24.8 all-gather.7
  241.8 37.4 reduce-scatter.1

commit v6 on v5

--- a/solution.py
+++ b/solution.py
@@ -157,18 +157,38 @@
     projected = split_dot(attended, out_mine, out_other)
     mid_hidden = (rows.astype(jnp.float32) + gate_attn * projected).astype(jnp.bfloat16)
     normed_mlp = (layer_norm(mid_hidden) * (1.0 + scale_mlp) + shift_mlp).astype(jnp.bfloat16)
-    gathered = lax.all_gather(normed_mlp, "mlp", axis=0, tiled=True)
+    split = width // 2
+    gathered_sc = lax.all_gather(normed_mlp[:, :split], "mlp", axis=0, tiled=True)
+    gathered_aa = lax.all_to_all(
+        jnp.broadcast_to(normed_mlp[None, :, split:], (mlp_count, tok_rows, width - split)),
+        "mlp",
+        split_axis=0,
+        concat_axis=0,
+        tiled=True,
+    ).reshape(group_rows, width - split)
     inner = jax.nn.gelu(
-        jnp.dot(gathered, up_weight, preferred_element_type=jnp.float32)
+        jnp.dot(gathered_sc, up_weight[:split], preferred_element_type=jnp.float32)
+        + jnp.dot(gathered_aa, up_weight[split:], preferred_element_type=jnp.float32)
         + up_bias.astype(jnp.float32),
         approximate=True,
     ).astype(jnp.bfloat16)
-    mlp_out = lax.psum_scatter(
-        jnp.dot(inner, down_weight, preferred_element_type=jnp.float32).astype(jnp.bfloat16),
-        "mlp",
-        scatter_dimension=0,
-        tiled=True,
+    partial_out = jnp.dot(inner, down_weight, preferred_element_type=jnp.float32).astype(
+        jnp.bfloat16
+    )
+    reduced_sc = lax.psum_scatter(
+        partial_out[:, :split], "mlp", scatter_dimension=0, tiled=True
     ).astype(jnp.float32)
+    reduced_aa = jnp.sum(
+        lax.all_to_all(
+            partial_out[:, split:].reshape(mlp_count, tok_rows, width - split),
+            "mlp",
+            split_axis=0,
+            concat_axis=0,
+            tiled=True,
+        ).astype(jnp.float32),
+        axis=0,
+    )
+    mlp_out = jnp.concatenate([reduced_sc, reduced_aa], axis=1)
     final_hidden = mid_hidden.astype(jnp.float32) + gate_mlp * (
         mlp_out + down_bias.astype(jnp.float32)
     )

time: 294 us -> 306 us (1.041)
  waiting for transfers between devices: 185 us -> 174 us
  local copies, waits for them, and re-layouts: 24.1 us -> 32.9 us
  starting transfers between devices: 19.7 us -> 28.4 us
  matrix products: 38.5 us -> 42.2 us
    reduce_scatter x1, waiting for transfers between devices: 37 us -> 10.2 us  [block_body(): lax.psum_scatter(partial_out[:, :split], 'mlp', scatter_dimension=0, tile...]
    all_to_all x0 -> x2, waiting for transfers between devices: none -> 20.5 us  [the longest x1 20.5 us: block_body(): lax.all_to_all(partial_out[:, split:].reshape(mlp_count, tok_rows, width...]
    all_to_all x0 -> x2, starting transfers between devices: none -> 8.5 us  [the longest x1 4.25 us: block_body(): lax.all_to_all(partial_out[:, split:].reshape(mlp_count, tok_rows, width...]
    all_gather x1, waiting for transfers between devices: 25 us -> 19.4 us  [block_body(): lax.all_gather(normed_mlp[:, :split], 'mlp', axis=0, tiled=True)]
    slice x0 -> x3, local copies, waits for them, and re-layouts: none -> 4.76 us  [the longest x1 3.91 us: block_body(): partial_out[:, :split]]
    dot_general x0 -> x1, matrix products: none -> 4.06 us  [block_body(): jnp.dot(gathered_sc, up_weight[:split], preferred_element_type=jnp.float32)]
  transfers between devices with their start and end apart: 10 -> 12, of which waited for: 7 -> 8; matrix products, arithmetic and copies ran while one was open for 16% -> 18% of each run, Pallas kernels for 0% -> 0%
where the time goes in v6:
time: 306 us; the launch traced here: 304 us
  waiting for transfers between devices  174 us (57%)
  matrix products  42.2 us (14%)
  local copies, waits for them, and re-layouts  32.9 us (11%)
  starting transfers between devices  28.4 us (9%)
  other arithmetic  13.7 us (4%)
  between operations  13.6 us (4%)
    all_gather x2, waiting for transfers between devices, half_gather(): lax.all_gather(jnp.concatenate([mine, bias_rows], axis=0), 'req', axis=1,...  107 us
    all_to_all x1, waiting for transfers between devices, block_body(): lax.all_to_all(partial_out[:, split:].reshape(mlp_count, tok_rows, width...  20.5 us
    all_gather x1, waiting for transfers between devices, block_body(): lax.all_gather(normed_mlp[:, :split], 'mlp', axis=0, tiled=True)  19.4 us
    all_gather x2, local copies, waits for them, and re-layouts, half_gather(): lax.all_gather(jnp.concatenate([mine, bias_rows], axis=0), 'req', axis=1,...  10.7 us
    reduce_scatter x1, waiting for transfers between devices, block_body(): lax.psum_scatter(partial_out[:, :split], 'mlp', scatter_dimension=0, tile...  10.2 us
    all_to_all x1, starting transfers between devices, block_body(): lax.all_to_all(local_mod, 'req', split_axis=0, concat_axis=2, tiled=True)[0]  9.51 us
    sub x1, matrix products, attention(): expo = jnp.where(same, jnp.exp(masked - row_max), 0.0)  8.43 us
    all_to_all x1, waiting for transfers between devices, block_body(): lax.all_to_all(local_mod, 'req', split_axis=0, concat_axis=2, tiled=True)[0]  7.89 us
  transfers between devices with their start and end apart: 12, of which 8 were waited for; matrix products, arithmetic and copies ran while one was open for 18% of the time, Pallas kernels for 0%

profile of v6, /device:TPU:8, one launch (start us, length us, event | category | flops | bytes accessed | tf_op | source)
XLA Modules:
  0.0 304.4 jit_solution(3028427828606349392)
XLA Ops:
  9.5 79.9 %all-gather.4.cloned.1.call-done = bf16[592,3456]{0,1:T(8,128)(2,1)} async-done(((bf16[592,216]{0,1:T(8,128)(2,1)}), bf16[592,3456]{0,1:T(8,128)(2,1)}) %all-gather.4.cloned.1.call-update) | async-done | bytes 4091920 | tf_op jit(solution)/shard_map/all_gather | solution.py:122
  89.3 7.1 %copy.94 = bf16[592,3456]{1,0:T(8,128)(2,1)} copy(bf16[592,3456]{0,1:T(8,128)(2,1)} %all-gather.4.cloned.1.call-done) | data formatting | bytes 8183808 | tf_op jit(solution)/shard_map/all_gather | solution.py:122
  97.1 1.8 convolution_add_fusion.3
  98.9 3.0 fusion.39
  102.6 9.5 %all-to-all-start = ((bf16[16,4,576]{2,1,0:T(4,128)(2,1)}), bf16[16,4,576]{2,1,0:T(4,128)(2,1)S(1)}, u32[]{:S(2)}, u32[]{:S(2)}) async-start(bf16[16,4,576]{2,1,0:T(4,128)(2,1)} %reshape.209), calls=%async_computation | async-start | bytes 163840 | tf_op jit(solution)/shard_map/all_to_all | solution.py:103
  112.9 7.9 %all-to-all-done = bf16[16,4,576]{2,1,0:T(4,128)(2,1)S(1)} async-done(((bf16[16,4,576]{2,1,0:T(4,128)(2,1)}), bf16[16,4,576]{2,1,0:T(4,128)(2,1)S(1)}, u32[]{:S(2)}, u32[]{:S(2)}) %all-to-all-start) | async-done | bytes 73760 | tf_op jit(solution)/shard_map/all_to_all | solution.py:103
  122.8 2.1 copy-done.1
  125.1 1.8 convert_reduce_fusion.1
  126.9 3.7 %fusion.4 = f32[128,3456]{1,0:T(8,128)S(1)} fusion(bf16[592,3456]{0,1:T(8,128)(2,1)} %all-gather.4.cloned.1.call-done, bf16[128,1152]{1,0:T(8,128)(2,1)S(1)} %fusion.54, s32[]{:T(128)S(6)} %select_n.66), kind=kOutput, calls=%fused_computation.7 | convolution fusion | flops 509607936 | bytes 6025220 | tf_op jit(solution)/shard_map/dot_general | solution.py:137
  130.7 4.1 %fusion.3 = bf16[128,3456]{1,0:T(8,128)(2,1)} fusion(f32[128,3456]{1,0:T(8,128)S(1)} %fusion.4, bf16[592,3456]{1,0:T(8,128)(2,1)} %collective-permute-done, f32[3456]{0:T(1024)S(1)} %convert_reduce_fusion.1, bf16[128,1152]{1,0:T(8,128)(2,1)S(1)} %fusion.54, s32[]{:T(128)S(6)} %select_n.67), kind=kOutput, calls=%fused_computation.6 | convolution fusion | flops 510935040 | bytes 6815748 | tf_op jit(solution)/shard_map/dot_general | solution.py:138
  134.8 2.2 copy.95
  137.0 2.2 copy.96
  139.2 4.2 %all-to-all-start.1 = ((bf16[128,8,432]{0,2,1:T(8,128)(2,1)}), bf16[128,8,432]{0,2,1:T(8,128)(2,1)}, u32[]{:S(2)}, u32[]{:S(2)}) async-start(bf16[128,8,432]{0,2,1:T(8,128)(2,1)} %bitcast.83), calls=%async_computation.1 | async-start | bytes 1769472 | tf_op jit(solution)/shard_map/all_to_all | solution.py:148
  143.4 1.6 broadcast_compare_fusion
  145.1 27.0 %all-gather.6.cloned.1.call-done = bf16[592,1152]{0,1:T(8,128)(2,1)} async-done(((bf16[592,72]{0,1:T(8,128)(2,1)}), bf16[592,1152]{0,1:T(8,128)(2,1)}) %all-gather.6.cloned.1.call-update) | async-done | bytes 1363984 | tf_op jit(solution)/shard_map/all_gather | solution.py:122
  172.1 3.6 %copy.101 = bf16[592,1152]{1,0:T(8,128)(2,1)} copy(bf16[592,1152]{0,1:T(8,128)(2,1)} %all-gather.6.cloned.1.call-done) | data formatting | bytes 2727936 | tf_op jit(solution)/shard_map/all_gather | solution.py:122
  177.8 8.4 %fusion.104 = (f32[2,1024]{1,0:T(2,128)S(1)}, bf16[2,1024,1024]{1,2,0:T(8,128)(2,1)}) fusion(pred[1024,1024]{0,1:T(8,128)(4,1)} %broadcast_compare_fusion, bf16[1024,2,72]{0,2,1:T(8,128)(2,1)} %bitcast.91, bf16[1024,2,72]{0,2,1:T(8,128)(2,1)S(1)} %bitcast.90), kind=kOutput, calls=%fused_computation.139 | convolution fusion | flops 314573824 | bytes 5840896 | tf_op jit(solution)/shard_map/sub | solution.py:40
  186.3 3.0 %fusion.34 = bf16[1024,2,72]{0,2,1:T(8,128)(2,1)S(1)} fusion(bf16[1024,2,72]{0,2,1:T(8,128)(2,1)S(1)} %bitcast.89, bf16[2,1024,1024]{1,2,0:T(8,128)(2,1)} %get-tuple-element.48, f32[1024,2]{0,1:T(2,128)S(1)} %bitcast.99), kind=kOutput, calls=%fused_computation.42 | convolution fusion | flops 302284800 | bytes 4792320 | tf_op jit(solution)/shard_map/hqk,khd->qhd/dot_general | solution.py:43
  190.1 4.2 %all-to-all-start.2 = ((bf16[8,128,144]{1,2,0:T(8,128)(2,1)}), bf16[8,128,144]{1,2,0:T(8,128)(2,1)S(1)}, u32[]{:S(2)}, u32[]{:S(2)}) async-start(bf16[8,128,144]{1,2,0:T(8,128)(2,1)} %copy.99), calls=%async_computation.2 | async-start | bytes 589824 | tf_op jit(solution)/shard_map/all_to_all | solution.py:156
  195.6 6.6 %all-to-all-done.2 = bf16[8,128,144]{1,2,0:T(8,128)(2,1)S(1)} async-done(((bf16[8,128,144]{1,2,0:T(8,128)(2,1)}), bf16[8,128,144]{1,2,0:T(8,128)(2,1)S(1)}, u32[]{:S(2)}, u32[]{:S(2)}) %all-to-all-start.2) | async-done | bytes 294944 | tf_op jit(solution)/shard_map/all_to_all | solution.py:156
  202.2 2.1 fusion.25
  204.3 2.1 fusion.105
  210.2 4.3 %all-to-all-start.3 = ((bf16[8,128,576]{1,2,0:T(8,128)(2,1)}), bf16[8,128,576]{1,2,0:T(8,128)(2,1)}, u32[]{:S(2)}, u32[]{:S(2)}) async-start(bf16[8,128,576]{1,2,0:T(8,128)(2,1)} %broadcast_in_dim.24), calls=%async_computation.3 | async-start | bytes 2359296 | tf_op jit(solution)/shard_map/all_to_all | solution.py:162
  214.7 19.4 %all-gather.8.cloned.1.call-done = bf16[1024,576]{1,0:T(8,128)(2,1)} async-done(((bf16[128,576]{1,0:T(8,128)(2,1)}), bf16[1024,576]{1,0:T(8,128)(2,1)}) %all-gather.8.cloned.1.call-update) | async-done | bytes 1179664 | tf_op jit(solution)/shard_map/all_gather | solution.py:161
  234.2 4.1 %fusion.46 = f32[1024,576]{0,1:T(8,128)} fusion(bf16[1024,576]{1,0:T(8,128)(2,1)} %all-gather.8.cloned.1.call-done, bf16[1152,576]{0,1:T(8,128)(2,1)} %param.48), kind=kOutput, calls=%fused_computation.51 | convolution fusion | flops 679477248 | bytes 4407296 | tf_op jit(solution)/shard_map/dot_general | solution.py:170
  238.2 7.5 %convolution_convert_fusion = bf16[1024,1152]{1,0:T(8,128)(2,1)} fusion(bf16[576,1152]{1,0:T(8,128)(2,1)} %param.50, f32[1024,576]{0,1:T(8,128)} %fusion.46, f32[576]{0:T(1024)S(1)} %convert_element_type.110, bf16[1152,576]{0,1:T(8,128)(2,1)} %param.48, bf16[8,128,576]{1,2,0:T(8,128)(2,1)} %all-to-all-done.3), kind=kOutput, calls=%fused_computation.15 | convolution fusion | flops 2046099456 | bytes 7964928 | tf_op jit(solution)/shard_map/dot_general | solution.py:175
  245.7 3.9 %fusion.101 = (bf16[1024,576]{1,0:T(8,128)(2,1)}, bf16[1024,576]{1,0:T(8,128)(2,1)}) fusion(bf16[1024,1152]{1,0:T(8,128)(2,1)} %convolution_convert_fusion), kind=kLoop, calls=%fused_computation.136 | loop fusion | bytes 4718592 | tf_op jit(solution)/shard_map/slice | solution.py:179
  249.7 2.4 copy.104
  252.1 4.3 %all-to-all-start.4 = ((bf16[8,128,576]{1,2,0:T(8,128)(2,1)}), bf16[8,128,576]{1,2,0:T(8,128)(2,1)}, u32[]{:S(2)}, u32[]{:S(2)}) async-start(bf16[8,128,576]{1,2,0:T(8,128)(2,1)} %copy.104), calls=%async_computation.5 | async-start | bytes 2359296 | tf_op jit(solution)/shard_map/all_to_all | solution.py:182
  256.4 20.5 %all-to-all-done.4 = bf16[8,128,576]{1,2,0:T(8,128)(2,1)} async-done(((bf16[8,128,576]{1,2,0:T(8,128)(2,1)}), bf16[8,128,576]{1,2,0:T(8,128)(2,1)}, u32[]{:S(2)}, u32[]{:S(2)}) %all-to-all-start.4) | async-done | bytes 1179680 | tf_op jit(solution)/shard_map/all_to_all | solution.py:182
  279.3 10.2 %reduce-scatter.2.cloned.1.call-done = bf16[128,576]{1,0:T(8,128)(2,1)} async-done(((bf16[1024,576]{1,0:T(8,128)(2,1)}), bf16[128,576]{1,0:T(8,128)(2,1)}) %reduce-scatter.2.cloned.1.call-update) | async-done | bytes 147472 | tf_op jit(solution)/shard_map/reduce_scatter | solution.py:178
  295.3 2.0 collective-permute-done.2
  (113 shorter events, 24.1 us)
Async XLA Ops:
  6.5 90.5 %copy-start = (bf16[1152,1152]{1,0:T(8,128)(2,1)S(1)}, bf16[1152,1152]{1,0:T(8,128)(2,1)}, u32[]{:S(2)}) copy-start(bf16[1152,1152]{1,0:T(8,128)(2,1)} %param.40) | copy-start | bytes 7962628
  6.5 82.8 %all-gather.4.cloned.1.call-start = ((), (), s32[]{:S(2)}) async-start(), calls=%async_computation.6 | async-start | bytes 4700160 | tf_op jit(solution)/shard_map/all_gather | solution.py:122
  9.4 87.0 %copy-start.14 = (s32[16,4]{0,1:T(4,128)S(1)}, s32[16,4]{0,1:T(4,128)}, u32[]{:S(2)}) copy-start(s32[16,4]{0,1:T(4,128)} %param.31) | copy-start | bytes 772
  9.4 87.2 %copy-start.15 = (s32[16,4]{0,1:T(4,128)S(1)}, s32[16,4]{0,1:T(4,128)}, u32[]{:S(2)}) copy-start(s32[16,4]{0,1:T(4,128)} %param.32) | copy-start | bytes 772
  9.4 87.3 %copy-start.6 = (bf16[1152]{0:T(1024)(128)(2,1)S(1)}, bf16[1152]{0:T(1024)(128)(2,1)}, u32[]{:S(2)}) copy-start(bf16[1152]{0:T(1024)(128)(2,1)} %param.39) | copy-start | bytes 6916
  9.4 87.4 %copy-start.7 = (bf16[1152]{0:T(1024)(128)(2,1)S(1)}, bf16[1152]{0:T(1024)(128)(2,1)}, u32[]{:S(2)}) copy-start(bf16[1152]{0:T(1024)(128)(2,1)} %param.41) | copy-start | bytes 6916
  9.4 87.4 %copy-start.12 = (bf16[576]{0:T(1024)(128)(2,1)S(1)}, bf16[576]{0:T(1024)(128)(2,1)}, u32[]{:S(2)}) copy-start(bf16[576]{0:T(1024)(128)(2,1)} %param.43) | copy-start | bytes 3460
  96.4 34.3 %collective-permute-start = (bf16[592,3456]{1,0:T(8,128)(2,1)}, bf16[592,3456]{1,0:T(8,128)(2,1)}, u32[]{:S(2)}, u32[]{:S(2)}) collective-permute-start(bf16[592,3456]{1,0:T(8,128)(2,1)} %copy.94), channel_id=1, source_target_pairs={{0,1},{1,0},{2,3},{3,2},{4,5},{5,4},{6,7},{7,6},{8,9},{9,8},{10,11... | collective-permute-start | bytes 12275720 | tf_op jit(solution)/shard_map/ppermute | solution.py:130
  98.9 13.3 %copy-start.20 = (s32[1,4]{1,0:T(1,128)S(1)}, s32[1,4]{1,0:T(1,128)}, u32[]{:S(2)}) copy-start(s32[1,4]{1,0:T(1,128)} %param.33) | copy-start | bytes 52
  98.9 13.6 %copy-start.2 = (bf16[1,128,1152]{2,1,0:T(8,128)(2,1)S(1)}, bf16[1,128,1152]{2,1,0:T(8,128)(2,1)}, u32[]{:S(2)}) copy-start(bf16[1,128,1152]{2,1,0:T(8,128)(2,1)} %param.29) | copy-start | bytes 884740
  98.9 22.0 %copy-start.16 = (bf16[72]{0:T(256)(128)(2,1)S(1)}, bf16[72]{0:T(256)(128)(2,1)}, u32[]{:S(2)}) copy-start(bf16[72]{0:T(256)(128)(2,1)} %param.47) | copy-start | bytes 436
  98.9 22.2 %copy-start.4 = (bf16[1152,72]{0,1:T(8,128)(2,1)S(1)}, bf16[1152,72]{0,1:T(8,128)(2,1)}, u32[]{:S(2)}) copy-start(bf16[1152,72]{0,1:T(8,128)(2,1)} %param.46) | copy-start | bytes 497668
  102.6 18.2 %all-to-all-start = ((bf16[16,4,576]{2,1,0:T(4,128)(2,1)}), bf16[16,4,576]{2,1,0:T(4,128)(2,1)S(1)}, u32[]{:S(2)}, u32[]{:S(2)}) async-start(bf16[16,4,576]{2,1,0:T(4,128)(2,1)} %reshape.209), calls=%async_computation | async-start | bytes 163840 | tf_op jit(solution)/shard_map/all_to_all | solution.py:103
  112.1 60.0 %all-gather.6.cloned.1.call-start = ((), (), s32[]{:S(2)}) async-start(), calls=%async_computation.7 | async-start | bytes 1566720 | tf_op jit(solution)/shard_map/all_gather | solution.py:122
  112.5 10.2 %copy-start.10 = (s32[128]{0:T(128)}, s32[128]{0:T(128)S(1)}, u32[]{:S(2)}) copy-start(s32[128]{0:T(128)S(1)} %dynamic_slice.27) | copy-start | bytes 1540
  139.2 36.6 %all-to-all-start.1 = ((bf16[128,8,432]{0,2,1:T(8,128)(2,1)}), bf16[128,8,432]{0,2,1:T(8,128)(2,1)}, u32[]{:S(2)}, u32[]{:S(2)}) async-start(bf16[128,8,432]{0,2,1:T(8,128)(2,1)} %bitcast.83), calls=%async_computation.1 | async-start | bytes 1769472 | tf_op jit(solution)/shard_map/all_to_all | solution.py:148
  175.7 28.6 %collective-permute-start.1 = (bf16[592,1152]{1,0:T(8,128)(2,1)}, bf16[592,1152]{1,0:T(8,128)(2,1)}, u32[]{:S(2)}, u32[]{:S(2)}) collective-permute-start(bf16[592,1152]{1,0:T(8,128)(2,1)} %copy.101), channel_id=1, source_target_pairs={{0,1},{1,0},{2,3},{3,2},{4,5},{5,4},{6,7},{7,6},{8,9},{9,8},{10,11... | collective-permute-start | bytes 4091912 | tf_op jit(solution)/shard_map/ppermute | solution.py:131
  190.1 12.1 %all-to-all-start.2 = ((bf16[8,128,144]{1,2,0:T(8,128)(2,1)}), bf16[8,128,144]{1,2,0:T(8,128)(2,1)S(1)}, u32[]{:S(2)}, u32[]{:S(2)}) async-start(bf16[8,128,144]{1,2,0:T(8,128)(2,1)} %copy.99), calls=%async_computation.2 | async-start | bytes 589824 | tf_op jit(solution)/shard_map/all_to_all | solution.py:156
  194.4 39.8 %all-gather.8.cloned.1.call-start = ((), (), s32[]{:S(2)}) async-start(), calls=%async_computation.8 | async-start | bytes 1474560 | tf_op jit(solution)/shard_map/all_gather | solution.py:161
  209.0 5.7 %copy-start.13 = (bf16[576]{0:T(1024)(128)(2,1)S(1)}, bf16[576]{0:T(1024)(128)(2,1)}, u32[]{:S(2)}) copy-start(bf16[576]{0:T(1024)(128)(2,1)} %param.49) | copy-start | bytes 3460
  210.2 28.1 %all-to-all-start.3 = ((bf16[8,128,576]{1,2,0:T(8,128)(2,1)}), bf16[8,128,576]{1,2,0:T(8,128)(2,1)}, u32[]{:S(2)}, u32[]{:S(2)}) async-start(bf16[8,128,576]{1,2,0:T(8,128)(2,1)} %broadcast_in_dim.24), calls=%async_computation.3 | async-start | bytes 2359296 | tf_op jit(solution)/shard_map/all_to_all | solution.py:162
  214.4 75.1 %reduce-scatter.2.cloned.1.call-start = ((), (), s32[]{:S(2)}) async-start(), calls=%async_computation.9 | async-start | bytes 1474560 | tf_op jit(solution)/shard_map/reduce_scatter | solution.py:178
  249.7 6.7 %copy-start.8 = (bf16[1152]{0:T(1024)(128)(2,1)S(1)}, bf16[1152]{0:T(1024)(128)(2,1)}, u32[]{:S(2)}) copy-start(bf16[1152]{0:T(1024)(128)(2,1)} %param.51) | copy-start | bytes 6916
  249.7 6.7 %copy-start.21 = (bf16[16]{0:T(256)(128)(2,1)S(1)}, bf16[16]{0:T(256)(128)(2,1)}, u32[]{:S(2)}) copy-start(bf16[16]{0:T(256)(128)(2,1)} %param.53) | copy-start | bytes 100
  252.1 24.8 %all-to-all-start.4 = ((bf16[8,128,576]{1,2,0:T(8,128)(2,1)}), bf16[8,128,576]{1,2,0:T(8,128)(2,1)}, u32[]{:S(2)}, u32[]{:S(2)}) async-start(bf16[8,128,576]{1,2,0:T(8,128)(2,1)} %copy.104), calls=%async_computation.5 | async-start | bytes 2359296 | tf_op jit(solution)/shard_map/all_to_all | solution.py:182
  279.3 12.8 %copy-start.5 = (bf16[1152,16]{0,1:T(8,128)(2,1)S(1)}, bf16[1152,16]{0,1:T(8,128)(2,1)}, u32[]{:S(2)}) copy-start(bf16[1152,16]{0,1:T(8,128)(2,1)} %param.52) | copy-start | bytes 110596
  279.3 15.9 %copy-start.11 = (s32[128]{0:T(128)S(1)}, s32[128]{0:T(128)}, u32[]{:S(2)}) copy-start(s32[128]{0:T(128)} %copy-done.10) | copy-start | bytes 1540
  279.3 15.9 %copy-start.17 = (f32[1,4]{1,0:T(1,128)S(1)}, f32[1,4]{1,0:T(1,128)}, u32[]{:S(2)}) copy-start(f32[1,4]{1,0:T(1,128)} %param.35) | copy-start | bytes 52
  279.3 15.9 %copy-start.18 = (f32[1,4]{1,0:T(1,128)S(1)}, f32[1,4]{1,0:T(1,128)}, u32[]{:S(2)}) copy-start(f32[1,4]{1,0:T(1,128)} %param.34) | copy-start | bytes 52
  279.3 15.9 %copy-start.19 = (f32[1,4]{1,0:T(1,128)S(1)}, f32[1,4]{1,0:T(1,128)}, u32[]{:S(2)}) copy-start(f32[1,4]{1,0:T(1,128)} %param.36) | copy-start | bytes 52
  279.3 18.0 %copy-start.9 = (f32[128,8]{0,1:T(8,128)S(1)}, f32[128,8]{0,1:T(8,128)}, u32[]{:S(2)}) copy-start(f32[128,8]{0,1:T(8,128)} %param.30) | copy-start | bytes 12292
  293.6 3.7 %collective-permute-start.2 = (f32[128,8]{0,1:T(8,128)S(1)}, f32[128,8]{0,1:T(8,128)S(1)}, u32[]{:S(2)}, u32[]{:S(2)}) collective-permute-start(f32[128,8]{0,1:T(8,128)S(1)} %constant_dynamic-slice_fusion), channel_id=1, source_target_pairs={{0,128},{128,0},{1,129},{129,1},{2,130},{130,2},{3,131},{131,3},{4... | collective-permute-start | bytes 12296 | tf_op jit(solution)/shard_map/ppermute | solution.py:203
  (2 other events, 4.2 us)
Sparse Core Ops, SparseCore 0:
  9.8 79.4 all-gather.3
  122.0 50.0 all-gather.5
  208.9 25.1 all-gather.7
  249.8 39.6 reduce-scatter.1

commit v7 on v5

--- a/solution.py
+++ b/solution.py
@@ -125,8 +125,27 @@
         return gathered
 
     qkv_mine = half_gather(qkv_weight, qkv_bias)
-    out_weight, out_bias, modulation = lax.optimization_barrier((out_weight, out_bias, modulation))
-    out_mine = half_gather(out_weight, out_bias)
+    out_ext = jnp.concatenate(
+        [
+            lax.dynamic_slice_in_dim(out_weight, core * half_rows, half_rows, axis=0),
+            jnp.zeros((16, out_weight.shape[1]), out_weight.dtype).at[0].set(out_bias),
+        ],
+        axis=0,
+    )
+    req_index = lax.axis_index("req")
+    pieces = [out_ext] + [
+        lax.ppermute(
+            out_ext, "req", [(index, (index + shift) % req_count) for index in range(req_count)]
+        )
+        for shift in range(1, req_count)
+    ]
+    reverse = jnp.stack(pieces[::-1])
+    ordered = lax.dynamic_slice_in_dim(
+        jnp.concatenate([reverse, reverse], axis=0), (req_count - 1 - req_index) % req_count, req_count
+    )
+    out_mine = jnp.transpose(ordered, (1, 0, 2)).reshape(
+        half_rows + 16, req_count * out_weight.shape[1]
+    )
     qkv_other = lax.ppermute(qkv_mine, "mlp", pair)
     out_other = lax.ppermute(out_mine, "mlp", pair)
 

time: 294 us -> 290 us (0.986)
  waiting for transfers between devices: 185 us -> 96.8 us
  starting transfers between devices: 19.7 us -> 65.7 us
  local copies, waits for them, and re-layouts: 24.1 us -> 60 us
    all_gather x2 -> x1, waiting for transfers between devices: 107 us -> 5.12 us  [half_gather(): lax.all_gather(jnp.concatenate([mine, bias_rows], axis=0), 'req', axis=1,...]
    ppermute x0 -> x15, starting transfers between devices: none -> 42 us  [block_body(): lax.ppermute(out_ext, 'req', [(index, (index + shift) % req_count) for in...]
    unnamed x42 -> x88, local copies, waits for them, and re-layouts: 2.99 us -> 31.9 us
    ppermute x0 -> x15, waiting for transfers between devices: none -> 10.9 us  [block_body(): lax.ppermute(out_ext, 'req', [(index, (index + shift) % req_count) for in...]
    all_to_all x1, waiting for transfers between devices: 7.89 us -> 0.01 us  [block_body(): lax.all_to_all(local_mod, 'req', split_axis=0, concat_axis=2, tiled=True)[0]]
    all_gather x1, waiting for transfers between devices: 25 us -> 31.6 us  [block_body(): gathered = lax.all_gather(normed_mlp, 'mlp', axis=0, tiled=True)]
    all_to_all x1, waiting for transfers between devices: 0.01 us -> 4.93 us  [block_body(): lax.all_to_all(packed, 'mlp', split_axis=1, concat_axis=0, tiled=True)]
    all_to_all x1, starting transfers between devices: 4.24 us -> 7.97 us  [block_body(): lax.all_to_all(packed, 'mlp', split_axis=1, concat_axis=0, tiled=True)]
  transfers between devices with their start and end apart: 10 -> 24, of which waited for: 7 -> 9; matrix products, arithmetic and copies ran while one was open for 16% -> 28% of each run, Pallas kernels for 0% -> 0%
where the time goes in v7:
time: 290 us; the launch traced here: 288 us
  waiting for transfers between devices  96.8 us (33%)
  starting transfers between devices  65.7 us (23%)
  local copies, waits for them, and re-layouts  60 us (21%)
  matrix products  37.7 us (13%)
  other arithmetic  14.7 us (5%)
  between operations  13.5 us (5%)
    ppermute x15, starting transfers between devices, block_body(): lax.ppermute(out_ext, 'req', [(index, (index + shift) % req_count) for in...  42 us
    reduce_scatter x1, waiting for transfers between devices, block_body(): lax.psum_scatter(jnp.dot(inner, down_weight, preferred_element_type=jnp.f...  37.6 us
    unnamed x88, local copies, waits for them, and re-layouts  31.9 us
    all_gather x1, waiting for transfers between devices, block_body(): gathered = lax.all_gather(normed_mlp, 'mlp', axis=0, tiled=True)  31.6 us
    ppermute x15, waiting for transfers between devices, block_body(): lax.ppermute(out_ext, 'req', [(index, (index + shift) % req_count) for in...  10.9 us
    all_to_all x1, starting transfers between devices, block_body(): lax.all_to_all(local_mod, 'req', split_axis=0, concat_axis=2, tiled=True)[0]  10 us
    sub x1, matrix products, attention(): expo = jnp.where(same, jnp.exp(masked - row_max), 0.0)  8.39 us
    all_to_all x1, starting transfers between devices, block_body(): lax.all_to_all(packed, 'mlp', split_axis=1, concat_axis=0, tiled=True)  7.97 us
  transfers between devices with their start and end apart: 24, of which 9 were waited for; matrix products, arithmetic and copies ran while one was open for 28% of the time, Pallas kernels for 0%

profile of v7, /device:TPU:8, one launch (start us, length us, event | category | flops | bytes accessed | tf_op | source)
XLA Modules:
  0.0 288.4 jit_solution(10641925751163221688)
XLA Ops:
  11.9 6.2 %collective-permute-start.1 = (bf16[592,72]{0,1:T(8,128)(2,1)}, bf16[592,72]{0,1:T(8,128)(2,1)S(1)}, u32[]{:S(2)}, u32[]{:S(2)}) collective-permute-start(bf16[592,72]{0,1:T(8,128)(2,1)} %fusion.64), channel_id=1, source_target_pairs={{0,120},{8,0},{16,8},{24,16},{32,24},{40,32},{48,40},{56,48},{64,5... | collective-permute-start | bytes 255752 | tf_op jit(solution)/shard_map/ppermute | solution.py:137
  18.9 5.4 %collective-permute-start.3 = (bf16[592,72]{0,1:T(8,128)(2,1)}, bf16[592,72]{0,1:T(8,128)(2,1)S(1)}, u32[]{:S(2)}, u32[]{:S(2)}) collective-permute-start(bf16[592,72]{0,1:T(8,128)(2,1)} %fusion.64), channel_id=1, source_target_pairs={{0,104},{8,112},{16,120},{24,0},{32,8},{40,16},{48,24},{56,32},{64... | collective-permute-start | bytes 255752 | tf_op jit(solution)/shard_map/ppermute | solution.py:137
  29.6 2.5 convolution_add_fusion.3
  32.1 3.7 %fusion.35 = bf16[64,576]{1,0:T(8,128)(2,1)} fusion(bf16[1152,576]{0,1:T(8,128)(2,1)} %param.42, f32[64,1152]{1,0:T(8,128)} %convolution_add_fusion.3, bf16[1001,1152]{1,0:T(8,128)(2,1)} %param.37, s32[64]{0:T(128)S(1)} %select_n.71, f32[576]{0:T(1024)S(1)} %convert_element_type.106), kind=kOutput, calls=%fused_computation.41 | convolution fusion | flops 233118272 | bytes 4004608 | tf_op jit(solution)/shard_map/dot_general | solution.py:99
  37.4 10.0 %all-to-all-start = ((bf16[16,4,576]{2,1,0:T(4,128)(2,1)}), bf16[16,4,576]{2,1,0:T(4,128)(2,1)}, u32[]{:S(2)}, u32[]{:S(2)}) async-start(bf16[16,4,576]{2,1,0:T(4,128)(2,1)} %reshape.215), calls=%async_computation | async-start | bytes 163840 | tf_op jit(solution)/shard_map/all_to_all | solution.py:103
  49.8 6.9 %collective-permute-start.6 = (bf16[592,72]{0,1:T(8,128)(2,1)}, bf16[592,72]{0,1:T(8,128)(2,1)S(1)}, u32[]{:S(2)}, u32[]{:S(2)}) collective-permute-start(bf16[592,72]{0,1:T(8,128)(2,1)} %fusion.64), channel_id=1, source_target_pairs={{0,80},{8,88},{16,96},{24,104},{32,112},{40,120},{48,0},{56,8},{64... | collective-permute-start | bytes 255752 | tf_op jit(solution)/shard_map/ppermute | solution.py:137
  59.4 2.1 collective-permute-start.8
  62.2 3.6 %collective-permute-start.9 = (bf16[592,72]{0,1:T(8,128)(2,1)}, bf16[592,72]{0,1:T(8,128)(2,1)S(1)}, u32[]{:S(2)}, u32[]{:S(2)}) collective-permute-start(bf16[592,72]{0,1:T(8,128)(2,1)} %fusion.64), channel_id=1, source_target_pairs={{0,56},{8,64},{16,72},{24,80},{32,88},{40,96},{48,104},{56,112},{6... | collective-permute-start | bytes 255752 | tf_op jit(solution)/shard_map/ppermute | solution.py:137
  66.4 2.1 collective-permute-start.10
  73.0 3.0 %collective-permute-start.13 = (bf16[592,72]{0,1:T(8,128)(2,1)}, bf16[592,72]{0,1:T(8,128)(2,1)S(1)}, u32[]{:S(2)}, u32[]{:S(2)}) collective-permute-start(bf16[592,72]{0,1:T(8,128)(2,1)} %fusion.64), channel_id=1, source_target_pairs={{0,24},{8,32},{16,40},{24,48},{32,56},{40,64},{48,72},{56,80},{64,... | collective-permute-start | bytes 255752 | tf_op jit(solution)/shard_map/ppermute | solution.py:137
  76.9 6.6 %collective-permute-start.14 = (bf16[592,72]{0,1:T(8,128)(2,1)}, bf16[592,72]{0,1:T(8,128)(2,1)S(1)}, u32[]{:S(2)}, u32[]{:S(2)}) collective-permute-start(bf16[592,72]{0,1:T(8,128)(2,1)} %fusion.64), channel_id=1, source_target_pairs={{0,16},{8,24},{16,32},{24,40},{32,48},{40,56},{48,64},{56,72},{64,... | collective-permute-start | bytes 255752 | tf_op jit(solution)/shard_map/ppermute | solution.py:137
  87.5 8.8 %collective-permute-done.14 = bf16[592,72]{0,1:T(8,128)(2,1)S(1)} collective-permute-done((bf16[592,72]{0,1:T(8,128)(2,1)}, bf16[592,72]{0,1:T(8,128)(2,1)S(1)}, u32[]{:S(2)}, u32[]{:S(2)}) %collective-permute-start.14) | collective-permute-done | bytes 85280 | tf_op jit(solution)/shard_map/ppermute | solution.py:137
  101.5 5.1 %all-gather.3.cloned.1.call-done = bf16[592,3456]{0,1:T(8,128)(2,1)} async-done(((bf16[592,216]{0,1:T(8,128)(2,1)}), bf16[592,3456]{0,1:T(8,128)(2,1)}) %all-gather.3.cloned.1.call-update) | async-done | bytes 4091920 | tf_op jit(solution)/shard_map/all_gather | solution.py:122
  106.6 7.0 %copy.87 = bf16[592,3456]{1,0:T(8,128)(2,1)} copy(bf16[592,3456]{0,1:T(8,128)(2,1)} %all-gather.3.cloned.1.call-done) | data formatting | bytes 8183808 | tf_op jit(solution)/shard_map/all_gather | solution.py:122
  129.5 2.1 copy-done.2
  134.2 4.1 %fusion.3 = bf16[128,3456]{1,0:T(8,128)(2,1)} fusion(f32[128,3456]{1,0:T(8,128)S(1)} %fusion.4, bf16[592,3456]{1,0:T(8,128)(2,1)} %collective-permute-done, f32[3456]{0:T(1024)S(1)} %convert_reduce_fusion, bf16[128,1152]{1,0:T(8,128)(2,1)S(1)} %fusion.44, s32[]{:T(128)S(6)} %select_n.74), kind=kOutput, calls=%fused_computation.6 | convolution fusion | flops 510935040 | bytes 6815748 | tf_op jit(solution)/shard_map/dot_general | solution.py:157
  138.3 2.3 copy.88
  140.6 2.2 copy.89
  142.7 8.0 %all-to-all-start.1 = ((bf16[128,8,432]{0,2,1:T(8,128)(2,1)}), bf16[128,8,432]{0,2,1:T(8,128)(2,1)}, u32[]{:S(2)}, u32[]{:S(2)}) async-start(bf16[128,8,432]{0,2,1:T(8,128)(2,1)} %bitcast.129), calls=%async_computation.1 | async-start | bytes 1769472 | tf_op jit(solution)/shard_map/all_to_all | solution.py:167
  153.4 2.6 constant_dynamic-slice_fusion.1
  156.0 3.5 %copy.94 = bf16[592,1152]{1,0:T(8,128)(2,1)} copy(bf16[592,1152]{0,1:T(8,128)(2,1)} %bitcast.128) | data formatting | bytes 2727936 | tf_op jit(solution)/shard_map/reshape | solution.py:146
  160.1 4.9 %all-to-all-done.1 = bf16[128,8,432]{0,2,1:T(8,128)(2,1)} async-done(((bf16[128,8,432]{0,2,1:T(8,128)(2,1)}), bf16[128,8,432]{0,2,1:T(8,128)(2,1)}, u32[]{:S(2)}, u32[]{:S(2)}) %all-to-all-start.1) | async-done | bytes 884768 | tf_op jit(solution)/shard_map/all_to_all | solution.py:167
  167.1 8.4 %fusion.93 = (f32[2,1024]{1,0:T(2,128)S(1)}, bf16[2,1024,1024]{1,2,0:T(8,128)(2,1)}) fusion(pred[1024,1024]{0,1:T(8,128)(4,1)} %broadcast_compare_fusion, bf16[1024,2,72]{0,2,1:T(8,128)(2,1)} %bitcast.136, bf16[1024,2,72]{0,2,1:T(8,128)(2,1)S(1)} %bitcast.135), kind=kOutput, calls=%fused_computation.162 | convolution fusion | flops 314573824 | bytes 5840896 | tf_op jit(solution)/shard_map/sub | solution.py:40
  175.4 3.0 %fusion.32 = bf16[1024,2,72]{0,2,1:T(8,128)(2,1)S(1)} fusion(bf16[1024,2,72]{0,2,1:T(8,128)(2,1)S(1)} %bitcast.134, bf16[2,1024,1024]{1,2,0:T(8,128)(2,1)} %get-tuple-element.40, f32[1024,2]{0,1:T(2,128)S(1)} %bitcast.144), kind=kOutput, calls=%fused_computation.39 | convolution fusion | flops 302284800 | bytes 4792320 | tf_op jit(solution)/shard_map/hqk,khd->qhd/dot_general | solution.py:43
  179.3 3.4 %all-to-all-start.2 = ((bf16[8,128,144]{1,2,0:T(8,128)(2,1)}), bf16[8,128,144]{1,2,0:T(8,128)(2,1)S(1)}, u32[]{:S(2)}, u32[]{:S(2)}) async-start(bf16[8,128,144]{1,2,0:T(8,128)(2,1)} %copy.92), calls=%async_computation.2 | async-start | bytes 589824 | tf_op jit(solution)/shard_map/all_to_all | solution.py:175
  185.9 4.6 %all-to-all-done.2 = bf16[8,128,144]{1,2,0:T(8,128)(2,1)S(1)} async-done(((bf16[8,128,144]{1,2,0:T(8,128)(2,1)}), bf16[8,128,144]{1,2,0:T(8,128)(2,1)S(1)}, u32[]{:S(2)}, u32[]{:S(2)}) %all-to-all-start.2) | async-done | bytes 294944 | tf_op jit(solution)/shard_map/all_to_all | solution.py:175
  190.5 2.1 fusion.57
  192.6 2.1 fusion.94
  195.0 2.1 fusion.47
  197.2 31.6 %all-gather.5.cloned.1.call-done = bf16[1024,1152]{1,0:T(8,128)(2,1)} async-done(((bf16[128,1152]{1,0:T(8,128)(2,1)}), bf16[1024,1152]{1,0:T(8,128)(2,1)}) %all-gather.5.cloned.1.call-update) | async-done | bytes 2359312 | tf_op jit(solution)/shard_map/all_gather | solution.py:179
  228.8 7.9 %convolution_convert_fusion = bf16[1024,1152]{1,0:T(8,128)(2,1)} fusion(bf16[576,1152]{1,0:T(8,128)(2,1)} %param.50, bf16[1024,1152]{1,0:T(8,128)(2,1)} %all-gather.5.cloned.1.call-done, bf16[1152,576]{0,1:T(8,128)(2,1)} %param.48, f32[576]{0:T(1024)S(1)} %convert_element_type.117), kind=kOutput, calls=%fused_computation.15 | convolution fusion | flops 2724986880 | bytes 7375104 | tf_op jit(solution)/shard_map/dot_general | solution.py:186
  236.8 37.6 %reduce-scatter.2.cloned.1.call-done = bf16[128,1152]{1,0:T(8,128)(2,1)} async-done(((bf16[1024,1152]{1,0:T(8,128)(2,1)}), bf16[128,1152]{1,0:T(8,128)(2,1)}) %reduce-scatter.2.cloned.1.call-update) | async-done | bytes 294928 | tf_op jit(solution)/shard_map/reduce_scatter | solution.py:185
  (174 shorter events, 69.1 us)
Async XLA Ops:
  6.5 23.0 %copy-start = (bf16[1152,1152]{1,0:T(8,128)(2,1)S(1)}, bf16[1152,1152]{1,0:T(8,128)(2,1)}, u32[]{:S(2)}) copy-start(bf16[1152,1152]{1,0:T(8,128)(2,1)} %param.40) | copy-start | bytes 7962628
  6.5 100.1 %all-gather.3.cloned.1.call-start = ((), (), s32[]{:S(2)}) async-start(), calls=%async_computation.4 | async-start | bytes 4700160 | tf_op jit(solution)/shard_map/all_gather | solution.py:122
  11.9 37.9 %collective-permute-start.1 = (bf16[592,72]{0,1:T(8,128)(2,1)}, bf16[592,72]{0,1:T(8,128)(2,1)S(1)}, u32[]{:S(2)}, u32[]{:S(2)}) collective-permute-start(bf16[592,72]{0,1:T(8,128)(2,1)} %fusion.64), channel_id=1, source_target_pairs={{0,120},{8,0},{16,8},{24,16},{32,24},{40,32},{48,40},{56,48},{64,5... | collective-permute-start | bytes 255752 | tf_op jit(solution)/shard_map/ppermute | solution.py:137
  18.1 39.3 %collective-permute-start.2 = (bf16[592,72]{0,1:T(8,128)(2,1)}, bf16[592,72]{0,1:T(8,128)(2,1)S(1)}, u32[]{:S(2)}, u32[]{:S(2)}) collective-permute-start(bf16[592,72]{0,1:T(8,128)(2,1)} %fusion.64), channel_id=1, source_target_pairs={{0,112},{8,120},{16,0},{24,8},{32,16},{40,24},{48,32},{56,40},{64,... | collective-permute-start | bytes 255752 | tf_op jit(solution)/shard_map/ppermute | solution.py:137
  18.9 40.5 %collective-permute-start.3 = (bf16[592,72]{0,1:T(8,128)(2,1)}, bf16[592,72]{0,1:T(8,128)(2,1)S(1)}, u32[]{:S(2)}, u32[]{:S(2)}) collective-permute-start(bf16[592,72]{0,1:T(8,128)(2,1)} %fusion.64), channel_id=1, source_target_pairs={{0,104},{8,112},{16,120},{24,0},{32,8},{40,16},{48,24},{56,32},{64... | collective-permute-start | bytes 255752 | tf_op jit(solution)/shard_map/ppermute | solution.py:137
  24.3 37.8 %collective-permute-start.4 = (bf16[592,72]{0,1:T(8,128)(2,1)}, bf16[592,72]{0,1:T(8,128)(2,1)S(1)}, u32[]{:S(2)}, u32[]{:S(2)}) collective-permute-start(bf16[592,72]{0,1:T(8,128)(2,1)} %fusion.64), channel_id=1, source_target_pairs={{0,96},{8,104},{16,112},{24,120},{32,0},{40,8},{48,16},{56,24},{64... | collective-permute-start | bytes 255752 | tf_op jit(solution)/shard_map/ppermute | solution.py:137
  25.1 41.3 %collective-permute-start.5 = (bf16[592,72]{0,1:T(8,128)(2,1)}, bf16[592,72]{0,1:T(8,128)(2,1)S(1)}, u32[]{:S(2)}, u32[]{:S(2)}) collective-permute-start(bf16[592,72]{0,1:T(8,128)(2,1)} %fusion.64), channel_id=1, source_target_pairs={{0,88},{8,96},{16,104},{24,112},{32,120},{40,0},{48,8},{56,16},{64... | collective-permute-start | bytes 255752 | tf_op jit(solution)/shard_map/ppermute | solution.py:137
  37.4 90.3 %all-to-all-start = ((bf16[16,4,576]{2,1,0:T(4,128)(2,1)}), bf16[16,4,576]{2,1,0:T(4,128)(2,1)}, u32[]{:S(2)}, u32[]{:S(2)}) async-start(bf16[16,4,576]{2,1,0:T(4,128)(2,1)} %reshape.215), calls=%async_computation | async-start | bytes 163840 | tf_op jit(solution)/shard_map/all_to_all | solution.py:103
  49.8 19.3 %collective-permute-start.6 = (bf16[592,72]{0,1:T(8,128)(2,1)}, bf16[592,72]{0,1:T(8,128)(2,1)S(1)}, u32[]{:S(2)}, u32[]{:S(2)}) collective-permute-start(bf16[592,72]{0,1:T(8,128)(2,1)} %fusion.64), channel_id=1, source_target_pairs={{0,80},{8,88},{16,96},{24,104},{32,112},{40,120},{48,0},{56,8},{64... | collective-permute-start | bytes 255752 | tf_op jit(solution)/shard_map/ppermute | solution.py:137
  57.3 13.6 %collective-permute-start.7 = (bf16[592,72]{0,1:T(8,128)(2,1)}, bf16[592,72]{0,1:T(8,128)(2,1)S(1)}, u32[]{:S(2)}, u32[]{:S(2)}) collective-permute-start(bf16[592,72]{0,1:T(8,128)(2,1)} %fusion.64), channel_id=1, source_target_pairs={{0,72},{8,80},{16,88},{24,96},{32,104},{40,112},{48,120},{56,0},{6... | collective-permute-start | bytes 255752 | tf_op jit(solution)/shard_map/ppermute | solution.py:137
  59.4 13.6 %collective-permute-start.8 = (bf16[592,72]{0,1:T(8,128)(2,1)}, bf16[592,72]{0,1:T(8,128)(2,1)S(1)}, u32[]{:S(2)}, u32[]{:S(2)}) collective-permute-start(bf16[592,72]{0,1:T(8,128)(2,1)} %fusion.64), channel_id=1, source_target_pairs={{0,64},{8,72},{16,80},{24,88},{32,96},{40,104},{48,112},{56,120},{... | collective-permute-start | bytes 255752 | tf_op jit(solution)/shard_map/ppermute | solution.py:137
  62.2 14.7 %collective-permute-start.9 = (bf16[592,72]{0,1:T(8,128)(2,1)}, bf16[592,72]{0,1:T(8,128)(2,1)S(1)}, u32[]{:S(2)}, u32[]{:S(2)}) collective-permute-start(bf16[592,72]{0,1:T(8,128)(2,1)} %fusion.64), channel_id=1, source_target_pairs={{0,56},{8,64},{16,72},{24,80},{32,88},{40,96},{48,104},{56,112},{6... | collective-permute-start | bytes 255752 | tf_op jit(solution)/shard_map/ppermute | solution.py:137
  66.4 17.8 %collective-permute-start.10 = (bf16[592,72]{0,1:T(8,128)(2,1)}, bf16[592,72]{0,1:T(8,128)(2,1)S(1)}, u32[]{:S(2)}, u32[]{:S(2)}) collective-permute-start(bf16[592,72]{0,1:T(8,128)(2,1)} %fusion.64), channel_id=1, source_target_pairs={{0,48},{8,56},{16,64},{24,72},{32,80},{40,88},{48,96},{56,104},{64... | collective-permute-start | bytes 255752 | tf_op jit(solution)/shard_map/ppermute | solution.py:137
  69.1 15.7 %collective-permute-start.11 = (bf16[592,72]{0,1:T(8,128)(2,1)}, bf16[592,72]{0,1:T(8,128)(2,1)S(1)}, u32[]{:S(2)}, u32[]{:S(2)}) collective-permute-start(bf16[592,72]{0,1:T(8,128)(2,1)} %fusion.64), channel_id=1, source_target_pairs={{0,40},{8,48},{16,56},{24,64},{32,72},{40,80},{48,88},{56,96},{64,... | collective-permute-start | bytes 255752 | tf_op jit(solution)/shard_map/ppermute | solution.py:137
  70.9 14.6 %collective-permute-start.12 = (bf16[592,72]{0,1:T(8,128)(2,1)}, bf16[592,72]{0,1:T(8,128)(2,1)S(1)}, u32[]{:S(2)}, u32[]{:S(2)}) collective-permute-start(bf16[592,72]{0,1:T(8,128)(2,1)} %fusion.64), channel_id=1, source_target_pairs={{0,32},{8,40},{16,48},{24,56},{32,64},{40,72},{48,80},{56,88},{64,... | collective-permute-start | bytes 255752 | tf_op jit(solution)/shard_map/ppermute | solution.py:137
  73.0 13.2 %collective-permute-start.13 = (bf16[592,72]{0,1:T(8,128)(2,1)}, bf16[592,72]{0,1:T(8,128)(2,1)S(1)}, u32[]{:S(2)}, u32[]{:S(2)}) collective-permute-start(bf16[592,72]{0,1:T(8,128)(2,1)} %fusion.64), channel_id=1, source_target_pairs={{0,24},{8,32},{16,40},{24,48},{32,56},{40,64},{48,72},{56,80},{64,... | collective-permute-start | bytes 255752 | tf_op jit(solution)/shard_map/ppermute | solution.py:137
  76.9 19.4 %collective-permute-start.14 = (bf16[592,72]{0,1:T(8,128)(2,1)}, bf16[592,72]{0,1:T(8,128)(2,1)S(1)}, u32[]{:S(2)}, u32[]{:S(2)}) collective-permute-start(bf16[592,72]{0,1:T(8,128)(2,1)} %fusion.64), channel_id=1, source_target_pairs={{0,16},{8,24},{16,32},{24,40},{32,48},{40,56},{48,64},{56,72},{64,... | collective-permute-start | bytes 255752 | tf_op jit(solution)/shard_map/ppermute | solution.py:137
  84.2 15.3 %collective-permute-start.15 = (bf16[592,72]{0,1:T(8,128)(2,1)}, bf16[592,72]{0,1:T(8,128)(2,1)S(1)}, u32[]{:S(2)}, u32[]{:S(2)}) collective-permute-start(bf16[592,72]{0,1:T(8,128)(2,1)} %fusion.64), channel_id=1, source_target_pairs={{0,8},{8,16},{16,24},{24,32},{32,40},{40,48},{48,56},{56,64},{64,7... | collective-permute-start | bytes 255752 | tf_op jit(solution)/shard_map/ppermute | solution.py:137
  113.6 20.6 %collective-permute-start = (bf16[592,3456]{1,0:T(8,128)(2,1)}, bf16[592,3456]{1,0:T(8,128)(2,1)}, u32[]{:S(2)}, u32[]{:S(2)}) collective-permute-start(bf16[592,3456]{1,0:T(8,128)(2,1)} %copy.87), channel_id=1, source_target_pairs={{0,1},{1,0},{2,3},{3,2},{4,5},{5,4},{6,7},{7,6},{8,9},{9,8},{10,11... | collective-permute-start | bytes 12275720 | tf_op jit(solution)/shard_map/ppermute | solution.py:149
  142.7 22.3 %all-to-all-start.1 = ((bf16[128,8,432]{0,2,1:T(8,128)(2,1)}), bf16[128,8,432]{0,2,1:T(8,128)(2,1)}, u32[]{:S(2)}, u32[]{:S(2)}) async-start(bf16[128,8,432]{0,2,1:T(8,128)(2,1)} %bitcast.129), calls=%async_computation.1 | async-start | bytes 1769472 | tf_op jit(solution)/shard_map/all_to_all | solution.py:167
  159.5 33.1 %collective-permute-start.16 = (bf16[592,1152]{1,0:T(8,128)(2,1)}, bf16[592,1152]{1,0:T(8,128)(2,1)}, u32[]{:S(2)}, u32[]{:S(2)}) collective-permute-start(bf16[592,1152]{1,0:T(8,128)(2,1)} %copy.94), channel_id=1, source_target_pairs={{0,1},{1,0},{2,3},{3,2},{4,5},{5,4},{6,7},{7,6},{8,9},{9,8},{10,11... | collective-permute-start | bytes 4091912 | tf_op jit(solution)/shard_map/ppermute | solution.py:150
  179.3 11.2 %all-to-all-start.2 = ((bf16[8,128,144]{1,2,0:T(8,128)(2,1)}), bf16[8,128,144]{1,2,0:T(8,128)(2,1)S(1)}, u32[]{:S(2)}, u32[]{:S(2)}) async-start(bf16[8,128,144]{1,2,0:T(8,128)(2,1)} %copy.92), calls=%async_computation.2 | async-start | bytes 589824 | tf_op jit(solution)/shard_map/all_to_all | solution.py:175
  182.7 46.1 %all-gather.5.cloned.1.call-start = ((), (), s32[]{:S(2)}) async-start(), calls=%async_computation.5 | async-start | bytes 2654208 | tf_op jit(solution)/shard_map/all_gather | solution.py:179
  197.1 77.3 %reduce-scatter.2.cloned.1.call-start = ((), (), s32[]{:S(2)}) async-start(), calls=%async_computation.6 | async-start | bytes 2654208 | tf_op jit(solution)/shard_map/reduce_scatter | solution.py:185
  197.2 39.6 %copy-start.20 = (bf16[1152]{0:T(1024)(128)(2,1)S(1)}, bf16[1152]{0:T(1024)(128)(2,1)}, u32[]{:S(2)}) copy-start(bf16[1152]{0:T(1024)(128)(2,1)} %param.51) | copy-start | bytes 6916
  197.2 39.6 %copy-start.27 = (bf16[16]{0:T(256)(128)(2,1)S(1)}, bf16[16]{0:T(256)(128)(2,1)}, u32[]{:S(2)}) copy-start(bf16[16]{0:T(256)(128)(2,1)} %param.53) | copy-start | bytes 100
  236.7 39.3 %copy-start.19 = (bf16[1152,16]{0,1:T(8,128)(2,1)S(1)}, bf16[1152,16]{0,1:T(8,128)(2,1)}, u32[]{:S(2)}) copy-start(bf16[1152,16]{0,1:T(8,128)(2,1)} %param.52) | copy-start | bytes 110596
  236.7 42.5 %copy-start.23 = (f32[1,4]{1,0:T(1,128)S(1)}, f32[1,4]{1,0:T(1,128)}, u32[]{:S(2)}) copy-start(f32[1,4]{1,0:T(1,128)} %param.35) | copy-start | bytes 52
  236.7 42.5 %copy-start.24 = (f32[1,4]{1,0:T(1,128)S(1)}, f32[1,4]{1,0:T(1,128)}, u32[]{:S(2)}) copy-start(f32[1,4]{1,0:T(1,128)} %param.34) | copy-start | bytes 52
  236.7 42.5 %copy-start.25 = (f32[1,4]{1,0:T(1,128)S(1)}, f32[1,4]{1,0:T(1,128)}, u32[]{:S(2)}) copy-start(f32[1,4]{1,0:T(1,128)} %param.36) | copy-start | bytes 52
  236.8 44.5 %copy-start.21 = (f32[128,8]{0,1:T(8,128)S(1)}, f32[128,8]{0,1:T(8,128)}, u32[]{:S(2)}) copy-start(f32[128,8]{0,1:T(8,128)} %param.30) | copy-start | bytes 12292
  277.6 3.7 %collective-permute-start.17 = (f32[128,8]{0,1:T(8,128)S(1)}, f32[128,8]{0,1:T(8,128)S(1)}, u32[]{:S(2)}, u32[]{:S(2)}) collective-permute-start(f32[128,8]{0,1:T(8,128)S(1)} %constant_dynamic-slice_fusion), channel_id=1, source_target_pairs={{0,128},{128,0},{1,129},{129,1},{2,130},{130,2},{3,131},{131,3},{4... | collective-permute-start | bytes 12296 | tf_op jit(solution)/shard_map/ppermute | solution.py:202
  (20 other events, 170.9 us)
Sparse Core Ops, SparseCore 0:
  9.8 96.7 all-gather.2
  197.3 31.5 all-gather.4
  236.9 37.4 reduce-scatter.1

commit v8 on v5

--- a/solution.py
+++ b/solution.py
@@ -130,13 +130,25 @@
     qkv_other = lax.ppermute(qkv_mine, "mlp", pair)
     out_other = lax.ppermute(out_mine, "mlp", pair)
 
+    bias_pick = (jnp.arange(16) == 0).astype(jnp.bfloat16)
+
     def split_dot(values, mine, other):
-        values_mine = lax.dynamic_slice_in_dim(values, core * half_rows, half_rows, axis=1)
-        values_other = lax.dynamic_slice_in_dim(values, (1 - core) * half_rows, half_rows, axis=1)
-        return (
-            jnp.dot(values_mine, mine[:half_rows], preferred_element_type=jnp.float32)
-            + jnp.dot(values_other, other[:half_rows], preferred_element_type=jnp.float32)
-            + mine[half_rows].astype(jnp.float32)
+        values_mine = jnp.concatenate(
+            [
+                lax.dynamic_slice_in_dim(values, core * half_rows, half_rows, axis=1),
+                jnp.broadcast_to(bias_pick, (values.shape[0], 16)),
+            ],
+            axis=1,
+        )
+        values_other = jnp.concatenate(
+            [
+                lax.dynamic_slice_in_dim(values, (1 - core) * half_rows, half_rows, axis=1),
+                jnp.zeros((values.shape[0], 16), values.dtype),
+            ],
+            axis=1,
+        )
+        return jnp.dot(values_mine, mine, preferred_element_type=jnp.float32) + jnp.dot(
+            values_other, other, preferred_element_type=jnp.float32
         )
 
     qkv = split_dot(normed, qkv_mine, qkv_other).astype(jnp.bfloat16)

time: 294 us -> 292 us (level)
  blocking collectives: 0 us -> 12 us
  waiting for transfers between devices: 185 us -> 180 us
  starting transfers between devices: 19.7 us -> 15.5 us
  other arithmetic: 12 us -> 8.94 us
    all_to_all x0 -> x1, blocking collectives: none -> 12 us  [block_body(): lax.all_to_all(attended_heads, 'mlp', split_axis=0, concat_axis=1, tiled=...]
    all_to_all x1 -> x0, waiting for transfers between devices: 6.58 us -> none  [block_body(): lax.all_to_all(attended_heads, 'mlp', split_axis=0, concat_axis=1, tiled=...]
    all_to_all x1 -> x0, starting transfers between devices: 4.22 us -> none  [block_body(): lax.all_to_all(attended_heads, 'mlp', split_axis=0, concat_axis=1, tiled=...]
    add x2 -> x0, other arithmetic: 3.03 us -> none  [split_dot(): jnp.dot(values_mine, mine[:half_rows], preferred_element_type=jnp.float32)]
  transfers between devices with their start and end apart: 10 -> 9, of which waited for: 7 -> 6; matrix products, arithmetic and copies ran while one was open for 16% -> 14% of each run, Pallas kernels for 0% -> 0%
where the time goes in v8:
time: 292 us; the launch traced here: 291 us
  waiting for transfers between devices  180 us (62%)
  matrix products  37 us (13%)
  local copies, waits for them, and re-layouts  23.7 us (8%)
  starting transfers between devices  15.5 us (5%)
  between operations  13.6 us (5%)
  blocking collectives  12 us (4%)
  other arithmetic  8.94 us (3%)
    all_gather x2, waiting for transfers between devices, half_gather(): lax.all_gather(jnp.concatenate([mine, bias_rows], axis=0), 'req', axis=1,...  108 us
    reduce_scatter x1, waiting for transfers between devices, block_body(): lax.psum_scatter(jnp.dot(inner, down_weight, preferred_element_type=jnp.f...  37 us
    all_gather x1, waiting for transfers between devices, block_body(): gathered = lax.all_gather(normed_mlp, 'mlp', axis=0, tiled=True)  25 us
    all_to_all x1, blocking collectives, block_body(): lax.all_to_all(attended_heads, 'mlp', split_axis=0, concat_axis=1, tiled=...  12 us
    all_gather x2, local copies, waits for them, and re-layouts, half_gather(): lax.all_gather(jnp.concatenate([mine, bias_rows], axis=0), 'req', axis=1,...  10.6 us
    all_to_all x1, starting transfers between devices, block_body(): lax.all_to_all(local_mod, 'req', split_axis=0, concat_axis=2, tiled=True)[0]  9.51 us
    sub x1, matrix products, attention(): expo = jnp.where(same, jnp.exp(masked - row_max), 0.0)  8.44 us
    all_to_all x1, waiting for transfers between devices, block_body(): lax.all_to_all(local_mod, 'req', split_axis=0, concat_axis=2, tiled=True)[0]  7.97 us
  transfers between devices with their start and end apart: 9, of which 6 were waited for; matrix products, arithmetic and copies ran while one was open for 14% of the time, Pallas kernels for 0%

profile of v8, /device:TPU:8, one launch (start us, length us, event | category | flops | bytes accessed | tf_op | source)
XLA Modules:
  0.0 291.1 jit_solution(4638609540781609865)
XLA Ops:
  6.5 0.9 reshape.209
  7.4 1.1 constant_dynamic-slice_fusion.5
  9.5 79.9 %all-gather.4.cloned.1.call-done = bf16[592,3456]{0,1:T(8,128)(2,1)} async-done(((bf16[592,216]{0,1:T(8,128)(2,1)}), bf16[592,3456]{0,1:T(8,128)(2,1)}) %all-gather.4.cloned.1.call-update) | async-done | bytes 4091920 | tf_op jit(solution)/shard_map/all_gather | solution.py:122
  89.3 7.0 %copy.79 = bf16[592,3456]{1,0:T(8,128)(2,1)} copy(bf16[592,3456]{0,1:T(8,128)(2,1)} %all-gather.4.cloned.1.call-done) | data formatting | bytes 8183808 | tf_op jit(solution)/shard_map/all_gather | solution.py:122
  97.0 1.8 convolution_add_fusion.3
  98.9 3.0 %fusion.29 = bf16[64,576]{1,0:T(8,128)(2,1)S(1)} fusion(bf16[1152,576]{0,1:T(8,128)(2,1)} %param.42, f32[64,1152]{1,0:T(8,128)S(1)} %convolution_add_fusion.3, bf16[1001,1152]{1,0:T(8,128)(2,1)} %param.37, s32[64]{0:T(128)S(1)} %select_n.64, f32[576]{0:T(1024)S(1)} %convert_element_type.99), kind=kOutput, calls=%fused_computation.34 | convolution fusion | flops 233118272 | bytes 4004608 | tf_op jit(solution)/shard_map/dot_general | solution.py:99
  102.6 9.5 %all-to-all-start = ((bf16[16,4,576]{2,1,0:T(4,128)(2,1)}), bf16[16,4,576]{2,1,0:T(4,128)(2,1)S(1)}, u32[]{:S(2)}, u32[]{:S(2)}) async-start(bf16[16,4,576]{2,1,0:T(4,128)(2,1)} %reshape.202), calls=%async_computation | async-start | bytes 163840 | tf_op jit(solution)/shard_map/all_to_all | solution.py:103
  112.8 8.0 %all-to-all-done = bf16[16,4,576]{2,1,0:T(4,128)(2,1)S(1)} async-done(((bf16[16,4,576]{2,1,0:T(4,128)(2,1)}), bf16[16,4,576]{2,1,0:T(4,128)(2,1)S(1)}, u32[]{:S(2)}, u32[]{:S(2)}) %all-to-all-start) | async-done | bytes 73760 | tf_op jit(solution)/shard_map/all_to_all | solution.py:103
  122.1 0.8 fusion.72
  122.9 2.1 copy-done.1
  125.5 3.6 %fusion.48 = f32[128,3456]{1,0:T(8,128)S(1)} fusion(bf16[592,3456]{0,1:T(8,128)(2,1)} %all-gather.4.cloned.1.call-done, bf16[128,576]{1,0:T(8,128)(2,1)S(1)} %get-tuple-element.44, bf16[592]{0:T(1024)(128)(2,1)S(1)} %pad.15.clone), kind=kOutput, calls=%fused_computation.68 | convolution fusion | flops 524066816 | bytes 6010016 | tf_op jit(solution)/shard_map/dot_general | solution.py:150
  129.2 4.0 %fusion.2 = bf16[128,3456]{1,0:T(8,128)(2,1)} fusion(f32[128,3456]{1,0:T(8,128)S(1)} %fusion.48, bf16[592,3456]{1,0:T(8,128)(2,1)} %collective-permute-done, bf16[128,576]{1,0:T(8,128)(2,1)S(1)} %get-tuple-element.43), kind=kOutput, calls=%fused_computation.5 | convolution fusion | flops 524648448 | bytes 6893568 | tf_op jit(solution)/shard_map/dot_general | solution.py:150
  133.2 2.2 copy.80
  135.4 2.2 copy.81
  137.6 4.2 %all-to-all-start.1 = ((bf16[128,8,432]{0,2,1:T(8,128)(2,1)}), bf16[128,8,432]{0,2,1:T(8,128)(2,1)}, u32[]{:S(2)}, u32[]{:S(2)}) async-start(bf16[128,8,432]{0,2,1:T(8,128)(2,1)} %bitcast.76), calls=%async_computation.1 | async-start | bytes 1769472 | tf_op jit(solution)/shard_map/all_to_all | solution.py:160
  141.9 1.7 broadcast_compare_fusion
  143.6 28.5 %all-gather.6.cloned.1.call-done = bf16[592,1152]{0,1:T(8,128)(2,1)} async-done(((bf16[592,72]{0,1:T(8,128)(2,1)}), bf16[592,1152]{0,1:T(8,128)(2,1)}) %all-gather.6.cloned.1.call-update) | async-done | bytes 1363984 | tf_op jit(solution)/shard_map/all_gather | solution.py:122
  172.1 3.6 %copy.87 = bf16[592,1152]{1,0:T(8,128)(2,1)} copy(bf16[592,1152]{0,1:T(8,128)(2,1)} %all-gather.6.cloned.1.call-done) | data formatting | bytes 2727936 | tf_op jit(solution)/shard_map/all_gather | solution.py:122
  175.6 1.3 copy_bitcast_fusion
  176.9 0.8 fusion.91
  177.7 8.4 %fusion.92 = (f32[2,1024]{1,0:T(2,128)S(1)}, bf16[2,1024,1024]{1,2,0:T(8,128)(2,1)}) fusion(pred[1024,1024]{0,1:T(8,128)(4,1)} %broadcast_compare_fusion, bf16[1024,2,72]{0,2,1:T(8,128)(2,1)} %bitcast.83, bf16[1024,2,72]{0,2,1:T(8,128)(2,1)S(1)} %bitcast.82), kind=kOutput, calls=%fused_computation.131 | convolution fusion | flops 314573824 | bytes 5840896 | tf_op jit(solution)/shard_map/sub | solution.py:40
  186.2 3.0 %fusion.26 = bf16[1024,2,72]{0,2,1:T(8,128)(2,1)S(1)} fusion(bf16[1024,2,72]{0,2,1:T(8,128)(2,1)S(1)} %bitcast.81, bf16[2,1024,1024]{1,2,0:T(8,128)(2,1)} %get-tuple-element.48, f32[1024,2]{0,1:T(2,128)S(1)} %bitcast.91), kind=kOutput, calls=%fused_computation.32 | convolution fusion | flops 302284800 | bytes 4792320 | tf_op jit(solution)/shard_map/hqk,khd->qhd/dot_general | solution.py:43
  189.3 12.0 %all_to_all.53 = bf16[8,128,144]{1,2,0:T(8,128)(2,1)S(1)} all-to-all(bf16[8,128,144]{1,2,0:T(8,128)(2,1)S(1)} %copy.84), channel_id=1, replica_groups=mesh['cfg'=2,'req'=16,'mlp'=8] {'mlp'}, dimensions={0} | all-to-all | bytes 589824 | tf_op jit(solution)/shard_map/all_to_all | solution.py:168
  202.1 2.0 fusion.93
  204.4 2.2 fusion.41
  206.6 25.0 %all-gather.8.cloned.1.call-done = bf16[1024,1152]{1,0:T(8,128)(2,1)} async-done(((bf16[128,1152]{1,0:T(8,128)(2,1)}), bf16[1024,1152]{1,0:T(8,128)(2,1)}) %all-gather.8.cloned.1.call-update) | async-done | bytes 2359312 | tf_op jit(solution)/shard_map/all_gather | solution.py:172
  231.6 7.9 %convolution_convert_fusion = bf16[1024,1152]{1,0:T(8,128)(2,1)} fusion(bf16[576,1152]{1,0:T(8,128)(2,1)} %param.50, bf16[1024,1152]{1,0:T(8,128)(2,1)} %all-gather.8.cloned.1.call-done, bf16[1152,576]{0,1:T(8,128)(2,1)} %param.48, f32[576]{0:T(1024)S(1)} %convert_element_type.109), kind=kOutput, calls=%fused_computation.11 | convolution fusion | flops 2724986880 | bytes 7375104 | tf_op jit(solution)/shard_map/dot_general | solution.py:179
  240.2 37.0 %reduce-scatter.2.cloned.1.call-done = bf16[128,1152]{1,0:T(8,128)(2,1)} async-done(((bf16[1024,1152]{1,0:T(8,128)(2,1)}), bf16[128,1152]{1,0:T(8,128)(2,1)}) %reduce-scatter.2.cloned.1.call-update) | async-done | bytes 294928 | tf_op jit(solution)/shard_map/reduce_scatter | solution.py:178
  277.2 1.3 fusion.89
  278.8 1.5 convolution_add_fusion.6
  280.3 1.6 collective-permute-start.2
  282.0 2.0 collective-permute-done.2
  (97 shorter events, 7.2 us)
Async XLA Ops:
  6.5 90.5 %copy-start = (bf16[1152,1152]{1,0:T(8,128)(2,1)S(1)}, bf16[1152,1152]{1,0:T(8,128)(2,1)}, u32[]{:S(2)}) copy-start(bf16[1152,1152]{1,0:T(8,128)(2,1)} %param.40) | copy-start | bytes 7962628
  6.5 82.8 %all-gather.4.cloned.1.call-start = ((), (), s32[]{:S(2)}) async-start(), calls=%async_computation.4 | async-start | bytes 4700160 | tf_op jit(solution)/shard_map/all_gather | solution.py:122
  9.4 87.0 %copy-start.12 = (s32[16,4]{0,1:T(4,128)S(1)}, s32[16,4]{0,1:T(4,128)}, u32[]{:S(2)}) copy-start(s32[16,4]{0,1:T(4,128)} %param.31) | copy-start | bytes 772
  9.4 87.1 %copy-start.13 = (s32[16,4]{0,1:T(4,128)S(1)}, s32[16,4]{0,1:T(4,128)}, u32[]{:S(2)}) copy-start(s32[16,4]{0,1:T(4,128)} %param.32) | copy-start | bytes 772
  9.4 87.3 %copy-start.6 = (bf16[1152]{0:T(1024)(128)(2,1)S(1)}, bf16[1152]{0:T(1024)(128)(2,1)}, u32[]{:S(2)}) copy-start(bf16[1152]{0:T(1024)(128)(2,1)} %param.39) | copy-start | bytes 6916
  9.4 87.3 %copy-start.7 = (bf16[1152]{0:T(1024)(128)(2,1)S(1)}, bf16[1152]{0:T(1024)(128)(2,1)}, u32[]{:S(2)}) copy-start(bf16[1152]{0:T(1024)(128)(2,1)} %param.41) | copy-start | bytes 6916
  9.4 87.3 %copy-start.10 = (bf16[576]{0:T(1024)(128)(2,1)S(1)}, bf16[576]{0:T(1024)(128)(2,1)}, u32[]{:S(2)}) copy-start(bf16[576]{0:T(1024)(128)(2,1)} %param.43) | copy-start | bytes 3460
  96.4 32.8 %collective-permute-start = (bf16[592,3456]{1,0:T(8,128)(2,1)}, bf16[592,3456]{1,0:T(8,128)(2,1)}, u32[]{:S(2)}, u32[]{:S(2)}) collective-permute-start(bf16[592,3456]{1,0:T(8,128)(2,1)} %copy.79), channel_id=1, source_target_pairs={{0,1},{1,0},{2,3},{3,2},{4,5},{5,4},{6,7},{7,6},{8,9},{9,8},{10,11... | collective-permute-start | bytes 12275720 | tf_op jit(solution)/shard_map/ppermute | solution.py:130
  98.8 13.3 %copy-start.3 = (bf16[1,128,1152]{2,1,0:T(8,128)(2,1)S(1)}, bf16[1,128,1152]{2,1,0:T(8,128)(2,1)}, u32[]{:S(2)}) copy-start(bf16[1,128,1152]{2,1,0:T(8,128)(2,1)} %param.29) | copy-start | bytes 884740
  98.9 13.7 %copy-start.18 = (s32[1,4]{1,0:T(1,128)S(1)}, s32[1,4]{1,0:T(1,128)}, u32[]{:S(2)}) copy-start(s32[1,4]{1,0:T(1,128)} %param.33) | copy-start | bytes 52
  98.9 22.0 %copy-start.14 = (bf16[72]{0:T(256)(128)(2,1)S(1)}, bf16[72]{0:T(256)(128)(2,1)}, u32[]{:S(2)}) copy-start(bf16[72]{0:T(256)(128)(2,1)} %param.47) | copy-start | bytes 436
  98.9 22.2 %copy-start.4 = (bf16[1152,72]{0,1:T(8,128)(2,1)S(1)}, bf16[1152,72]{0,1:T(8,128)(2,1)}, u32[]{:S(2)}) copy-start(bf16[1152,72]{0,1:T(8,128)(2,1)} %param.46) | copy-start | bytes 497668
  102.6 18.2 %all-to-all-start = ((bf16[16,4,576]{2,1,0:T(4,128)(2,1)}), bf16[16,4,576]{2,1,0:T(4,128)(2,1)S(1)}, u32[]{:S(2)}, u32[]{:S(2)}) async-start(bf16[16,4,576]{2,1,0:T(4,128)(2,1)} %reshape.202), calls=%async_computation | async-start | bytes 163840 | tf_op jit(solution)/shard_map/all_to_all | solution.py:103
  112.1 60.0 %all-gather.6.cloned.1.call-start = ((), (), s32[]{:S(2)}) async-start(), calls=%async_computation.5 | async-start | bytes 1566720 | tf_op jit(solution)/shard_map/all_gather | solution.py:122
  122.9 2.1 copy-start.1
  137.6 38.0 %all-to-all-start.1 = ((bf16[128,8,432]{0,2,1:T(8,128)(2,1)}), bf16[128,8,432]{0,2,1:T(8,128)(2,1)}, u32[]{:S(2)}, u32[]{:S(2)}) async-start(bf16[128,8,432]{0,2,1:T(8,128)(2,1)} %bitcast.76), calls=%async_computation.1 | async-start | bytes 1769472 | tf_op jit(solution)/shard_map/all_to_all | solution.py:160
  141.8 89.8 %all-gather.8.cloned.1.call-start = ((), (), s32[]{:S(2)}) async-start(), calls=%async_computation.6 | async-start | bytes 2654208 | tf_op jit(solution)/shard_map/all_gather | solution.py:172
  175.6 26.4 %collective-permute-start.1 = (bf16[592,1152]{1,0:T(8,128)(2,1)}, bf16[592,1152]{1,0:T(8,128)(2,1)}, u32[]{:S(2)}, u32[]{:S(2)}) collective-permute-start(bf16[592,1152]{1,0:T(8,128)(2,1)} %copy.87), channel_id=1, source_target_pairs={{0,1},{1,0},{2,3},{3,2},{4,5},{5,4},{6,7},{7,6},{8,9},{9,8},{10,11... | collective-permute-start | bytes 4091912 | tf_op jit(solution)/shard_map/ppermute | solution.py:131
  189.2 12.1 %copy-start.2 = (bf16[592,1152]{0,1:T(8,128)(2,1)S(1)}, bf16[592,1152]{0,1:T(8,128)(2,1)}, u32[]{:S(2)}) copy-start(bf16[592,1152]{0,1:T(8,128)(2,1)} %all-gather.6.cloned.1.call-done) | copy-start | bytes 4091908
  204.1 2.5 copy-start.11
  206.5 70.7 %reduce-scatter.2.cloned.1.call-start = ((), (), s32[]{:S(2)}) async-start(), calls=%async_computation.7 | async-start | bytes 2654208 | tf_op jit(solution)/shard_map/reduce_scatter | solution.py:178
  239.5 0.7 copy-start.8
  239.5 0.7 copy-start.19
  239.5 39.3 %copy-start.5 = (bf16[1152,16]{0,1:T(8,128)(2,1)S(1)}, bf16[1152,16]{0,1:T(8,128)(2,1)}, u32[]{:S(2)}) copy-start(bf16[1152,16]{0,1:T(8,128)(2,1)} %param.52) | copy-start | bytes 110596
  239.5 42.4 %copy-start.15 = (f32[1,4]{1,0:T(1,128)S(1)}, f32[1,4]{1,0:T(1,128)}, u32[]{:S(2)}) copy-start(f32[1,4]{1,0:T(1,128)} %param.35) | copy-start | bytes 52
  239.5 42.4 %copy-start.16 = (f32[1,4]{1,0:T(1,128)S(1)}, f32[1,4]{1,0:T(1,128)}, u32[]{:S(2)}) copy-start(f32[1,4]{1,0:T(1,128)} %param.34) | copy-start | bytes 52
  239.5 42.4 %copy-start.17 = (f32[1,4]{1,0:T(1,128)S(1)}, f32[1,4]{1,0:T(1,128)}, u32[]{:S(2)}) copy-start(f32[1,4]{1,0:T(1,128)} %param.36) | copy-start | bytes 52
  239.5 44.5 %copy-start.9 = (f32[128,8]{0,1:T(8,128)S(1)}, f32[128,8]{0,1:T(8,128)}, u32[]{:S(2)}) copy-start(f32[128,8]{0,1:T(8,128)} %param.30) | copy-start | bytes 12292
  280.3 3.7 %collective-permute-start.2 = (f32[128,8]{0,1:T(8,128)S(1)}, f32[128,8]{0,1:T(8,128)S(1)}, u32[]{:S(2)}, u32[]{:S(2)}) collective-permute-start(f32[128,8]{0,1:T(8,128)S(1)} %constant_dynamic-slice_fusion), channel_id=1, source_target_pairs={{0,128},{128,0},{1,129},{129,1},{2,130},{130,2},{3,131},{131,3},{4... | collective-permute-start | bytes 12296 | tf_op jit(solution)/shard_map/ppermute | solution.py:195
Sparse Core Ops, SparseCore 0:
  9.8 79.4 all-gather.3
  122.0 50.0 all-gather.5
  206.7 24.8 all-gather.7
  239.6 37.5 reduce-scatter.1
